TPU v7x, 512 devices: a whole 4x4x16 slice. The times are simulated.
512 devices in a mesh: slab: 64 (over y, z_lo, core), plane: 8 (over x, z_hi).
Axes of the slice: x: 4, y: 4, z: 16 (z_hi: 2, z_lo: 8; z = z_hi * 8 + z_lo), core: 2. Of those that a mesh axis runs over, the one named last changes fastest.
Arguments:
- rock_state: float32 [2, 128, 64, 512], P(None, 'slab', 'plane'), may hold values from -6 to 6
- rock_source: float32 [2, 128, 64, 512], P(None, 'slab', 'plane'), may hold values from -6 to 6
- transmissibility: bfloat16 [3, 128, 64, 512], P(None, 'slab', 'plane'), may hold values from 0.039794922 to 0.29882812
- cell_inverse: bfloat16 [4, 128, 64, 512], P(None, 'slab', 'plane'), may hold values from -0.06 to 0.3
- fracture_state: float32 [2, 524288], P(None, ('slab', 'plane')), may hold values from -6 to 6
- fracture_source: float32 [2, 524288], P(None, ('slab', 'plane')), may hold values from -6 to 6
- fracture_coupling: bfloat16 [4096, 3, 128, 128], P(('slab', 'plane')), may hold values from -0.25 to 0.25
- fracture_inverse: bfloat16 [4096, 128, 128], P(('slab', 'plane')), may hold values from -0.044194174 to 0.3941942
- fracture_neighbours: int32 [4096, 3], P(('slab', 'plane')), may hold values from 0 to 4095, as said below
- contact_cell: int32 [64, 512, 128], P('slab', 'plane'), may hold values from 0 to 8191
- contact_segment: int32 [64, 512, 128], P('slab', 'plane'), may hold values from 0 to 1023
- contact_weight: float32 [64, 512, 128], P('slab', 'plane'), may hold values from 0.3 to 1.5
- contact_count: int32 [64, 512], P('slab', 'plane'), may hold values from 32 to 128, as said below
Outputs:
- rock_final: float32 [2, 128, 64, 512], P(None, 'slab', 'plane')
- fracture_final: float32 [2, 524288], P(None, ('slab', 'plane'))
Inputs may be any that keep to these rules, and one draw needn't show every extreme that they name: `contact_count`: live contact slots from one rock device to one fracture part of the same plane index; for every plane index some fracture part receives 128 live slots from every rock slab. `fracture_neighbours`: a block's neighbours are other blocks of its own part or of the parts one step away along slab with the same plane index.
All inputs are finite; a program needn't handle non-finite values.
Results may differ from a plain program's by a relative error of at most 0.0033.
Values may be sent and summed in bfloat16 or wider, within the bound.
No kernel may reach another device: no remote copies, remote signals or barrier semaphores. Data moves between devices by JAX's collectives and lax.ppermute only.
A program may use at most 64 MiB of HBM per device.

v0:
```python
import jax
import jax.numpy as jnp
from jax import lax
from jax.sharding import PartitionSpec as P


ITERS = 3


def shifted(value, axis, steps):
    count = lax.axis_size(axis)
    first, last = (max(0, -steps), min(count, count - steps))
    return lax.ppermute(value, axis, [(source, source + steps) for source in range(first, last)])


def split_bf16(value):
    high = lax.reduce_precision(value, exponent_bits=8, mantissa_bits=7)
    return high.astype(jnp.bfloat16), (value - high).astype(jnp.bfloat16)


def pick_values(row_onehot, col_mask, table):
    fields = table.shape[0]
    high, low = split_bf16(table)
    parts = jnp.concatenate([high, low], 0)
    by_row = jnp.einsum("kc,grc->gkr", col_mask, parts, preferred_element_type=jnp.float32)
    picked = jnp.sum(by_row * row_onehot.astype(jnp.float32)[None], axis=-1)
    return picked[:fields] + picked[fields:]


def place_values(row_onehot, col_mask, values):
    fields = values.shape[0]
    high, low = split_bf16(values)
    parts = jnp.concatenate([high, low], 0)
    spread = parts[:, :, None] * row_onehot[None]
    placed = jnp.einsum("gkr,kc->grc", spread, col_mask, preferred_element_type=jnp.float32)
    return placed[:fields] + placed[fields:]


def shards(
    rock_state,
    rock_source,
    transmissibility,
    cell_inverse,
    fracture_state,
    fracture_source,
    fracture_coupling,
    fracture_inverse,
    fracture_neighbours,
    contact_cell,
    contact_segment,
    contact_weight,
    contact_count,
):
    plane_count = lax.axis_size("plane")
    slab_count = lax.axis_size("slab")
    blocks = fracture_coupling.shape[0]
    segment_width = fracture_coupling.shape[-1]
    cell_table = contact_cell[0]
    slot_shape = cell_table.shape
    slot_index = lax.broadcasted_iota(jnp.int32, slot_shape, 1)
    slot_weight = jnp.where(slot_index < contact_count[0][:, None], contact_weight[0], 0.0)
    slot_weight_flat = slot_weight.reshape(-1)
    arrived_segment = lax.all_to_all(
        contact_segment[0], "slab", split_axis=0, concat_axis=0, tiled=True
    )
    my_part = lax.axis_index("slab") * plane_count + lax.axis_index("plane")
    owner_part = fracture_neighbours // blocks
    position = ((owner_part - my_part) // plane_count + 1) * blocks + fracture_neighbours % blocks
    rim_onehot = (
        position[:, :, None] == lax.broadcasted_iota(jnp.int32, (1, 1, 3 * blocks), 2)
    ).astype(jnp.bfloat16)
    cell_total = rock_state[0].size
    cell_rows = cell_total // 128
    cell_flat = cell_table.reshape(-1)
    cell_row_onehot = (
        (cell_flat // 128)[:, None] == lax.broadcasted_iota(jnp.int32, (1, cell_rows), 1)
    ).astype(jnp.bfloat16)
    cell_col_mask = (
        (cell_flat % 128)[:, None] == lax.broadcasted_iota(jnp.int32, (1, 128), 1)
    ).astype(jnp.bfloat16)
    segment_flat = arrived_segment.reshape(-1)
    segment_row_onehot = (
        (segment_flat // segment_width)[:, None] == lax.broadcasted_iota(jnp.int32, (1, blocks), 1)
    ).astype(jnp.bfloat16)
    segment_col_mask = (
        (segment_flat % segment_width)[:, None]
        == lax.broadcasted_iota(jnp.int32, (1, segment_width), 1)
    ).astype(jnp.bfloat16)
    coef_z = transmissibility[0]
    coef_x = transmissibility[1]
    coef_y = transmissibility[2]
    layer_above = shifted(transmissibility[0, :1], "slab", -1)
    layer_beside = shifted(transmissibility[1, :, :1], "plane", -1)
    upper_z = jnp.concatenate([coef_z[1:], layer_above], 0)
    upper_x = jnp.concatenate([coef_x[:, 1:], layer_beside], 1)
    upper_y = jnp.pad(coef_y[..., 1:], ((0, 0), (0, 0), (0, 1)))
    forward_slab = [(i, i + 1) for i in range(slab_count - 1)]
    backward_slab = [(i + 1, i) for i in range(slab_count - 1)]
    forward_plane = [(i, i + 1) for i in range(plane_count - 1)]
    backward_plane = [(i + 1, i) for i in range(plane_count - 1)]
    rock_now = rock_state
    fracture_now = fracture_state
    source_blocks = fracture_source.reshape(2, blocks, segment_width)
    for _ in range(ITERS):
        rock_table = rock_now.reshape(2, cell_rows, 128)
        rock_picked = pick_values(cell_row_onehot, cell_col_mask, rock_table)
        send_rock = slot_weight_flat[None] * rock_picked
        fracture_table = fracture_now.reshape(2, blocks, segment_width)
        send_fracture = pick_values(segment_row_onehot, segment_col_mask, fracture_table)
        send = jnp.concatenate([send_rock, send_fracture], 0).reshape((4,) + slot_shape)
        got = lax.all_to_all(
            send.transpose(1, 0, 2), "slab", split_axis=0, concat_axis=0, tiled=True
        ).transpose(1, 0, 2)
        got_rock = got[:2].reshape(2, -1)
        got_fracture = got[2:].reshape(2, -1)
        fracture_low = fracture_now.astype(jnp.bfloat16).reshape(2, blocks, segment_width)
        fracture_wide = fracture_low.astype(jnp.float32).reshape(2, -1, rock_now.shape[-1])
        from_below = lax.ppermute(
            jnp.concatenate([rock_now[:, -1], fracture_wide], 1), "slab", forward_slab
        )
        from_above = lax.ppermute(
            jnp.concatenate([rock_now[:, 0], fracture_wide], 1), "slab", backward_slab
        )
        from_left = lax.ppermute(rock_now[:, :, -1], "plane", forward_plane)
        from_right = lax.ppermute(rock_now[:, :, 0], "plane", backward_plane)
        layer_rows = rock_now.shape[2]
        rock_below = from_below[:, None, :layer_rows]
        rock_above = from_above[:, None, :layer_rows]
        fracture_prev = from_below[:, layer_rows:].reshape(fracture_low.shape).astype(jnp.bfloat16)
        fracture_next_part = from_above[:, layer_rows:].reshape(
            fracture_low.shape
        ).astype(jnp.bfloat16)
        fracture_padded = jnp.concatenate([fracture_prev, fracture_low, fracture_next_part], 1)
        gathered = jnp.einsum(
            "bkq,fqj->fbkj", rim_onehot, fracture_padded, preferred_element_type=jnp.float32
        ).astype(jnp.bfloat16)
        coupled = jnp.einsum(
            "bkij,fbkj->fbi", fracture_coupling, gathered, preferred_element_type=jnp.float32
        )
        fracture_part = lax.optimization_barrier(source_blocks - coupled)
        below_z = jnp.concatenate([rock_below, rock_now[:, :-1]], 1)
        above_z = jnp.concatenate([rock_now[:, 1:], rock_above], 1)
        below_x = jnp.concatenate([from_left[:, :, None], rock_now[:, :, :-1]], 2)
        above_x = jnp.concatenate([rock_now[:, :, 1:], from_right[:, :, None]], 2)
        below_y = jnp.pad(rock_now[..., :-1], ((0, 0), (0, 0), (0, 0), (1, 0)))
        above_y = jnp.pad(rock_now[..., 1:], ((0, 0), (0, 0), (0, 0), (0, 1)))
        total = coef_z * below_z + upper_z * above_z
        total = total + coef_x * below_x + upper_x * above_x
        total = total + coef_y * below_y + upper_y * above_y
        rock_part = lax.optimization_barrier(rock_source + total)
        leak_fracture = place_values(segment_row_onehot, segment_col_mask, got_rock)
        leak_rock = place_values(
            cell_row_onehot, cell_col_mask, slot_weight_flat[None] * got_fracture
        ).reshape(rock_now.shape)
        fracture_rhs = (fracture_part + leak_fracture).astype(jnp.bfloat16)
        fracture_next = jnp.einsum(
            "bij,fbj->fbi", fracture_inverse, fracture_rhs, preferred_element_type=jnp.float32
        ).reshape(2, -1)
        rock_rhs = rock_part + leak_rock
        rock_now = jnp.stack(
            [
                cell_inverse[0] * rock_rhs[0] + cell_inverse[1] * rock_rhs[1],
                cell_inverse[2] * rock_rhs[0] + cell_inverse[3] * rock_rhs[1],
            ]
        )
        fracture_now = fracture_next
    return (rock_now, fracture_now)


def solution(mesh):
    return jax.shard_map(
        shards,
        mesh=mesh,
        in_specs=(
            P(None, "slab", "plane", None),
            P(None, "slab", "plane", None),
            P(None, "slab", "plane", None),
            P(None, "slab", "plane", None),
            P(None, ("slab", "plane")),
            P(None, ("slab", "plane")),
            P(("slab", "plane"), None, None, None),
            P(("slab", "plane"), None, None),
            P(("slab", "plane"), None),
            P("slab", "plane", None),
            P("slab", "plane", None),
            P("slab", "plane", None),
            P("slab", "plane"),
        ),
        out_specs=(P(None, "slab", "plane", None), P(None, ("slab", "plane"))),
        check_vma=False,
    )
```

profile of v0, /device:TPU:6, one launch (start us, length us, event | category | flops | bytes accessed | tf_op | source)
XLA Modules:
  0.0 250.7 jit_solution(8915325327840510913)
XLA Ops:
  0.6 16.3 %all-to-all-start = ((s32[64,1,128]{2,1,0:T(1,128)}), s32[64,1,128]{2,1,0:T(1,128)S(1)}, u32[]{:S(2)}, u32[]{:S(2)}) async-start(s32[64,1,128]{2,1,0:T(1,128)} %bitcast.335), calls=%async_computation | async-start | bytes 65536 | tf_op jit(solution)/shard_map/all_to_all | solution.py:63
  17.7 8.5 %collective-permute-start.4 = (bf16[2,1,512]{2,0,1:T(2,128)(2,1)S(1)}, bf16[2,1,512]{2,0,1:T(2,128)(2,1)S(1)}, u32[]{:S(2)}, u32[]{:S(2)}) collective-permute-start(bf16[2,1,512]{2,0,1:T(2,128)(2,1)S(1)} %bitcast.345), channel_id=1, source_target_pairs={{1,0},{2,1},{3,2},{4,3},{5,4},{6,5},{7,6},{9,8},{10,9},{11,10},{12... | collective-permute-start | bytes 6152 | tf_op jit(solution)/shard_map/ppermute | solution.py:13
  27.1 6.3 %collective-permute-start.5 = (f32[2,2,512]{2,1,0:T(2,128)S(1)}, f32[2,2,512]{2,1,0:T(2,128)S(1)}, u32[]{:S(2)}, u32[]{:S(2)}) collective-permute-start(f32[2,2,512]{2,1,0:T(2,128)S(1)} %bitcast.341), channel_id=1, source_target_pairs={{1,0},{2,1},{3,2},{4,3},{5,4},{6,5},{7,6},{9,8},{10,9},{11,10},{12... | collective-permute-start | bytes 24584 | tf_op jit(solution)/shard_map/ppermute | solution.py:125
  33.5 8.2 %collective-permute-start.3 = (f32[2,2,512]{2,0,1:T(2,128)S(1)}, f32[2,2,512]{2,0,1:T(2,128)}, u32[]{:S(2)}, u32[]{:S(2)}) collective-permute-start(f32[2,2,512]{2,0,1:T(2,128)S(1)} %bitcast.343), channel_id=1, source_target_pairs={{0,1},{1,2},{2,3},{3,4},{4,5},{5,6},{6,7},{8,9},{9,10},{10,11},{11... | collective-permute-start | bytes 24584 | tf_op jit(solution)/shard_map/ppermute | solution.py:124
  42.4 1.3 collective-permute-start.1
  43.7 1.4 slice_bitcast_fusion.15
  45.9 1.3 collective-permute-start.2
  48.0 1.4 slice_bitcast_fusion.17
  49.4 1.6 fusion.225
  51.0 1.6 fusion.223
  52.6 1.3 reduce-precision_convert_fusion.11
  54.8 1.3 fusion.82
  56.8 2.5 fusion.29
  59.3 3.7 %collective-permute-start = (f32[2,10,512]{2,1,0:T(8,128)S(1)}, f32[2,10,512]{2,1,0:T(8,128)S(1)}, u32[]{:S(2)}, u32[]{:S(2)}) collective-permute-start(f32[2,10,512]{2,1,0:T(8,128)S(1)} %get-tuple-element.91), channel_id=1, source_target_pairs={{0,8},{8,16},{16,24},{24,32},{32,40},{40,48},{48,56},{56,64},{64,7... | collective-permute-start | bytes 122888 | tf_op jit(solution)/shard_map/ppermute | solution.py:118
  64.3 1.3 broadcast_in_dim.30
  69.1 2.8 %fusion.57 = f32[4,8192]{1,0:T(4,128)S(1)} fusion(s32[8192]{0:T(1024)S(1)} %get-tuple-element.71, f32[8192,8]{0,1:T(8,128)S(1)} %get-tuple-element.65, bf16[2,8,128]{2,1,0:T(8,128)(2,1)} %get-tuple-element.89, bf16[2,8,128]{2,1,0:T(8,128)(2,1)} %get-tuple-element.88), kind=kOutput, calls=%fused_computation.48 | convolution fusion | flops 68653056 | bytes 434176 | tf_op jit(solution)/shard_map/kc,grc->gkr/dot_general | solution.py:25
  72.8 21.9 %all-to-all-start.1 = ((f32[64,4,128]{2,1,0:T(4,128)}), f32[64,4,128]{2,1,0:T(4,128)S(1)}, u32[]{:S(2)}, u32[]{:S(2)}) async-start(f32[64,4,128]{2,1,0:T(4,128)} %maximum_bitcast_fusion), calls=%async_computation.1 | async-start | bytes 262144 | tf_op jit(solution)/shard_map/all_to_all | solution.py:111
  96.2 1.7 fusion.115
  98.0 11.5 %all-to-all-done.1 = f32[64,4,128]{2,1,0:T(4,128)S(1)} async-done(((f32[64,4,128]{2,1,0:T(4,128)}), f32[64,4,128]{2,1,0:T(4,128)S(1)}, u32[]{:S(2)}, u32[]{:S(2)}) %all-to-all-start.1) | async-done | bytes 131104 | tf_op jit(solution)/shard_map/all_to_all | solution.py:111
  109.7 2.3 fusion.26
  113.5 1.5 fusion.10
  118.3 1.9 collective-permute-start.8
  120.2 13.5 %collective-permute-start.9 = (f32[2,2,512]{2,1,0:T(2,128)}, f32[2,2,512]{2,1,0:T(2,128)}, u32[]{:S(2)}, u32[]{:S(2)}) collective-permute-start(f32[2,2,512]{2,1,0:T(2,128)} %bitcast.324), channel_id=1, source_target_pairs={{1,0},{2,1},{3,2},{4,3},{5,4},{6,5},{7,6},{9,8},{10,9},{11,10},{12... | collective-permute-start | bytes 24584 | tf_op jit(solution)/shard_map/ppermute | solution.py:125
  133.9 2.5 fusion.32
  136.5 2.1 fusion.60
  139.3 1.9 collective-permute-start.6
  141.2 1.3 collective-permute-start.7
  143.8 13.4 %all-to-all-start.2 = ((f32[64,4,128]{2,1,0:T(4,128)}), f32[64,4,128]{2,1,0:T(4,128)}, u32[]{:S(2)}, u32[]{:S(2)}) async-start(f32[64,4,128]{2,1,0:T(4,128)} %maximum_bitcast_fusion.1), calls=%async_computation.2 | async-start | bytes 262144 | tf_op jit(solution)/shard_map/all_to_all | solution.py:111
  157.2 1.3 copy.168
  158.5 1.3 copy.169
  164.8 1.7 fusion.107
  166.5 5.1 %all-to-all-done.2 = f32[64,4,128]{2,1,0:T(4,128)} async-done(((f32[64,4,128]{2,1,0:T(4,128)}), f32[64,4,128]{2,1,0:T(4,128)}, u32[]{:S(2)}, u32[]{:S(2)}) %all-to-all-start.2) | async-done | bytes 131104 | tf_op jit(solution)/shard_map/all_to_all | solution.py:111
  171.7 1.2 reduce-precision_convert_fusion.5
  172.9 2.2 fusion.23
  176.0 1.5 fusion.8
  178.1 1.5 reshape.347
  183.6 3.3 %fusion.63 = f32[4,8192]{1,0:T(4,128)S(1)} fusion(s32[8192]{0:T(1024)} %copy-done.32, f32[8192,8]{0,1:T(8,128)} %copy-done.23, bf16[2,8,128]{2,1,0:T(8,128)(2,1)S(1)} %get-tuple-element.79, bf16[2,8,128]{2,1,0:T(8,128)(2,1)S(1)} %get-tuple-element.78), kind=kOutput, calls=%fused_computation.50 | convolution fusion | flops 68653056 | bytes 434176 | tf_op jit(solution)/shard_map/kc,grc->gkr/dot_general | solution.py:25
  188.3 1.3 copy.265
  189.6 1.3 copy.266
  190.9 1.9 collective-permute-start.12
  192.8 13.5 %collective-permute-start.13 = (f32[2,2,512]{2,1,0:T(2,128)}, f32[2,2,512]{2,1,0:T(2,128)}, u32[]{:S(2)}, u32[]{:S(2)}) collective-permute-start(f32[2,2,512]{2,1,0:T(2,128)} %bitcast.322), channel_id=1, source_target_pairs={{1,0},{2,1},{3,2},{4,3},{5,4},{6,5},{7,6},{9,8},{10,9},{11,10},{12... | collective-permute-start | bytes 24584 | tf_op jit(solution)/shard_map/ppermute | solution.py:125
  207.9 2.5 fusion.35
  210.5 1.4 collective-permute-start.11
  212.0 3.0 %collective-permute-start.10 = (f32[2,10,512]{2,1,0:T(8,128)S(1)}, f32[2,10,512]{2,1,0:T(8,128)S(1)}, u32[]{:S(2)}, u32[]{:S(2)}) collective-permute-start(f32[2,10,512]{2,1,0:T(8,128)S(1)} %get-tuple-element.81), channel_id=1, source_target_pairs={{0,8},{8,16},{16,24},{24,32},{32,40},{40,48},{48,56},{56,64},{64,7... | collective-permute-start | bytes 122888 | tf_op jit(solution)/shard_map/ppermute | solution.py:118
  215.7 15.6 %all-to-all-start.3 = ((f32[64,4,128]{2,1,0:T(4,128)}), f32[64,4,128]{2,1,0:T(4,128)S(1)}, u32[]{:S(2)}, u32[]{:S(2)}) async-start(f32[64,4,128]{2,1,0:T(4,128)} %maximum_bitcast_fusion.2), calls=%async_computation.3 | async-start | bytes 262144 | tf_op jit(solution)/shard_map/all_to_all | solution.py:111
  234.3 11.8 %all-to-all-done.3 = f32[64,4,128]{2,1,0:T(4,128)S(1)} async-done(((f32[64,4,128]{2,1,0:T(4,128)}), f32[64,4,128]{2,1,0:T(4,128)S(1)}, u32[]{:S(2)}, u32[]{:S(2)}) %all-to-all-start.3) | async-done | bytes 131104 | tf_op jit(solution)/shard_map/all_to_all | solution.py:111
  246.3 1.3 fusion.20
  247.7 1.5 fusion.6
  (210 shorter events, 38.8 us)
Async XLA Ops:
  0.6 66.7 %copy-start = (bf16[8,3,128,128]{3,2,1,0:T(8,128)(2,1)S(1)}, bf16[8,3,128,128]{3,2,1,0:T(8,128)(2,1)}, u32[]{:S(2)}) copy-start(bf16[8,3,128,128]{3,2,1,0:T(8,128)(2,1)} %param.19) | copy-start | bytes 2359300
  0.6 67.0 %all-to-all-start = ((s32[64,1,128]{2,1,0:T(1,128)}), s32[64,1,128]{2,1,0:T(1,128)S(1)}, u32[]{:S(2)}, u32[]{:S(2)}) async-start(s32[64,1,128]{2,1,0:T(1,128)} %bitcast.335), calls=%async_computation | async-start | bytes 65536 | tf_op jit(solution)/shard_map/all_to_all | solution.py:63
  17.7 41.6 %collective-permute-start.4 = (bf16[2,1,512]{2,0,1:T(2,128)(2,1)S(1)}, bf16[2,1,512]{2,0,1:T(2,128)(2,1)S(1)}, u32[]{:S(2)}, u32[]{:S(2)}) collective-permute-start(bf16[2,1,512]{2,0,1:T(2,128)(2,1)S(1)} %bitcast.345), channel_id=1, source_target_pairs={{1,0},{2,1},{3,2},{4,3},{5,4},{6,5},{7,6},{9,8},{10,9},{11,10},{12... | collective-permute-start | bytes 6152 | tf_op jit(solution)/shard_map/ppermute | solution.py:13
  27.1 36.5 %collective-permute-start.5 = (f32[2,2,512]{2,1,0:T(2,128)S(1)}, f32[2,2,512]{2,1,0:T(2,128)S(1)}, u32[]{:S(2)}, u32[]{:S(2)}) collective-permute-start(f32[2,2,512]{2,1,0:T(2,128)S(1)} %bitcast.341), channel_id=1, source_target_pairs={{1,0},{2,1},{3,2},{4,3},{5,4},{6,5},{7,6},{9,8},{10,9},{11,10},{12... | collective-permute-start | bytes 24584 | tf_op jit(solution)/shard_map/ppermute | solution.py:125
  33.5 30.8 %collective-permute-start.3 = (f32[2,2,512]{2,0,1:T(2,128)S(1)}, f32[2,2,512]{2,0,1:T(2,128)}, u32[]{:S(2)}, u32[]{:S(2)}) collective-permute-start(f32[2,2,512]{2,0,1:T(2,128)S(1)} %bitcast.343), channel_id=1, source_target_pairs={{0,1},{1,2},{2,3},{3,4},{4,5},{5,6},{6,7},{8,9},{9,10},{10,11},{11... | collective-permute-start | bytes 24584 | tf_op jit(solution)/shard_map/ppermute | solution.py:124
  42.4 21.2 %collective-permute-start.1 = (bf16[1,8,512]{2,1,0:T(8,128)(2,1)S(1)}, bf16[1,8,512]{2,1,0:T(8,128)(2,1)S(1)}, u32[]{:S(2)}, u32[]{:S(2)}) collective-permute-start(bf16[1,8,512]{2,1,0:T(8,128)(2,1)S(1)} %get-tuple-element.63), channel_id=1, source_target_pairs={{8,0},{16,8},{24,16},{32,24},{40,32},{48,40},{56,48},{64,56},{72,6... | collective-permute-start | bytes 24584 | tf_op jit(solution)/shard_map/ppermute | solution.py:13
  45.9 19.7 %collective-permute-start.2 = (f32[2,10,512]{2,1,0:T(8,128)S(1)}, f32[2,10,512]{2,1,0:T(8,128)}, u32[]{:S(2)}, u32[]{:S(2)}) collective-permute-start(f32[2,10,512]{2,1,0:T(8,128)S(1)} %get-tuple-element.90), channel_id=1, source_target_pairs={{8,0},{16,8},{24,16},{32,24},{40,32},{48,40},{56,48},{64,56},{72,6... | collective-permute-start | bytes 122888 | tf_op jit(solution)/shard_map/ppermute | solution.py:121
  48.0 8.1 %copy-start.39 = (s32[8,3]{0,1:T(4,128)S(1)}, s32[8,3]{0,1:T(4,128)}, u32[]{:S(2)}) copy-start(s32[8,3]{0,1:T(4,128)} %param.21) | copy-start | bytes 292
  48.0 8.7 %copy-start.35 = (f32[1,64,128]{2,1,0:T(8,128)S(1)}, f32[1,64,128]{2,1,0:T(8,128)}, u32[]{:S(2)}) copy-start(f32[1,64,128]{2,1,0:T(8,128)} %param.24) | copy-start | bytes 98308
  48.0 8.7 %copy-start.40 = (s32[1,64]{1,0:T(1,128)S(1)}, s32[1,64]{1,0:T(1,128)}, u32[]{:S(2)}) copy-start(s32[1,64]{1,0:T(1,128)} %param.25) | copy-start | bytes 772
  49.4 46.8 %copy-start.11 = (f32[2,8,512]{2,1,0:T(8,128)}, f32[2,8,512]{2,1,0:T(8,128)S(1)}, u32[]{:S(2)}) copy-start(f32[2,8,512]{2,1,0:T(8,128)S(1)} %get-tuple-element.58) | copy-start | bytes 98308
  49.4 46.8 %copy-start.13 = (f32[2,8,512]{2,1,0:T(8,128)}, f32[2,8,512]{2,1,0:T(8,128)S(1)}, u32[]{:S(2)}) copy-start(f32[2,8,512]{2,1,0:T(8,128)S(1)} %get-tuple-element.59) | copy-start | bytes 98308
  56.8 10.5 %copy-start.31 = (f32[2,1024]{1,0:T(2,128)S(1)}, f32[2,1024]{1,0:T(2,128)}, u32[]{:S(2)}) copy-start(f32[2,1024]{1,0:T(2,128)} %param.18) | copy-start | bytes 24580
  59.3 36.9 %copy-start.7 = (f32[2,8,512]{2,1,0:T(8,128)}, f32[2,8,512]{2,1,0:T(8,128)S(1)}, u32[]{:S(2)}) copy-start(f32[2,8,512]{2,1,0:T(8,128)S(1)} %pad_convert_fusion) | copy-start | bytes 98308
  59.3 7.1 %collective-permute-start = (f32[2,10,512]{2,1,0:T(8,128)S(1)}, f32[2,10,512]{2,1,0:T(8,128)S(1)}, u32[]{:S(2)}, u32[]{:S(2)}) collective-permute-start(f32[2,10,512]{2,1,0:T(8,128)S(1)} %get-tuple-element.91), channel_id=1, source_target_pairs={{0,8},{8,16},{16,24},{24,32},{32,40},{40,48},{48,56},{56,64},{64,7... | collective-permute-start | bytes 122888 | tf_op jit(solution)/shard_map/ppermute | solution.py:118
  63.6 32.6 %copy-start.9 = (f32[2,8,512]{2,1,0:T(8,128)}, f32[2,8,512]{2,1,0:T(8,128)S(1)}, u32[]{:S(2)}) copy-start(f32[2,8,512]{2,1,0:T(8,128)S(1)} %maximum_convert_fusion) | copy-start | bytes 98308
  64.3 31.9 %copy-start.5 = (f32[2,2,8,512]{3,2,1,0:T(8,128)S(1)}, f32[2,2,8,512]{3,2,1,0:T(8,128)}, u32[]{:S(2)}) copy-start(f32[2,2,8,512]{3,2,1,0:T(8,128)} %param.14) | copy-start | bytes 196612
  71.9 40.0 %copy-start.1 = (bf16[8,128,128]{2,1,0:T(8,128)(2,1)S(1)}, bf16[8,128,128]{2,1,0:T(8,128)(2,1)}, u32[]{:S(2)}) copy-start(bf16[8,128,128]{2,1,0:T(8,128)(2,1)} %param.20) | copy-start | bytes 786436
  72.8 36.7 %all-to-all-start.1 = ((f32[64,4,128]{2,1,0:T(4,128)}), f32[64,4,128]{2,1,0:T(4,128)S(1)}, u32[]{:S(2)}, u32[]{:S(2)}) async-start(f32[64,4,128]{2,1,0:T(4,128)} %maximum_bitcast_fusion), calls=%async_computation.1 | async-start | bytes 262144 | tf_op jit(solution)/shard_map/all_to_all | solution.py:111
  109.5 4.0 %copy-start.2 = (bf16[8192,64]{0,1:T(8,128)(2,1)S(1)}, bf16[8192,64]{0,1:T(8,128)(2,1)}, u32[]{:S(2)}) copy-start(bf16[8192,64]{0,1:T(8,128)(2,1)} %get-tuple-element.69) | copy-start | bytes 3145732
  118.3 38.9 %collective-permute-start.8 = (f32[2,2,512]{2,1,0:T(2,128)}, f32[2,2,512]{2,1,0:T(2,128)}, u32[]{:S(2)}, u32[]{:S(2)}) collective-permute-start(f32[2,2,512]{2,1,0:T(2,128)} %bitcast.325), channel_id=1, source_target_pairs={{0,1},{1,2},{2,3},{3,4},{4,5},{5,6},{6,7},{8,9},{9,10},{10,11},{11... | collective-permute-start | bytes 24584 | tf_op jit(solution)/shard_map/ppermute | solution.py:124
  120.2 38.3 %collective-permute-start.9 = (f32[2,2,512]{2,1,0:T(2,128)}, f32[2,2,512]{2,1,0:T(2,128)}, u32[]{:S(2)}, u32[]{:S(2)}) collective-permute-start(f32[2,2,512]{2,1,0:T(2,128)} %bitcast.324), channel_id=1, source_target_pairs={{1,0},{2,1},{3,2},{4,3},{5,4},{6,5},{7,6},{9,8},{10,9},{11,10},{12... | collective-permute-start | bytes 24584 | tf_op jit(solution)/shard_map/ppermute | solution.py:125
  133.9 4.8 %copy-start.17 = (f32[2,1,8,512]{3,2,1,0:T(8,128)S(1)}, f32[2,1,8,512]{3,2,1,0:T(8,128)}, u32[]{:S(2)}) copy-start(f32[2,1,8,512]{3,2,1,0:T(8,128)} %get-tuple-element.40) | copy-start | bytes 98308
  133.9 4.8 %copy-start.25 = (f32[2,8,512]{2,1,0:T(8,128)S(1)}, f32[2,8,512]{2,1,0:T(8,128)}, u32[]{:S(2)}) copy-start(f32[2,8,512]{2,1,0:T(8,128)} %get-tuple-element.39) | copy-start | bytes 98308
  136.4 28.4 %copy-start.8 = (f32[2,8,512]{2,1,0:T(8,128)S(1)}, f32[2,8,512]{2,1,0:T(8,128)}, u32[]{:S(2)}) copy-start(f32[2,8,512]{2,1,0:T(8,128)} %copy-done.7) | copy-start | bytes 98308
  136.4 28.4 %copy-start.10 = (f32[2,8,512]{2,1,0:T(8,128)S(1)}, f32[2,8,512]{2,1,0:T(8,128)}, u32[]{:S(2)}) copy-start(f32[2,8,512]{2,1,0:T(8,128)} %copy-done.9) | copy-start | bytes 98308
  136.4 28.4 %copy-start.12 = (f32[2,8,512]{2,1,0:T(8,128)S(1)}, f32[2,8,512]{2,1,0:T(8,128)}, u32[]{:S(2)}) copy-start(f32[2,8,512]{2,1,0:T(8,128)} %copy-done.11) | copy-start | bytes 98308
  136.4 28.4 %copy-start.14 = (f32[2,8,512]{2,1,0:T(8,128)S(1)}, f32[2,8,512]{2,1,0:T(8,128)}, u32[]{:S(2)}) copy-start(f32[2,8,512]{2,1,0:T(8,128)} %copy-done.13) | copy-start | bytes 98308
  139.3 20.5 %collective-permute-start.6 = (f32[2,10,512]{2,1,0:T(8,128)}, f32[2,10,512]{2,1,0:T(8,128)}, u32[]{:S(2)}, u32[]{:S(2)}) collective-permute-start(f32[2,10,512]{2,1,0:T(8,128)} %get-tuple-element.84), channel_id=1, source_target_pairs={{0,8},{8,16},{16,24},{24,32},{32,40},{40,48},{48,56},{56,64},{64,7... | collective-permute-start | bytes 122888 | tf_op jit(solution)/shard_map/ppermute | solution.py:118
  141.2 19.4 %collective-permute-start.7 = (f32[2,10,512]{2,1,0:T(8,128)}, f32[2,10,512]{2,1,0:T(8,128)}, u32[]{:S(2)}, u32[]{:S(2)}) collective-permute-start(f32[2,10,512]{2,1,0:T(8,128)} %get-tuple-element.85), channel_id=1, source_target_pairs={{8,0},{16,8},{24,16},{32,24},{40,32},{48,40},{56,48},{64,56},{72,6... | collective-permute-start | bytes 122888 | tf_op jit(solution)/shard_map/ppermute | solution.py:121
  143.8 27.8 %all-to-all-start.2 = ((f32[64,4,128]{2,1,0:T(4,128)}), f32[64,4,128]{2,1,0:T(4,128)}, u32[]{:S(2)}, u32[]{:S(2)}) async-start(f32[64,4,128]{2,1,0:T(4,128)} %maximum_bitcast_fusion.1), calls=%async_computation.2 | async-start | bytes 262144 | tf_op jit(solution)/shard_map/all_to_all | solution.py:111
  171.7 4.4 %copy-start.3 = (bf16[8192,64]{0,1:T(8,128)(2,1)S(1)}, bf16[8192,64]{0,1:T(8,128)(2,1)}, u32[]{:S(2)}) copy-start(bf16[8192,64]{0,1:T(8,128)(2,1)} %get-tuple-element.69) | copy-start | bytes 3145732
  176.0 3.6 %copy-start.21 = (f32[2,2,8,512]{3,2,1,0:T(8,128)S(1)}, f32[2,2,8,512]{3,2,1,0:T(8,128)}, u32[]{:S(2)}) copy-start(f32[2,2,8,512]{3,2,1,0:T(8,128)} %fusion.107) | copy-start | bytes 196612
  190.9 40.5 %collective-permute-start.12 = (f32[2,2,512]{2,1,0:T(2,128)}, f32[2,2,512]{2,1,0:T(2,128)}, u32[]{:S(2)}, u32[]{:S(2)}) collective-permute-start(f32[2,2,512]{2,1,0:T(2,128)} %bitcast.323), channel_id=1, source_target_pairs={{0,1},{1,2},{2,3},{3,4},{4,5},{5,6},{6,7},{8,9},{9,10},{10,11},{11... | collective-permute-start | bytes 24584 | tf_op jit(solution)/shard_map/ppermute | solution.py:124
  192.8 39.3 %collective-permute-start.13 = (f32[2,2,512]{2,1,0:T(2,128)}, f32[2,2,512]{2,1,0:T(2,128)}, u32[]{:S(2)}, u32[]{:S(2)}) collective-permute-start(f32[2,2,512]{2,1,0:T(2,128)} %bitcast.322), channel_id=1, source_target_pairs={{1,0},{2,1},{3,2},{4,3},{5,4},{6,5},{7,6},{9,8},{10,9},{11,10},{12... | collective-permute-start | bytes 24584 | tf_op jit(solution)/shard_map/ppermute | solution.py:125
  207.9 7.1 %copy-start.22 = (f32[2,8192]{1,0:T(2,128)S(1)}, f32[2,8192]{1,0:T(2,128)}, u32[]{:S(2)}) copy-start(f32[2,8192]{1,0:T(2,128)} %slice_add_fusion.1) | copy-start | bytes 196612
  210.4 23.8 %copy-start.15 = (f32[2,8,512]{2,1,0:T(8,128)S(1)}, f32[2,8,512]{2,1,0:T(8,128)}, u32[]{:S(2)}) copy-start(f32[2,8,512]{2,1,0:T(8,128)} %get-tuple-element.60) | copy-start | bytes 98308
  210.4 23.8 %copy-start.16 = (f32[2,8,512]{2,1,0:T(8,128)S(1)}, f32[2,8,512]{2,1,0:T(8,128)}, u32[]{:S(2)}) copy-start(f32[2,8,512]{2,1,0:T(8,128)} %maximum_convert_fusion.1) | copy-start | bytes 98308
  210.4 23.8 %copy-start.18 = (f32[2,2,7,512]{3,2,1,0:T(8,128)S(1)}, f32[2,2,7,512]{3,2,1,0:T(8,128)}, u32[]{:S(2)}) copy-start(f32[2,2,7,512]{3,2,1,0:T(8,128)} %get-tuple-element.32) | copy-start | bytes 172036
  210.4 23.8 %copy-start.19 = (f32[2,2,7,512]{3,2,1,0:T(8,128)S(1)}, f32[2,2,7,512]{3,2,1,0:T(8,128)}, u32[]{:S(2)}) copy-start(f32[2,2,7,512]{3,2,1,0:T(8,128)} %get-tuple-element.33) | copy-start | bytes 172036
  210.4 23.8 %copy-start.27 = (f32[2,1,8,512]{3,2,0,1:T(8,128)S(1)}, f32[2,1,8,512]{3,2,0,1:T(8,128)}, u32[]{:S(2)}) copy-start(f32[2,1,8,512]{3,2,0,1:T(8,128)} %get-tuple-element.28) | copy-start | bytes 98308
  210.4 23.8 %copy-start.28 = (f32[2,1,8,512]{3,2,0,1:T(8,128)S(1)}, f32[2,1,8,512]{3,2,0,1:T(8,128)}, u32[]{:S(2)}) copy-start(f32[2,1,8,512]{3,2,0,1:T(8,128)} %get-tuple-element.31) | copy-start | bytes 98308
  210.4 35.9 %copy-start.26 = (bf16[8192,8]{0,1:T(8,128)(2,1)S(1)}, bf16[8192,8]{0,1:T(8,128)(2,1)}, u32[]{:S(2)}) copy-start(bf16[8192,8]{0,1:T(8,128)(2,1)} %get-tuple-element.64) | copy-start | bytes 393220
  210.4 35.9 %copy-start.34 = (s32[8192]{0:T(1024)S(1)}, s32[8192]{0:T(1024)}, u32[]{:S(2)}) copy-start(s32[8192]{0:T(1024)} %copy-done.32) | copy-start | bytes 98308
  210.5 22.2 %collective-permute-start.11 = (f32[2,10,512]{2,1,0:T(8,128)S(1)}, f32[2,10,512]{2,1,0:T(8,128)S(1)}, u32[]{:S(2)}, u32[]{:S(2)}) collective-permute-start(f32[2,10,512]{2,1,0:T(8,128)S(1)} %get-tuple-element.80), channel_id=1, source_target_pairs={{8,0},{16,8},{24,16},{32,24},{40,32},{48,40},{56,48},{64,56},{72,6... | collective-permute-start | bytes 122888 | tf_op jit(solution)/shard_map/ppermute | solution.py:121
  212.0 20.8 %collective-permute-start.10 = (f32[2,10,512]{2,1,0:T(8,128)S(1)}, f32[2,10,512]{2,1,0:T(8,128)S(1)}, u32[]{:S(2)}, u32[]{:S(2)}) collective-permute-start(f32[2,10,512]{2,1,0:T(8,128)S(1)} %get-tuple-element.81), channel_id=1, source_target_pairs={{0,8},{8,16},{16,24},{24,32},{32,40},{40,48},{48,56},{56,64},{64,7... | collective-permute-start | bytes 122888 | tf_op jit(solution)/shard_map/ppermute | solution.py:118
  215.7 30.4 %all-to-all-start.3 = ((f32[64,4,128]{2,1,0:T(4,128)}), f32[64,4,128]{2,1,0:T(4,128)S(1)}, u32[]{:S(2)}, u32[]{:S(2)}) async-start(f32[64,4,128]{2,1,0:T(4,128)} %maximum_bitcast_fusion.2), calls=%async_computation.3 | async-start | bytes 262144 | tf_op jit(solution)/shard_map/all_to_all | solution.py:111
  233.8 13.9 %copy-start.4 = (bf16[8192,64]{0,1:T(8,128)(2,1)S(1)}, bf16[8192,64]{0,1:T(8,128)(2,1)}, u32[]{:S(2)}) copy-start(bf16[8192,64]{0,1:T(8,128)(2,1)} %get-tuple-element.69) | copy-start | bytes 3145732
  (11 other events, 21.7 us)
where the time goes:
time: 254 us; the launch traced here: 251 us
  starting transfers between devices  135 us (53%)
  local copies, waits for them, and re-layouts  31.5 us (12%)
  matrix products  30.7 us (12%)
  waiting for transfers between devices  28.5 us (11%)
  other arithmetic  23.3 us (9%)
    all_to_all x3, starting transfers between devices, shards(): lax.all_to_all(send.transpose(1, 0, 2), 'slab', split_axis=0, concat_axis...  50.8 us
    ppermute x3, starting transfers between devices, shards(): from_right = lax.ppermute(rock_now[:, :, 0], 'plane', backward_plane)  33.4 us
    all_to_all x3, waiting for transfers between devices, shards(): lax.all_to_all(send.transpose(1, 0, 2), 'slab', split_axis=0, concat_axis...  28.4 us
    all_to_all x1, starting transfers between devices, shards(): lax.all_to_all(contact_segment[0], 'slab', split_axis=0, concat_axis=0, t...  16.3 us
    dot_general x6, matrix products, pick_values(): jnp.einsum('kc,grc->gkr', col_mask, parts, preferred_element_type=jnp.flo...  15.6 us
    ppermute x3, starting transfers between devices, shards(): from_left = lax.ppermute(rock_now[:, :, -1], 'plane', forward_plane)  12 us
    dot_general x6, matrix products, place_values(): jnp.einsum('gkr,kc->grc', spread, col_mask, preferred_element_type=jnp.fl...  10.1 us
    ppermute x2, starting transfers between devices, shifted(): lax.ppermute(value, axis, [(source, source + steps) for source in range(f...  9.76 us
  transfers between devices with their start and end apart: 18, of which 3 were waited for; matrix products, arithmetic and copies ran while one was open for 19% of the time, Pallas kernels for 0%

commit v1 on v0

--- a/solution.py
+++ b/solution.py
@@ -96,8 +96,6 @@
     upper_y = jnp.pad(coef_y[..., 1:], ((0, 0), (0, 0), (0, 1)))
     forward_slab = [(i, i + 1) for i in range(slab_count - 1)]
     backward_slab = [(i + 1, i) for i in range(slab_count - 1)]
-    forward_plane = [(i, i + 1) for i in range(plane_count - 1)]
-    backward_plane = [(i + 1, i) for i in range(plane_count - 1)]
     rock_now = rock_state
     fracture_now = fracture_state
     source_blocks = fracture_source.reshape(2, blocks, segment_width)
@@ -121,9 +119,17 @@
         from_above = lax.ppermute(
             jnp.concatenate([rock_now[:, 0], fracture_wide], 1), "slab", backward_slab
         )
-        from_left = lax.ppermute(rock_now[:, :, -1], "plane", forward_plane)
-        from_right = lax.ppermute(rock_now[:, :, 0], "plane", backward_plane)
+        own_rims = jnp.stack([rock_now[:, :, 0], rock_now[:, :, -1]])
+        slot = lax.broadcasted_iota(jnp.int32, (plane_count, 1, 1, 1, 1), 0)
+        rims = lax.psum(jnp.where(slot == lax.axis_index("plane"), own_rims[None], 0.0), "plane")
         layer_rows = rock_now.shape[2]
+        plane = lax.axis_index("plane")
+        left_rim = lax.dynamic_index_in_dim(rims, jnp.maximum(plane - 1, 0), 0, False)[1]
+        right_rim = lax.dynamic_index_in_dim(
+            rims, jnp.minimum(plane + 1, plane_count - 1), 0, False
+        )[0]
+        from_left = jnp.where(plane > 0, left_rim, 0.0)
+        from_right = jnp.where(plane < plane_count - 1, right_rim, 0.0)
         rock_below = from_below[:, None, :layer_rows]
         rock_above = from_above[:, None, :layer_rows]
         fracture_prev = from_below[:, layer_rows:].reshape(fracture_low.shape).astype(jnp.bfloat16)

time: 254 us -> 562 us (2.21)
  the two profiles are of different devices: /device:TPU:6 before, /device:TPU:8 now
where the time goes in v1:
time: 562 us; the launch traced here: 559 us
  waiting for transfers between devices  371 us (66%)
  starting transfers between devices  82.2 us (15%)
  other arithmetic  32.8 us (6%)
  matrix products  31.3 us (6%)
  local copies, waits for them, and re-layouts  26.7 us (5%)
  between operations  14.8 us (3%)
    psum x3, waiting for transfers between devices, shards(): lax.psum(jnp.where(slot == lax.axis_index('plane'), own_rims[None], 0.0),...  362 us
    all_to_all x3, starting transfers between devices, shards(): lax.all_to_all(send.transpose(1, 0, 2), 'slab', split_axis=0, concat_axis...  25.8 us
    ppermute x3, starting transfers between devices, shards(): lax.ppermute(jnp.concatenate([rock_now[:, 0], fracture_wide], 1), 'slab',...  23.1 us
    dot_general x6, matrix products, pick_values(): jnp.einsum('kc,grc->gkr', col_mask, parts, preferred_element_type=jnp.flo...  16.8 us
    all_to_all x1, starting transfers between devices, shards(): lax.all_to_all(contact_segment[0], 'slab', split_axis=0, concat_axis=0, t...  16.3 us
  transfers between devices with their start and end apart: 15, of which 4 were waited for; matrix products, arithmetic and copies ran while one was open for 9% of the time, Pallas kernels for 0%

profile of v1, /device:TPU:8, one launch (start us, length us, event | category | flops | bytes accessed | tf_op | source)
XLA Modules:
  0.0 559.0 jit_solution(16512961113292060075)
XLA Ops:
  7.2 16.3 %all-to-all-start = ((s32[64,1,128]{2,1,0:T(1,128)}), s32[64,1,128]{2,1,0:T(1,128)S(1)}, u32[]{:S(2)}, u32[]{:S(2)}) async-start(s32[64,1,128]{2,1,0:T(1,128)} %bitcast.334), calls=%async_computation | async-start | bytes 65536 | tf_op jit(solution)/shard_map/all_to_all | solution.py:63
  24.3 1.3 collective-permute-start.3
  25.6 1.3 slice_bitcast_fusion.21
  26.9 9.7 %collective-permute-start.1 = (bf16[1,8,512]{2,1,0:T(8,128)(2,1)}, bf16[1,8,512]{2,1,0:T(8,128)(2,1)S(1)}, u32[]{:S(2)}, u32[]{:S(2)}) collective-permute-start(bf16[1,8,512]{2,1,0:T(8,128)(2,1)} %get-tuple-element.69), channel_id=1, source_target_pairs={{8,0},{16,8},{24,16},{32,24},{40,32},{48,40},{56,48},{64,56},{72,6... | collective-permute-start | bytes 24584 | tf_op jit(solution)/shard_map/ppermute | solution.py:13
  36.6 0.9 slice_bitcast_fusion.19
  38.4 1.4 slice_bitcast_fusion.15
  40.5 2.3 collective-permute-start.2
  42.8 2.0 collective-permute-start
  45.7 1.4 slice_bitcast_fusion.17
  47.1 1.6 fusion.233
  48.7 1.6 fusion.234
  50.3 1.3 reduce-precision_convert_fusion.11
  52.5 1.3 fusion.82
  53.9 2.5 fusion.29
  59.8 1.4 slice_bitcast_fusion.10
  62.6 2.8 fusion.57
  66.2 14.1 %all-to-all-start.1 = ((f32[64,4,128]{2,1,0:T(4,128)}), f32[64,4,128]{2,1,0:T(4,128)S(1)}, u32[]{:S(2)}, u32[]{:S(2)}) async-start(f32[64,4,128]{2,1,0:T(4,128)} %maximum_bitcast_fusion), calls=%async_computation.1 | async-start | bytes 262144 | tf_op jit(solution)/shard_map/all_to_all | solution.py:109
  80.4 1.4 slice_bitcast_fusion.11
  81.7 111.9 %all-reduce.11.cloned.1.call-done = f32[8,2,2,2,512]{4,0,3,2,1:T(8,128)} async-done(((f32[8,2,2,2,512]{4,0,3,2,1:T(8,128)}), f32[8,2,2,2,512]{4,0,3,2,1:T(8,128)}) %all-reduce.11.cloned.1.call-update) | async-done | bytes 131088 | tf_op jit(solution)/shard_map/psum | solution.py:124
  194.5 1.8 fusion.115
  196.5 2.3 fusion.26
  200.3 1.5 fusion.10
  204.7 2.5 fusion.32
  208.7 3.3 fusion.60
  212.0 1.5 pad_maximum_fusion.3
  213.5 1.9 collective-permute-start.4
  215.4 11.1 %collective-permute-start.5 = (f32[2,10,512]{2,1,0:T(8,128)}, f32[2,10,512]{2,1,0:T(8,128)}, u32[]{:S(2)}, u32[]{:S(2)}) collective-permute-start(f32[2,10,512]{2,1,0:T(8,128)} %get-tuple-element.91), channel_id=1, source_target_pairs={{8,0},{16,8},{24,16},{32,24},{40,32},{48,40},{56,48},{64,56},{72,6... | collective-permute-start | bytes 122888 | tf_op jit(solution)/shard_map/ppermute | solution.py:119
  226.6 1.6 maximum_bitcast_fusion.1
  228.1 5.6 %all-to-all-start.2 = ((f32[64,4,128]{2,1,0:T(4,128)}), f32[64,4,128]{2,1,0:T(4,128)}, u32[]{:S(2)}, u32[]{:S(2)}) async-start(f32[64,4,128]{2,1,0:T(4,128)} %maximum_bitcast_fusion.1), calls=%async_computation.2 | async-start | bytes 262144 | tf_op jit(solution)/shard_map/all_to_all | solution.py:109
  235.9 0.9 fusion.67
  237.1 1.4 slice_bitcast_fusion.9
  238.5 1.4 slice_bitcast_fusion.8
  239.9 111.3 %all-reduce.13.cloned.1.call-done = f32[8,2,2,2,512]{4,0,3,2,1:T(8,128)} async-done(((f32[8,2,2,2,512]{4,0,3,2,1:T(8,128)}), f32[8,2,2,2,512]{4,0,3,2,1:T(8,128)}) %all-reduce.13.cloned.1.call-update) | async-done | bytes 131088 | tf_op jit(solution)/shard_map/psum | solution.py:124
  352.2 1.7 fusion.107
  353.9 1.2 reduce-precision_convert_fusion.5
  355.1 2.2 fusion.23
  358.3 1.5 fusion.8
  360.4 1.5 reshape.445
  366.5 3.3 fusion.63
  374.1 2.5 fusion.35
  377.5 6.1 %all-to-all-start.3 = ((f32[64,4,128]{2,1,0:T(4,128)}), f32[64,4,128]{2,1,0:T(4,128)S(1)}, u32[]{:S(2)}, u32[]{:S(2)}) async-start(f32[64,4,128]{2,1,0:T(4,128)} %maximum_bitcast_fusion.2), calls=%async_computation.3 | async-start | bytes 262144 | tf_op jit(solution)/shard_map/all_to_all | solution.py:109
  384.4 9.7 %collective-permute-start.7 = (f32[2,10,512]{2,1,0:T(8,128)S(1)}, f32[2,10,512]{2,1,0:T(8,128)S(1)}, u32[]{:S(2)}, u32[]{:S(2)}) collective-permute-start(f32[2,10,512]{2,1,0:T(8,128)S(1)} %get-tuple-element.86), channel_id=1, source_target_pairs={{8,0},{16,8},{24,16},{32,24},{40,32},{48,40},{56,48},{64,56},{72,6... | collective-permute-start | bytes 122888 | tf_op jit(solution)/shard_map/ppermute | solution.py:119
  394.1 1.9 collective-permute-start.6
  396.0 1.5 broadcast_select_fusion
  397.5 9.6 %collective-permute-done.6 = f32[2,10,512]{2,1,0:T(8,128)S(1)} collective-permute-done((f32[2,10,512]{2,1,0:T(8,128)S(1)}, f32[2,10,512]{2,1,0:T(8,128)S(1)}, u32[]{:S(2)}, u32[]{:S(2)}) %collective-permute-start.6) | collective-permute-done | bytes 40992 | tf_op jit(solution)/shard_map/ppermute | solution.py:116
  408.4 138.4 %all-reduce.15.cloned.1.call-done = f32[8,2,2,2,512]{4,0,3,2,1:T(8,128)} async-done(((f32[8,2,2,2,512]{4,0,3,2,1:T(8,128)}), f32[8,2,2,2,512]{4,0,3,2,1:T(8,128)}) %all-reduce.15.cloned.1.call-update) | async-done | bytes 131088 | tf_op jit(solution)/shard_map/psum | solution.py:124
  548.1 1.3 fusion.20
  549.5 1.5 fusion.6
  (200 shorter events, 36.3 us)
Async XLA Ops:
  7.2 52.2 %copy-start = (bf16[8,3,128,128]{3,2,1,0:T(8,128)(2,1)S(1)}, bf16[8,3,128,128]{3,2,1,0:T(8,128)(2,1)}, u32[]{:S(2)}) copy-start(bf16[8,3,128,128]{3,2,1,0:T(8,128)(2,1)} %param.19) | copy-start | bytes 2359300
  7.2 54.0 %all-to-all-start = ((s32[64,1,128]{2,1,0:T(1,128)}), s32[64,1,128]{2,1,0:T(1,128)S(1)}, u32[]{:S(2)}, u32[]{:S(2)}) async-start(s32[64,1,128]{2,1,0:T(1,128)} %bitcast.334), calls=%async_computation | async-start | bytes 65536 | tf_op jit(solution)/shard_map/all_to_all | solution.py:63
  23.5 170.1 %all-reduce.11.cloned.1.call-start = ((), (), s32[]{:S(2)}) async-start(), calls=%async_computation.4 | async-start | bytes 262144 | tf_op jit(solution)/shard_map/psum | solution.py:124
  24.3 32.2 %collective-permute-start.3 = (bf16[2,1,512]{2,0,1:T(2,128)(2,1)S(1)}, bf16[2,1,512]{2,0,1:T(2,128)(2,1)}, u32[]{:S(2)}, u32[]{:S(2)}) collective-permute-start(bf16[2,1,512]{2,0,1:T(2,128)(2,1)S(1)} %bitcast.341), channel_id=1, source_target_pairs={{1,0},{2,1},{3,2},{4,3},{5,4},{6,5},{7,6},{9,8},{10,9},{11,10},{12... | collective-permute-start | bytes 6152 | tf_op jit(solution)/shard_map/ppermute | solution.py:13
  26.9 30.8 %collective-permute-start.1 = (bf16[1,8,512]{2,1,0:T(8,128)(2,1)}, bf16[1,8,512]{2,1,0:T(8,128)(2,1)S(1)}, u32[]{:S(2)}, u32[]{:S(2)}) collective-permute-start(bf16[1,8,512]{2,1,0:T(8,128)(2,1)} %get-tuple-element.69), channel_id=1, source_target_pairs={{8,0},{16,8},{24,16},{32,24},{40,32},{48,40},{56,48},{64,56},{72,6... | collective-permute-start | bytes 24584 | tf_op jit(solution)/shard_map/ppermute | solution.py:13
  36.6 1.7 copy-start.32
  40.5 17.3 %collective-permute-start.2 = (f32[2,10,512]{2,1,0:T(8,128)S(1)}, f32[2,10,512]{2,1,0:T(8,128)}, u32[]{:S(2)}, u32[]{:S(2)}) collective-permute-start(f32[2,10,512]{2,1,0:T(8,128)S(1)} %get-tuple-element.96), channel_id=1, source_target_pairs={{8,0},{16,8},{24,16},{32,24},{40,32},{48,40},{56,48},{64,56},{72,6... | collective-permute-start | bytes 122888 | tf_op jit(solution)/shard_map/ppermute | solution.py:119
  42.8 15.7 %collective-permute-start = (f32[2,10,512]{2,1,0:T(8,128)S(1)}, f32[2,10,512]{2,1,0:T(8,128)S(1)}, u32[]{:S(2)}, u32[]{:S(2)}) collective-permute-start(f32[2,10,512]{2,1,0:T(8,128)S(1)} %get-tuple-element.97), channel_id=1, source_target_pairs={{0,8},{8,16},{16,24},{24,32},{32,40},{40,48},{48,56},{56,64},{64,7... | collective-permute-start | bytes 122888 | tf_op jit(solution)/shard_map/ppermute | solution.py:116
  45.7 8.1 %copy-start.34 = (s32[8,3]{0,1:T(4,128)S(1)}, s32[8,3]{0,1:T(4,128)}, u32[]{:S(2)}) copy-start(s32[8,3]{0,1:T(4,128)} %param.21) | copy-start | bytes 292
  45.7 8.1 %copy-start.30 = (f32[1,64,128]{2,1,0:T(8,128)S(1)}, f32[1,64,128]{2,1,0:T(8,128)}, u32[]{:S(2)}) copy-start(f32[1,64,128]{2,1,0:T(8,128)} %param.24) | copy-start | bytes 98308
  45.7 8.1 %copy-start.36 = (s32[1,64]{1,0:T(1,128)S(1)}, s32[1,64]{1,0:T(1,128)}, u32[]{:S(2)}) copy-start(s32[1,64]{1,0:T(1,128)} %param.25) | copy-start | bytes 772
  47.1 147.4 %copy-start.11 = (f32[2,8,512]{2,1,0:T(8,128)}, f32[2,8,512]{2,1,0:T(8,128)S(1)}, u32[]{:S(2)}) copy-start(f32[2,8,512]{2,1,0:T(8,128)S(1)} %get-tuple-element.64) | copy-start | bytes 98308
  47.1 147.4 %copy-start.13 = (f32[2,8,512]{2,1,0:T(8,128)}, f32[2,8,512]{2,1,0:T(8,128)S(1)}, u32[]{:S(2)}) copy-start(f32[2,8,512]{2,1,0:T(8,128)S(1)} %get-tuple-element.65) | copy-start | bytes 98308
  53.8 5.4 copy-start.35
  53.9 5.5 copy-start.27
  56.4 138.1 %copy-start.7 = (f32[2,8,512]{2,1,0:T(8,128)}, f32[2,8,512]{2,1,0:T(8,128)S(1)}, u32[]{:S(2)}) copy-start(f32[2,8,512]{2,1,0:T(8,128)S(1)} %pad_convert_fusion) | copy-start | bytes 98308
  57.7 136.8 %copy-start.9 = (f32[2,8,512]{2,1,0:T(8,128)}, f32[2,8,512]{2,1,0:T(8,128)S(1)}, u32[]{:S(2)}) copy-start(f32[2,8,512]{2,1,0:T(8,128)S(1)} %maximum_convert_fusion) | copy-start | bytes 98308
  59.2 135.4 %copy-start.5 = (f32[2,2,8,512]{3,2,1,0:T(8,128)S(1)}, f32[2,2,8,512]{3,2,1,0:T(8,128)}, u32[]{:S(2)}) copy-start(f32[2,2,8,512]{3,2,1,0:T(8,128)} %param.14) | copy-start | bytes 196612
  65.4 133.4 %copy-start.1 = (bf16[8,128,128]{2,1,0:T(8,128)(2,1)S(1)}, bf16[8,128,128]{2,1,0:T(8,128)(2,1)}, u32[]{:S(2)}) copy-start(bf16[8,128,128]{2,1,0:T(8,128)(2,1)} %param.20) | copy-start | bytes 786436
  66.2 130.1 %all-to-all-start.1 = ((f32[64,4,128]{2,1,0:T(4,128)}), f32[64,4,128]{2,1,0:T(4,128)S(1)}, u32[]{:S(2)}, u32[]{:S(2)}) async-start(f32[64,4,128]{2,1,0:T(4,128)} %maximum_bitcast_fusion), calls=%async_computation.1 | async-start | bytes 262144 | tf_op jit(solution)/shard_map/all_to_all | solution.py:109
  80.3 270.9 %all-reduce.13.cloned.1.call-start = ((), (), s32[]{:S(2)}) async-start(), calls=%async_computation.5 | async-start | bytes 262144 | tf_op jit(solution)/shard_map/psum | solution.py:124
  196.3 4.0 copy-start.2
  200.3 1.5 copy-start.6
  204.7 3.2 copy-start.33
  207.2 145.0 %copy-start.8 = (f32[2,8,512]{2,1,0:T(8,128)S(1)}, f32[2,8,512]{2,1,0:T(8,128)}, u32[]{:S(2)}) copy-start(f32[2,8,512]{2,1,0:T(8,128)} %copy-done.7) | copy-start | bytes 98308
  207.2 145.0 %copy-start.10 = (f32[2,8,512]{2,1,0:T(8,128)S(1)}, f32[2,8,512]{2,1,0:T(8,128)}, u32[]{:S(2)}) copy-start(f32[2,8,512]{2,1,0:T(8,128)} %copy-done.9) | copy-start | bytes 98308
  207.2 145.0 %copy-start.12 = (f32[2,8,512]{2,1,0:T(8,128)S(1)}, f32[2,8,512]{2,1,0:T(8,128)}, u32[]{:S(2)}) copy-start(f32[2,8,512]{2,1,0:T(8,128)} %copy-done.11) | copy-start | bytes 98308
  207.2 145.0 %copy-start.14 = (f32[2,8,512]{2,1,0:T(8,128)S(1)}, f32[2,8,512]{2,1,0:T(8,128)}, u32[]{:S(2)}) copy-start(f32[2,8,512]{2,1,0:T(8,128)} %copy-done.13) | copy-start | bytes 98308
  213.5 20.2 %collective-permute-start.4 = (f32[2,10,512]{2,1,0:T(8,128)}, f32[2,10,512]{2,1,0:T(8,128)}, u32[]{:S(2)}, u32[]{:S(2)}) collective-permute-start(f32[2,10,512]{2,1,0:T(8,128)} %get-tuple-element.90), channel_id=1, source_target_pairs={{0,8},{8,16},{16,24},{24,32},{32,40},{40,48},{48,56},{56,64},{64,7... | collective-permute-start | bytes 122888 | tf_op jit(solution)/shard_map/ppermute | solution.py:116
  215.4 19.1 %collective-permute-start.5 = (f32[2,10,512]{2,1,0:T(8,128)}, f32[2,10,512]{2,1,0:T(8,128)}, u32[]{:S(2)}, u32[]{:S(2)}) collective-permute-start(f32[2,10,512]{2,1,0:T(8,128)} %get-tuple-element.91), channel_id=1, source_target_pairs={{8,0},{16,8},{24,16},{32,24},{40,32},{48,40},{56,48},{64,56},{72,6... | collective-permute-start | bytes 122888 | tf_op jit(solution)/shard_map/ppermute | solution.py:119
  228.1 125.8 %all-to-all-start.2 = ((f32[64,4,128]{2,1,0:T(4,128)}), f32[64,4,128]{2,1,0:T(4,128)}, u32[]{:S(2)}, u32[]{:S(2)}) async-start(f32[64,4,128]{2,1,0:T(4,128)} %maximum_bitcast_fusion.1), calls=%async_computation.2 | async-start | bytes 262144 | tf_op jit(solution)/shard_map/all_to_all | solution.py:109
  353.9 4.4 copy-start.3
  358.3 3.6 copy-start.20
  374.1 2.6 copy-start.22
  376.6 171.1 %copy-start.15 = (f32[2,8,512]{2,1,0:T(8,128)S(1)}, f32[2,8,512]{2,1,0:T(8,128)}, u32[]{:S(2)}) copy-start(f32[2,8,512]{2,1,0:T(8,128)} %get-tuple-element.66) | copy-start | bytes 98308
  376.6 171.1 %copy-start.16 = (f32[2,8,512]{2,1,0:T(8,128)S(1)}, f32[2,8,512]{2,1,0:T(8,128)}, u32[]{:S(2)}) copy-start(f32[2,8,512]{2,1,0:T(8,128)} %maximum_convert_fusion.1) | copy-start | bytes 98308
  376.6 171.1 %copy-start.17 = (f32[2,2,7,512]{3,2,1,0:T(8,128)S(1)}, f32[2,2,7,512]{3,2,1,0:T(8,128)}, u32[]{:S(2)}) copy-start(f32[2,2,7,512]{3,2,1,0:T(8,128)} %get-tuple-element.38) | copy-start | bytes 172036
  376.6 171.1 %copy-start.18 = (f32[2,2,7,512]{3,2,1,0:T(8,128)S(1)}, f32[2,2,7,512]{3,2,1,0:T(8,128)}, u32[]{:S(2)}) copy-start(f32[2,2,7,512]{3,2,1,0:T(8,128)} %get-tuple-element.39) | copy-start | bytes 172036
  376.6 171.1 %copy-start.21 = (f32[2,2,8,511]{3,2,1,0:T(8,128)S(1)}, f32[2,2,8,511]{3,2,1,0:T(8,128)}, u32[]{:S(2)}) copy-start(f32[2,2,8,511]{3,2,1,0:T(8,128)} %fusion.92) | copy-start | bytes 196228
  376.6 171.1 %copy-start.25 = (f32[2,1,8,512]{3,2,0,1:T(8,128)S(1)}, f32[2,1,8,512]{3,2,0,1:T(8,128)}, u32[]{:S(2)}) copy-start(f32[2,1,8,512]{3,2,0,1:T(8,128)} %get-tuple-element.34) | copy-start | bytes 98308
  376.6 171.1 %copy-start.26 = (f32[2,1,8,512]{3,2,0,1:T(8,128)S(1)}, f32[2,1,8,512]{3,2,0,1:T(8,128)}, u32[]{:S(2)}) copy-start(f32[2,1,8,512]{3,2,0,1:T(8,128)} %get-tuple-element.37) | copy-start | bytes 98308
  376.7 171.4 %copy-start.24 = (bf16[8192,8]{0,1:T(8,128)(2,1)S(1)}, bf16[8192,8]{0,1:T(8,128)(2,1)}, u32[]{:S(2)}) copy-start(bf16[8192,8]{0,1:T(8,128)(2,1)} %get-tuple-element.70) | copy-start | bytes 393220
  376.7 171.4 %copy-start.29 = (s32[8192]{0:T(1024)S(1)}, s32[8192]{0:T(1024)}, u32[]{:S(2)}) copy-start(s32[8192]{0:T(1024)} %copy-done.28) | copy-start | bytes 98308
  377.5 170.4 %all-to-all-start.3 = ((f32[64,4,128]{2,1,0:T(4,128)}), f32[64,4,128]{2,1,0:T(4,128)S(1)}, u32[]{:S(2)}, u32[]{:S(2)}) async-start(f32[64,4,128]{2,1,0:T(4,128)} %maximum_bitcast_fusion.2), calls=%async_computation.3 | async-start | bytes 262144 | tf_op jit(solution)/shard_map/all_to_all | solution.py:109
  383.5 163.3 %all-reduce.15.cloned.1.call-start = ((), (), s32[]{:S(2)}) async-start(), calls=%async_computation.6 | async-start | bytes 262144 | tf_op jit(solution)/shard_map/psum | solution.py:124
  384.4 13.1 %collective-permute-start.7 = (f32[2,10,512]{2,1,0:T(8,128)S(1)}, f32[2,10,512]{2,1,0:T(8,128)S(1)}, u32[]{:S(2)}, u32[]{:S(2)}) collective-permute-start(f32[2,10,512]{2,1,0:T(8,128)S(1)} %get-tuple-element.86), channel_id=1, source_target_pairs={{8,0},{16,8},{24,16},{32,24},{40,32},{48,40},{56,48},{64,56},{72,6... | collective-permute-start | bytes 122888 | tf_op jit(solution)/shard_map/ppermute | solution.py:119
  394.1 13.1 %collective-permute-start.6 = (f32[2,10,512]{2,1,0:T(8,128)S(1)}, f32[2,10,512]{2,1,0:T(8,128)S(1)}, u32[]{:S(2)}, u32[]{:S(2)}) collective-permute-start(f32[2,10,512]{2,1,0:T(8,128)S(1)} %get-tuple-element.87), channel_id=1, source_target_pairs={{0,8},{8,16},{16,24},{24,32},{32,40},{40,48},{48,56},{56,64},{64,7... | collective-permute-start | bytes 122888 | tf_op jit(solution)/shard_map/ppermute | solution.py:116
  408.0 141.4 %copy-start.4 = (bf16[8192,64]{0,1:T(8,128)(2,1)S(1)}, bf16[8192,64]{0,1:T(8,128)(2,1)}, u32[]{:S(2)}) copy-start(bf16[8192,64]{0,1:T(8,128)(2,1)} %get-tuple-element.75) | copy-start | bytes 3145732
  (4 other events, 3.5 us)
Sparse Core Ops, SparseCore 0:
  38.5 155.0 all-reduce.10
  208.8 142.4 all-reduce.12
  397.6 149.1 all-reduce.14

commit v2 on v0

--- a/solution.py
+++ b/solution.py
@@ -3,8 +3,12 @@
 from jax import lax
 from jax.sharding import PartitionSpec as P
 
+from jax.experimental import pallas as pl
+from jax.experimental.pallas import tpu as pltpu
+
 
 ITERS = 3
+INTERPRET = False
 
 
 def shifted(value, axis, steps):
@@ -34,6 +38,60 @@
     spread = parts[:, :, None] * row_onehot[None]
     placed = jnp.einsum("gkr,kc->grc", spread, col_mask, preferred_element_type=jnp.float32)
     return placed[:fields] + placed[fields:]
+
+
+def rock_kernel(
+    rock_ref, source_ref, leak_ref, below_ref, above_ref, left_ref, right_ref, coef_ref, inv_ref,
+    out_ref, low_ref, high_ref, first_ref, last_ref,
+):
+    depth, rows, lanes = rock_ref.shape[1:]
+    row = lax.broadcasted_iota(jnp.int32, (rows, lanes), 0)
+    lane = lax.broadcasted_iota(jnp.int32, (rows, lanes), 1)
+    for z in range(depth):
+        coef = [coef_ref[d, z].astype(jnp.float32) for d in range(6)]
+        rhs = []
+        for f in range(2):
+            here = rock_ref[f, z]
+            down = below_ref[f] if z == 0 else rock_ref[f, z - 1]
+            up = above_ref[f] if z == depth - 1 else rock_ref[f, z + 1]
+            west = jnp.where(row == 0, left_ref[f, z][None, :], pltpu.roll(here, 1, 0))
+            east = jnp.where(row == rows - 1, right_ref[f, z][None, :], pltpu.roll(here, rows - 1, 0))
+            south = jnp.where(lane == 0, 0.0, pltpu.roll(here, 1, 1))
+            north = jnp.where(lane == lanes - 1, 0.0, pltpu.roll(here, lanes - 1, 1))
+            total = coef[0] * down + coef[1] * up + coef[2] * west + coef[3] * east
+            total = total + coef[4] * south + coef[5] * north
+            rhs.append(source_ref[f, z] + total + leak_ref[f, z])
+        inv = [inv_ref[i, z].astype(jnp.float32) for i in range(4)]
+        for f in range(2):
+            value = inv[2 * f] * rhs[0] + inv[2 * f + 1] * rhs[1]
+            out_ref[f, z] = value
+            first_ref[f, z] = value[0]
+            last_ref[f, z] = value[rows - 1]
+            if z == 0:
+                low_ref[f] = value
+            if z == depth - 1:
+                high_ref[f] = value
+
+
+def rock_step(rock, source, leak, below, above, left, right, coef, inverse):
+    fields, depth, rows, lanes = rock.shape
+    vmem = pl.BlockSpec(memory_space=pltpu.VMEM)
+    return pl.pallas_call(
+        rock_kernel,
+        out_shape=(
+            jax.ShapeDtypeStruct(rock.shape, jnp.float32),
+            jax.ShapeDtypeStruct((fields, rows, lanes), jnp.float32),
+            jax.ShapeDtypeStruct((fields, rows, lanes), jnp.float32),
+            jax.ShapeDtypeStruct((fields, depth, lanes), jnp.float32),
+            jax.ShapeDtypeStruct((fields, depth, lanes), jnp.float32),
+        ),
+        in_specs=[vmem] * 9,
+        out_specs=(vmem,) * 5,
+        cost_estimate=pl.CostEstimate(
+            flops=40 * rock.size, transcendentals=0, bytes_accessed=20 * rock.size
+        ),
+        interpret=INTERPRET,
+    )(rock, source, leak, below, above, left, right, coef, inverse)
 
 
 def shards(
@@ -98,9 +156,13 @@
     backward_slab = [(i + 1, i) for i in range(slab_count - 1)]
     forward_plane = [(i, i + 1) for i in range(plane_count - 1)]
     backward_plane = [(i + 1, i) for i in range(plane_count - 1)]
+    coef_all = jnp.stack([coef_z, upper_z, coef_x, upper_x, coef_y, upper_y])
     rock_now = rock_state
+    rock_low, rock_high = rock_now[:, 0], rock_now[:, -1]
+    rock_first, rock_last = rock_now[:, :, 0], rock_now[:, :, -1]
     fracture_now = fracture_state
     source_blocks = fracture_source.reshape(2, blocks, segment_width)
+    layer_rows = rock_now.shape[2]
     for _ in range(ITERS):
         rock_table = rock_now.reshape(2, cell_rows, 128)
         rock_picked = pick_values(cell_row_onehot, cell_col_mask, rock_table)
@@ -116,16 +178,13 @@
         fracture_low = fracture_now.astype(jnp.bfloat16).reshape(2, blocks, segment_width)
         fracture_wide = fracture_low.astype(jnp.float32).reshape(2, -1, rock_now.shape[-1])
         from_below = lax.ppermute(
-            jnp.concatenate([rock_now[:, -1], fracture_wide], 1), "slab", forward_slab
+            jnp.concatenate([rock_high, fracture_wide], 1), "slab", forward_slab
         )
         from_above = lax.ppermute(
-            jnp.concatenate([rock_now[:, 0], fracture_wide], 1), "slab", backward_slab
-        )
-        from_left = lax.ppermute(rock_now[:, :, -1], "plane", forward_plane)
-        from_right = lax.ppermute(rock_now[:, :, 0], "plane", backward_plane)
-        layer_rows = rock_now.shape[2]
-        rock_below = from_below[:, None, :layer_rows]
-        rock_above = from_above[:, None, :layer_rows]
+            jnp.concatenate([rock_low, fracture_wide], 1), "slab", backward_slab
+        )
+        from_left = lax.ppermute(rock_last, "plane", forward_plane)
+        from_right = lax.ppermute(rock_first, "plane", backward_plane)
         fracture_prev = from_below[:, layer_rows:].reshape(fracture_low.shape).astype(jnp.bfloat16)
         fracture_next_part = from_above[:, layer_rows:].reshape(
             fracture_low.shape
@@ -138,16 +197,6 @@
             "bkij,fbkj->fbi", fracture_coupling, gathered, preferred_element_type=jnp.float32
         )
         fracture_part = lax.optimization_barrier(source_blocks - coupled)
-        below_z = jnp.concatenate([rock_below, rock_now[:, :-1]], 1)
-        above_z = jnp.concatenate([rock_now[:, 1:], rock_above], 1)
-        below_x = jnp.concatenate([from_left[:, :, None], rock_now[:, :, :-1]], 2)
-        above_x = jnp.concatenate([rock_now[:, :, 1:], from_right[:, :, None]], 2)
-        below_y = jnp.pad(rock_now[..., :-1], ((0, 0), (0, 0), (0, 0), (1, 0)))
-        above_y = jnp.pad(rock_now[..., 1:], ((0, 0), (0, 0), (0, 0), (0, 1)))
-        total = coef_z * below_z + upper_z * above_z
-        total = total + coef_x * below_x + upper_x * above_x
-        total = total + coef_y * below_y + upper_y * above_y
-        rock_part = lax.optimization_barrier(rock_source + total)
         leak_fracture = place_values(segment_row_onehot, segment_col_mask, got_rock)
         leak_rock = place_values(
             cell_row_onehot, cell_col_mask, slot_weight_flat[None] * got_fracture
@@ -156,12 +205,16 @@
         fracture_next = jnp.einsum(
             "bij,fbj->fbi", fracture_inverse, fracture_rhs, preferred_element_type=jnp.float32
         ).reshape(2, -1)
-        rock_rhs = rock_part + leak_rock
-        rock_now = jnp.stack(
-            [
-                cell_inverse[0] * rock_rhs[0] + cell_inverse[1] * rock_rhs[1],
-                cell_inverse[2] * rock_rhs[0] + cell_inverse[3] * rock_rhs[1],
-            ]
+        rock_now, rock_low, rock_high, rock_first, rock_last = rock_step(
+            rock_now,
+            rock_source,
+            leak_rock,
+            from_below[:, :layer_rows],
+            from_above[:, :layer_rows],
+            from_left,
+            from_right,
+            coef_all,
+            cell_inverse,
         )
         fracture_now = fracture_next
     return (rock_now, fracture_now)

time: 254 us -> 217 us (0.85)
  the two profiles are of different devices: /device:TPU:6 before, /device:TPU:30 now
where the time goes in v2:
time: 217 us; the launch traced here: 215 us
  starting transfers between devices  144 us (66%)
  matrix products  26.6 us (12%)
  local copies, waits for them, and re-layouts  19.6 us (9%)
  waiting for transfers between devices  9.18 us (4%)
  other arithmetic  8.76 us (4%)
  Pallas kernels  5.43 us (3%)
    all_to_all x3, starting transfers between devices, shards(): lax.all_to_all(send.transpose(1, 0, 2), 'slab', split_axis=0, concat_axis...  35 us
    ppermute x3, starting transfers between devices, shards(): from_right = lax.ppermute(rock_first, 'plane', backward_plane)  29.5 us
    ppermute x3, starting transfers between devices, shards(): lax.ppermute(jnp.concatenate([rock_low, fracture_wide], 1), 'slab', backw...  22 us
    ppermute x2, starting transfers between devices, shifted(): lax.ppermute(value, axis, [(source, source + steps) for source in range(f...  18.2 us
    ppermute x3, starting transfers between devices, shards(): from_left = lax.ppermute(rock_last, 'plane', forward_plane)  17 us
    all_to_all x1, starting transfers between devices, shards(): lax.all_to_all(contact_segment[0], 'slab', split_axis=0, concat_axis=0, t...  16.3 us
    dot_general x6, matrix products, pick_values(): jnp.einsum('kc,grc->gkr', col_mask, parts, preferred_element_type=jnp.flo...  14.4 us
    dot_general x6, matrix products, place_values(): jnp.einsum('gkr,kc->grc', spread, col_mask, preferred_element_type=jnp.fl...  9.18 us
  transfers between devices with their start and end apart: 18, of which 1 were waited for; matrix products, arithmetic and copies ran while one was open for 20% of the time, Pallas kernels for 0%

profile of v2, /device:TPU:30, one launch (start us, length us, event | category | flops | bytes accessed | tf_op | source)
XLA Modules:
  0.0 215.2 jit_solution(8466420564627541398)
XLA Ops:
  0.7 16.3 %all-to-all-start = ((s32[64,1,128]{2,1,0:T(1,128)}), s32[64,1,128]{2,1,0:T(1,128)S(1)}, u32[]{:S(2)}, u32[]{:S(2)}) async-start(s32[64,1,128]{2,1,0:T(1,128)} %bitcast.280), calls=%async_computation | async-start | bytes 65536 | tf_op jit(solution)/shard_map/all_to_all | solution.py:121
  17.0 1.3 slice_bitcast_fusion.12
  18.3 8.5 %collective-permute-start.5 = (bf16[2,1,512]{2,1,0:T(2,128)(2,1)}, bf16[2,1,512]{2,1,0:T(2,128)(2,1)S(1)}, u32[]{:S(2)}, u32[]{:S(2)}) collective-permute-start(bf16[2,1,512]{2,1,0:T(2,128)(2,1)} %slice_bitcast_fusion.12), channel_id=1, source_target_pairs={{1,0},{2,1},{3,2},{4,3},{5,4},{6,5},{7,6},{9,8},{10,9},{11,10},{12... | collective-permute-start | bytes 6152 | tf_op jit(solution)/shard_map/ppermute | solution.py:17
  27.5 9.7 %collective-permute-start.4 = (bf16[1,8,512]{2,1,0:T(8,128)(2,1)S(1)}, bf16[1,8,512]{2,1,0:T(8,128)(2,1)S(1)}, u32[]{:S(2)}, u32[]{:S(2)}) collective-permute-start(bf16[1,8,512]{2,1,0:T(8,128)(2,1)S(1)} %get-tuple-element.56), channel_id=1, source_target_pairs={{8,0},{16,8},{24,16},{32,24},{40,32},{48,40},{56,48},{64,56},{72,6... | collective-permute-start | bytes 24584 | tf_op jit(solution)/shard_map/ppermute | solution.py:17
  37.2 0.9 fusion.177
  38.7 6.1 %collective-permute-start.2 = (f32[2,2,512]{2,1,0:T(2,128)}, f32[2,2,512]{2,1,0:T(2,128)}, u32[]{:S(2)}, u32[]{:S(2)}) collective-permute-start(f32[2,2,512]{2,1,0:T(2,128)} %bitcast.272), channel_id=1, source_target_pairs={{0,1},{1,2},{2,3},{3,4},{4,5},{5,6},{6,7},{8,9},{9,10},{10,11},{11... | collective-permute-start | bytes 24584 | tf_op jit(solution)/shard_map/ppermute | solution.py:186
  45.4 9.4 %collective-permute-start.3 = (f32[2,2,512]{2,1,0:T(2,128)}, f32[2,2,512]{2,1,0:T(2,128)}, u32[]{:S(2)}, u32[]{:S(2)}) collective-permute-start(f32[2,2,512]{2,1,0:T(2,128)} %bitcast.271), channel_id=1, source_target_pairs={{1,0},{2,1},{3,2},{4,3},{5,4},{6,5},{7,6},{9,8},{10,9},{11,10},{12... | collective-permute-start | bytes 24584 | tf_op jit(solution)/shard_map/ppermute | solution.py:187
  54.7 0.8 slice_bitcast_fusion.6
  56.9 2.0 collective-permute-start.1
  58.9 0.8 reshape.303
  60.5 1.3 reduce-precision_convert_fusion.11
  61.8 0.8 add_select_fusion.3
  62.6 1.3 fusion.82
  64.0 2.5 %fusion.29 = f32[4,8192]{1,0:T(4,128)S(1)} fusion(f32[8192,64]{0,1:T(8,128)S(1)} %get-tuple-element.61, s32[8192]{0:T(1024)S(1)} %get-tuple-element.59, bf16[2,64,128]{2,1,0:T(8,128)(2,1)S(1)} %get-tuple-element.51, bf16[2,64,128]{2,1,0:T(8,128)(2,1)S(1)} %get-tuple-element.50), kind=kOutput, calls=%fused_computation.25 | convolution fusion | flops 542113792 | bytes 2326528 | tf_op jit(solution)/shard_map/kc,grc->gkr/dot_general | solution.py:29
  67.7 2.3 %collective-permute-start = (f32[2,10,512]{2,1,0:T(8,128)S(1)}, f32[2,10,512]{2,1,0:T(8,128)}, u32[]{:S(2)}, u32[]{:S(2)}) collective-permute-start(f32[2,10,512]{2,1,0:T(8,128)S(1)} %get-tuple-element.82), channel_id=1, source_target_pairs={{0,8},{8,16},{16,24},{24,32},{32,40},{40,48},{48,56},{56,64},{64,7... | collective-permute-start | bytes 122888 | tf_op jit(solution)/shard_map/ppermute | solution.py:180
  70.3 2.8 %fusion.57 = f32[4,8192]{1,0:T(4,128)S(1)} fusion(s32[8192]{0:T(1024)S(1)} %get-tuple-element.64, f32[8192,8]{0,1:T(8,128)S(1)} %get-tuple-element.58, bf16[2,8,128]{2,1,0:T(8,128)(2,1)} %get-tuple-element.84, bf16[2,8,128]{2,1,0:T(8,128)(2,1)} %get-tuple-element.83), kind=kOutput, calls=%fused_computation.48 | convolution fusion | flops 68653056 | bytes 434176 | tf_op jit(solution)/shard_map/kc,grc->gkr/dot_general | solution.py:29
  73.9 13.6 %all-to-all-start.1 = ((f32[64,4,128]{2,1,0:T(4,128)}), f32[64,4,128]{2,1,0:T(4,128)S(1)}, u32[]{:S(2)}, u32[]{:S(2)}) async-start(f32[64,4,128]{2,1,0:T(4,128)} %maximum_bitcast_fusion), calls=%async_computation.1 | async-start | bytes 262144 | tf_op jit(solution)/shard_map/all_to_all | solution.py:173
  87.6 0.8 slice.352
  89.5 1.4 slice.234.below_ref
  90.9 9.1 %all-to-all-done.1 = f32[64,4,128]{2,1,0:T(4,128)S(1)} async-done(((f32[64,4,128]{2,1,0:T(4,128)}), f32[64,4,128]{2,1,0:T(4,128)S(1)}, u32[]{:S(2)}, u32[]{:S(2)}) %all-to-all-start.1) | async-done | bytes 131104 | tf_op jit(solution)/shard_map/all_to_all | solution.py:173
  100.2 1.3 fusion.26
  101.6 1.5 fusion.10
  104.1 1.8 shard_map.140
  105.9 0.8 reshape.309
  106.8 2.5 %fusion.32 = f32[4,8192]{1,0:T(4,128)S(1)} fusion(f32[8192,64]{0,1:T(8,128)S(1)} %get-tuple-element.61, s32[8192]{0:T(1024)S(1)} %get-tuple-element.59, bf16[2,64,128]{2,1,0:T(8,128)(2,1)S(1)} %get-tuple-element.45, bf16[2,64,128]{2,1,0:T(8,128)(2,1)S(1)} %get-tuple-element.44), kind=kOutput, calls=%fused_computation.26 | convolution fusion | flops 542113792 | bytes 2326528 | tf_op jit(solution)/shard_map/kc,grc->gkr/dot_general | solution.py:29
  109.3 2.1 fusion.60
  112.2 8.0 %all-to-all-start.2 = ((f32[64,4,128]{2,1,0:T(4,128)}), f32[64,4,128]{2,1,0:T(4,128)S(1)}, u32[]{:S(2)}, u32[]{:S(2)}) async-start(f32[64,4,128]{2,1,0:T(4,128)} %maximum_bitcast_fusion.1), calls=%async_computation.2 | async-start | bytes 262144 | tf_op jit(solution)/shard_map/all_to_all | solution.py:173
  120.3 10.0 %collective-permute-start.7 = (f32[2,10,512]{2,1,0:T(8,128)S(1)}, f32[2,10,512]{2,1,0:T(8,128)S(1)}, u32[]{:S(2)}, u32[]{:S(2)}) collective-permute-start(f32[2,10,512]{2,1,0:T(8,128)S(1)} %get-tuple-element.75), channel_id=1, source_target_pairs={{8,0},{16,8},{24,16},{32,24},{40,32},{48,40},{56,48},{64,56},{72,6... | collective-permute-start | bytes 122888 | tf_op jit(solution)/shard_map/ppermute | solution.py:183
  130.2 1.9 collective-permute-start.6
  132.2 5.7 %collective-permute-start.8 = (f32[2,2,512]{2,1,0:T(2,128)}, f32[2,2,512]{2,1,0:T(2,128)S(1)}, u32[]{:S(2)}, u32[]{:S(2)}) collective-permute-start(f32[2,2,512]{2,1,0:T(2,128)} %get-tuple-element.16), channel_id=1, source_target_pairs={{0,1},{1,2},{2,3},{3,4},{4,5},{5,6},{6,7},{8,9},{9,10},{10,11},{11... | collective-permute-start | bytes 24584 | tf_op jit(solution)/shard_map/ppermute | solution.py:186
  137.9 9.9 %collective-permute-start.9 = (f32[2,2,512]{2,1,0:T(2,128)}, f32[2,2,512]{2,1,0:T(2,128)}, u32[]{:S(2)}, u32[]{:S(2)}) collective-permute-start(f32[2,2,512]{2,1,0:T(2,128)} %get-tuple-element.17), channel_id=1, source_target_pairs={{1,0},{2,1},{3,2},{4,3},{5,4},{6,5},{7,6},{9,8},{10,9},{11,10},{12... | collective-permute-start | bytes 24584 | tf_op jit(solution)/shard_map/ppermute | solution.py:187
  147.9 0.8 slice.350
  149.8 1.4 slice.250.below_ref
  151.4 2.3 %fusion.23 = f32[4,8,128]{2,1,0:T(8,128)S(1)} fusion(s32[8192]{0:T(1024)S(1)} %get-tuple-element.64, bf16[4,8192]{1,0:T(4,128)(2,1)S(1)} %pad_maximum_fusion.9, bf16[8192,8]{0,1:T(8,128)(2,1)} %copy-done.10), kind=kOutput, calls=%fused_computation.23 | convolution fusion | flops 68419584 | bytes 245760 | tf_op jit(solution)/shard_map/gkr,kc->grc/dot_general | solution.py:39
  153.9 2.1 fusion.63
  156.2 1.5 fusion.8
  158.9 1.8 shard_map.141
  160.7 0.8 reshape.318
  161.6 2.5 %fusion.35 = f32[4,8192]{1,0:T(4,128)S(1)} fusion(f32[8192,64]{0,1:T(8,128)S(1)} %get-tuple-element.61, s32[8192]{0:T(1024)S(1)} %get-tuple-element.59, bf16[2,64,128]{2,1,0:T(8,128)(2,1)S(1)} %get-tuple-element.43, bf16[2,64,128]{2,1,0:T(8,128)(2,1)S(1)} %get-tuple-element.42), kind=kOutput, calls=%fused_computation.27 | convolution fusion | flops 542113792 | bytes 2326528 | tf_op jit(solution)/shard_map/kc,grc->gkr/dot_general | solution.py:29
  164.9 13.4 %all-to-all-start.3 = ((f32[64,4,128]{2,1,0:T(4,128)}), f32[64,4,128]{2,1,0:T(4,128)S(1)}, u32[]{:S(2)}, u32[]{:S(2)}) async-start(f32[64,4,128]{2,1,0:T(4,128)} %maximum_bitcast_fusion.2), calls=%async_computation.3 | async-start | bytes 262144 | tf_op jit(solution)/shard_map/all_to_all | solution.py:173
  178.4 10.0 %collective-permute-start.11 = (f32[2,10,512]{2,1,0:T(8,128)S(1)}, f32[2,10,512]{2,1,0:T(8,128)S(1)}, u32[]{:S(2)}, u32[]{:S(2)}) collective-permute-start(f32[2,10,512]{2,1,0:T(8,128)S(1)} %get-tuple-element.71), channel_id=1, source_target_pairs={{8,0},{16,8},{24,16},{32,24},{40,32},{48,40},{56,48},{64,56},{72,6... | collective-permute-start | bytes 122888 | tf_op jit(solution)/shard_map/ppermute | solution.py:183
  188.4 1.9 collective-permute-start.10
  190.3 5.2 %collective-permute-start.12 = (f32[2,2,512]{2,1,0:T(2,128)S(1)}, f32[2,2,512]{2,1,0:T(2,128)S(1)}, u32[]{:S(2)}, u32[]{:S(2)}) collective-permute-start(f32[2,2,512]{2,1,0:T(2,128)S(1)} %copy-done.28), channel_id=1, source_target_pairs={{0,1},{1,2},{2,3},{3,4},{4,5},{5,6},{6,7},{8,9},{9,10},{10,11},{11... | collective-permute-start | bytes 24584 | tf_op jit(solution)/shard_map/ppermute | solution.py:186
  195.5 10.2 %collective-permute-start.13 = (f32[2,2,512]{2,1,0:T(2,128)S(1)}, f32[2,2,512]{2,1,0:T(2,128)S(1)}, u32[]{:S(2)}, u32[]{:S(2)}) collective-permute-start(f32[2,2,512]{2,1,0:T(2,128)S(1)} %copy-done.27), channel_id=1, source_target_pairs={{1,0},{2,1},{3,2},{4,3},{5,4},{6,5},{7,6},{9,8},{10,9},{11,10},{12... | collective-permute-start | bytes 24584 | tf_op jit(solution)/shard_map/ppermute | solution.py:187
  207.8 1.3 fusion.20
  209.2 1.5 fusion.6
  210.7 0.9 convolution_bitcast_fusion.6
  213.4 1.8 shard_map.142
  (153 shorter events, 17.3 us)
Async XLA Ops:
  0.6 87.9 %copy-start = (bf16[8,3,128,128]{3,2,1,0:T(8,128)(2,1)S(1)}, bf16[8,3,128,128]{3,2,1,0:T(8,128)(2,1)}, u32[]{:S(2)}) copy-start(bf16[8,3,128,128]{3,2,1,0:T(8,128)(2,1)} %param.19) | copy-start | bytes 2359300
  0.6 63.3 %copy-start.26 = (s32[1,64]{1,0:T(1,128)S(1)}, s32[1,64]{1,0:T(1,128)}, u32[]{:S(2)}) copy-start(s32[1,64]{1,0:T(1,128)} %param.25) | copy-start | bytes 772
  0.7 63.3 %copy-start.17 = (f32[1,64,128]{2,1,0:T(8,128)S(1)}, f32[1,64,128]{2,1,0:T(8,128)}, u32[]{:S(2)}) copy-start(f32[1,64,128]{2,1,0:T(8,128)} %param.24) | copy-start | bytes 98308
  0.7 69.5 %all-to-all-start = ((s32[64,1,128]{2,1,0:T(1,128)}), s32[64,1,128]{2,1,0:T(1,128)S(1)}, u32[]{:S(2)}, u32[]{:S(2)}) async-start(s32[64,1,128]{2,1,0:T(1,128)} %bitcast.280), calls=%async_computation | async-start | bytes 65536 | tf_op jit(solution)/shard_map/all_to_all | solution.py:121
  18.3 51.9 %collective-permute-start.5 = (bf16[2,1,512]{2,1,0:T(2,128)(2,1)}, bf16[2,1,512]{2,1,0:T(2,128)(2,1)S(1)}, u32[]{:S(2)}, u32[]{:S(2)}) collective-permute-start(bf16[2,1,512]{2,1,0:T(2,128)(2,1)} %slice_bitcast_fusion.12), channel_id=1, source_target_pairs={{1,0},{2,1},{3,2},{4,3},{5,4},{6,5},{7,6},{9,8},{10,9},{11,10},{12... | collective-permute-start | bytes 6152 | tf_op jit(solution)/shard_map/ppermute | solution.py:17
  27.5 40.2 %collective-permute-start.4 = (bf16[1,8,512]{2,1,0:T(8,128)(2,1)S(1)}, bf16[1,8,512]{2,1,0:T(8,128)(2,1)S(1)}, u32[]{:S(2)}, u32[]{:S(2)}) collective-permute-start(bf16[1,8,512]{2,1,0:T(8,128)(2,1)S(1)} %get-tuple-element.56), channel_id=1, source_target_pairs={{8,0},{16,8},{24,16},{32,24},{40,32},{48,40},{56,48},{64,56},{72,6... | collective-permute-start | bytes 24584 | tf_op jit(solution)/shard_map/ppermute | solution.py:17
  38.7 65.4 %collective-permute-start.2 = (f32[2,2,512]{2,1,0:T(2,128)}, f32[2,2,512]{2,1,0:T(2,128)}, u32[]{:S(2)}, u32[]{:S(2)}) collective-permute-start(f32[2,2,512]{2,1,0:T(2,128)} %bitcast.272), channel_id=1, source_target_pairs={{0,1},{1,2},{2,3},{3,4},{4,5},{5,6},{6,7},{8,9},{9,10},{10,11},{11... | collective-permute-start | bytes 24584 | tf_op jit(solution)/shard_map/ppermute | solution.py:186
  45.4 58.7 %collective-permute-start.3 = (f32[2,2,512]{2,1,0:T(2,128)}, f32[2,2,512]{2,1,0:T(2,128)}, u32[]{:S(2)}, u32[]{:S(2)}) collective-permute-start(f32[2,2,512]{2,1,0:T(2,128)} %bitcast.271), channel_id=1, source_target_pairs={{1,0},{2,1},{3,2},{4,3},{5,4},{6,5},{7,6},{9,8},{10,9},{11,10},{12... | collective-permute-start | bytes 24584 | tf_op jit(solution)/shard_map/ppermute | solution.py:187
  56.9 30.6 %collective-permute-start.1 = (f32[2,10,512]{2,1,0:T(8,128)}, f32[2,10,512]{2,1,0:T(8,128)S(1)}, u32[]{:S(2)}, u32[]{:S(2)}) collective-permute-start(f32[2,10,512]{2,1,0:T(8,128)} %get-tuple-element.81), channel_id=1, source_target_pairs={{8,0},{16,8},{24,16},{32,24},{40,32},{48,40},{56,48},{64,56},{72,6... | collective-permute-start | bytes 122888 | tf_op jit(solution)/shard_map/ppermute | solution.py:183
  64.0 2.5 %copy-start.22 = (s32[8,3]{0,1:T(4,128)S(1)}, s32[8,3]{0,1:T(4,128)}, u32[]{:S(2)}) copy-start(s32[8,3]{0,1:T(4,128)} %param.21) | copy-start | bytes 292
  64.0 6.0 %copy-start.9 = (bf16[3,2,8,512]{3,2,1,0:T(8,128)(2,1)S(1)}, bf16[3,2,8,512]{3,2,1,0:T(8,128)(2,1)}, u32[]{:S(2)}) copy-start(bf16[3,2,8,512]{3,2,1,0:T(8,128)(2,1)} %param.15) | copy-start | bytes 147460
  66.5 22.1 %copy-start.12 = (f32[2,1024]{1,0:T(2,128)S(1)}, f32[2,1024]{1,0:T(2,128)}, u32[]{:S(2)}) copy-start(f32[2,1024]{1,0:T(2,128)} %param.18) | copy-start | bytes 24580
  67.7 19.9 %collective-permute-start = (f32[2,10,512]{2,1,0:T(8,128)S(1)}, f32[2,10,512]{2,1,0:T(8,128)}, u32[]{:S(2)}, u32[]{:S(2)}) collective-permute-start(f32[2,10,512]{2,1,0:T(8,128)S(1)} %get-tuple-element.82), channel_id=1, source_target_pairs={{0,8},{8,16},{16,24},{24,32},{32,40},{40,48},{48,56},{56,64},{64,7... | collective-permute-start | bytes 122888 | tf_op jit(solution)/shard_map/ppermute | solution.py:180
  70.1 18.2 %copy-start.21 = (bf16[1,2,8,128]{3,2,1,0:T(8,128)(2,1)S(1)}, bf16[1,2,8,128]{3,2,1,0:T(8,128)(2,1)}, u32[]{:S(2)}) copy-start(bf16[1,2,8,128]{3,2,1,0:T(8,128)(2,1)} %copy.152) | copy-start | bytes 12292
  70.1 18.2 %copy-start.23 = (s32[8,3]{0,1:T(4,128)S(1)}, s32[8,3]{0,1:T(4,128)}, u32[]{:S(2)}) copy-start(s32[8,3]{0,1:T(4,128)} %fusion.165) | copy-start | bytes 292
  70.3 2.9 %copy-start.6 = (f32[8192,8]{0,1:T(8,128)}, f32[8192,8]{0,1:T(8,128)S(1)}, u32[]{:S(2)}) copy-start(f32[8192,8]{0,1:T(8,128)S(1)} %get-tuple-element.58) | copy-start | bytes 786436
  70.3 31.2 %copy-start.10 = (bf16[8192,8]{0,1:T(8,128)(2,1)}, bf16[8192,8]{0,1:T(8,128)(2,1)S(1)}, u32[]{:S(2)}) copy-start(bf16[8192,8]{0,1:T(8,128)(2,1)S(1)} %get-tuple-element.57) | copy-start | bytes 393220
  73.9 26.1 %all-to-all-start.1 = ((f32[64,4,128]{2,1,0:T(4,128)}), f32[64,4,128]{2,1,0:T(4,128)S(1)}, u32[]{:S(2)}, u32[]{:S(2)}) async-start(f32[64,4,128]{2,1,0:T(4,128)} %maximum_bitcast_fusion), calls=%async_computation.1 | async-start | bytes 262144 | tf_op jit(solution)/shard_map/all_to_all | solution.py:173
  87.5 15.6 %copy-start.5 = (bf16[6,2,8,512]{3,2,1,0:T(8,128)(2,1)}, bf16[6,2,8,512]{3,2,1,0:T(8,128)(2,1)S(1)}, u32[]{:S(2)}) copy-start(bf16[6,2,8,512]{3,2,1,0:T(8,128)(2,1)S(1)} %bitcast_dynamic-update-slice_fusion.coef_ref) | copy-start | bytes 294916
  100.0 1.6 copy-start.2
  101.6 1.5 copy-start.1
  106.7 2.6 %copy-start.7 = (f32[8192,8]{0,1:T(8,128)S(1)}, f32[8192,8]{0,1:T(8,128)}, u32[]{:S(2)}) copy-start(f32[8192,8]{0,1:T(8,128)} %copy-done.6) | copy-start | bytes 786436
  109.2 11.0 %copy-start.13 = (f32[2,8,512]{2,1,0:T(8,128)S(1)}, f32[2,8,512]{2,1,0:T(8,128)}, u32[]{:S(2)}) copy-start(f32[2,8,512]{2,1,0:T(8,128)} %get-tuple-element.15) | copy-start | bytes 98308
  109.2 11.0 %copy-start.14 = (f32[2,8,512]{2,1,0:T(8,128)S(1)}, f32[2,8,512]{2,1,0:T(8,128)}, u32[]{:S(2)}) copy-start(f32[2,8,512]{2,1,0:T(8,128)} %get-tuple-element.14) | copy-start | bytes 98308
  109.3 39.4 %copy-start.24 = (s32[8,3]{0,1:T(4,128)S(1)}, s32[8,3]{0,1:T(4,128)}, u32[]{:S(2)}) copy-start(s32[8,3]{0,1:T(4,128)} %fusion.165) | copy-start | bytes 292
  112.2 39.1 %all-to-all-start.2 = ((f32[64,4,128]{2,1,0:T(4,128)}), f32[64,4,128]{2,1,0:T(4,128)S(1)}, u32[]{:S(2)}, u32[]{:S(2)}) async-start(f32[64,4,128]{2,1,0:T(4,128)} %maximum_bitcast_fusion.1), calls=%async_computation.2 | async-start | bytes 262144 | tf_op jit(solution)/shard_map/all_to_all | solution.py:173
  120.3 27.6 %collective-permute-start.7 = (f32[2,10,512]{2,1,0:T(8,128)S(1)}, f32[2,10,512]{2,1,0:T(8,128)S(1)}, u32[]{:S(2)}, u32[]{:S(2)}) collective-permute-start(f32[2,10,512]{2,1,0:T(8,128)S(1)} %get-tuple-element.75), channel_id=1, source_target_pairs={{8,0},{16,8},{24,16},{32,24},{40,32},{48,40},{56,48},{64,56},{72,6... | collective-permute-start | bytes 122888 | tf_op jit(solution)/shard_map/ppermute | solution.py:183
  130.2 17.6 %collective-permute-start.6 = (f32[2,10,512]{2,1,0:T(8,128)S(1)}, f32[2,10,512]{2,1,0:T(8,128)}, u32[]{:S(2)}, u32[]{:S(2)}) collective-permute-start(f32[2,10,512]{2,1,0:T(8,128)S(1)} %get-tuple-element.76), channel_id=1, source_target_pairs={{0,8},{8,16},{16,24},{24,32},{32,40},{40,48},{48,56},{56,64},{64,7... | collective-permute-start | bytes 122888 | tf_op jit(solution)/shard_map/ppermute | solution.py:180
  132.2 26.1 %collective-permute-start.8 = (f32[2,2,512]{2,1,0:T(2,128)}, f32[2,2,512]{2,1,0:T(2,128)S(1)}, u32[]{:S(2)}, u32[]{:S(2)}) collective-permute-start(f32[2,2,512]{2,1,0:T(2,128)} %get-tuple-element.16), channel_id=1, source_target_pairs={{0,1},{1,2},{2,3},{3,4},{4,5},{5,6},{6,7},{8,9},{9,10},{10,11},{11... | collective-permute-start | bytes 24584 | tf_op jit(solution)/shard_map/ppermute | solution.py:186
  137.9 20.4 %collective-permute-start.9 = (f32[2,2,512]{2,1,0:T(2,128)}, f32[2,2,512]{2,1,0:T(2,128)}, u32[]{:S(2)}, u32[]{:S(2)}) collective-permute-start(f32[2,2,512]{2,1,0:T(2,128)} %get-tuple-element.17), channel_id=1, source_target_pairs={{1,0},{2,1},{3,2},{4,3},{5,4},{6,5},{7,6},{9,8},{10,9},{11,10},{12... | collective-permute-start | bytes 24584 | tf_op jit(solution)/shard_map/ppermute | solution.py:187
  151.2 2.7 %copy-start.8 = (f32[8192,8]{0,1:T(8,128)S(1)}, f32[8192,8]{0,1:T(8,128)}, u32[]{:S(2)}) copy-start(f32[8192,8]{0,1:T(8,128)} %copy-done.6) | copy-start | bytes 786436
  151.4 4.7 %copy-start.3 = (bf16[8192,64]{0,1:T(8,128)(2,1)S(1)}, bf16[8192,64]{0,1:T(8,128)(2,1)}, u32[]{:S(2)}) copy-start(bf16[8192,64]{0,1:T(8,128)(2,1)} %get-tuple-element.62) | copy-start | bytes 3145732
  158.3 0.6 copy-start.18
  161.6 16.7 %copy-start.15 = (f32[2,8,512]{2,1,0:T(8,128)S(1)}, f32[2,8,512]{2,1,0:T(8,128)}, u32[]{:S(2)}) copy-start(f32[2,8,512]{2,1,0:T(8,128)} %get-tuple-element.20) | copy-start | bytes 98308
  161.6 16.7 %copy-start.16 = (f32[2,8,512]{2,1,0:T(8,128)S(1)}, f32[2,8,512]{2,1,0:T(8,128)}, u32[]{:S(2)}) copy-start(f32[2,8,512]{2,1,0:T(8,128)} %get-tuple-element.19) | copy-start | bytes 98308
  161.6 28.7 %copy-start.28 = (f32[2,2,512]{2,1,0:T(2,128)S(1)}, f32[2,2,512]{2,1,0:T(2,128)}, u32[]{:S(2)}) copy-start(f32[2,2,512]{2,1,0:T(2,128)} %get-tuple-element.21) | copy-start | bytes 24580
  161.6 33.9 %copy-start.27 = (f32[2,2,512]{2,1,0:T(2,128)S(1)}, f32[2,2,512]{2,1,0:T(2,128)}, u32[]{:S(2)}) copy-start(f32[2,2,512]{2,1,0:T(2,128)} %get-tuple-element.22) | copy-start | bytes 24580
  161.6 44.2 %copy-start.25 = (s32[8,3]{0,1:T(4,128)S(1)}, s32[8,3]{0,1:T(4,128)}, u32[]{:S(2)}) copy-start(s32[8,3]{0,1:T(4,128)} %fusion.165) | copy-start | bytes 292
  164.1 43.7 %copy-start.11 = (bf16[8192,8]{0,1:T(8,128)(2,1)S(1)}, bf16[8192,8]{0,1:T(8,128)(2,1)}, u32[]{:S(2)}) copy-start(bf16[8192,8]{0,1:T(8,128)(2,1)} %copy-done.10) | copy-start | bytes 393220
  164.2 45.0 %copy-start.4 = (bf16[8192,64]{0,1:T(8,128)(2,1)S(1)}, bf16[8192,64]{0,1:T(8,128)(2,1)}, u32[]{:S(2)}) copy-start(bf16[8192,64]{0,1:T(8,128)(2,1)} %get-tuple-element.62) | copy-start | bytes 3145732
  164.9 42.7 %all-to-all-start.3 = ((f32[64,4,128]{2,1,0:T(4,128)}), f32[64,4,128]{2,1,0:T(4,128)S(1)}, u32[]{:S(2)}, u32[]{:S(2)}) async-start(f32[64,4,128]{2,1,0:T(4,128)} %maximum_bitcast_fusion.2), calls=%async_computation.3 | async-start | bytes 262144 | tf_op jit(solution)/shard_map/all_to_all | solution.py:173
  178.4 27.4 %collective-permute-start.11 = (f32[2,10,512]{2,1,0:T(8,128)S(1)}, f32[2,10,512]{2,1,0:T(8,128)S(1)}, u32[]{:S(2)}, u32[]{:S(2)}) collective-permute-start(f32[2,10,512]{2,1,0:T(8,128)S(1)} %get-tuple-element.71), channel_id=1, source_target_pairs={{8,0},{16,8},{24,16},{32,24},{40,32},{48,40},{56,48},{64,56},{72,6... | collective-permute-start | bytes 122888 | tf_op jit(solution)/shard_map/ppermute | solution.py:183
  188.4 17.5 %collective-permute-start.10 = (f32[2,10,512]{2,1,0:T(8,128)S(1)}, f32[2,10,512]{2,1,0:T(8,128)S(1)}, u32[]{:S(2)}, u32[]{:S(2)}) collective-permute-start(f32[2,10,512]{2,1,0:T(8,128)S(1)} %get-tuple-element.72), channel_id=1, source_target_pairs={{0,8},{8,16},{16,24},{24,32},{32,40},{40,48},{48,56},{56,64},{64,7... | collective-permute-start | bytes 122888 | tf_op jit(solution)/shard_map/ppermute | solution.py:180
  190.3 21.9 %collective-permute-start.12 = (f32[2,2,512]{2,1,0:T(2,128)S(1)}, f32[2,2,512]{2,1,0:T(2,128)S(1)}, u32[]{:S(2)}, u32[]{:S(2)}) collective-permute-start(f32[2,2,512]{2,1,0:T(2,128)S(1)} %copy-done.28), channel_id=1, source_target_pairs={{0,1},{1,2},{2,3},{3,4},{4,5},{5,6},{6,7},{8,9},{9,10},{10,11},{11... | collective-permute-start | bytes 24584 | tf_op jit(solution)/shard_map/ppermute | solution.py:186
  195.5 16.7 %collective-permute-start.13 = (f32[2,2,512]{2,1,0:T(2,128)S(1)}, f32[2,2,512]{2,1,0:T(2,128)S(1)}, u32[]{:S(2)}, u32[]{:S(2)}) collective-permute-start(f32[2,2,512]{2,1,0:T(2,128)S(1)} %copy-done.27), channel_id=1, source_target_pairs={{1,0},{2,1},{3,2},{4,3},{5,4},{6,5},{7,6},{9,8},{10,9},{11,10},{12... | collective-permute-start | bytes 24584 | tf_op jit(solution)/shard_map/ppermute | solution.py:187
  212.2 0.6 copy-start.19
  212.8 0.6 copy-start.20

commit v3 on v2

--- a/solution.py
+++ b/solution.py
@@ -26,8 +26,8 @@
     fields = table.shape[0]
     high, low = split_bf16(table)
     parts = jnp.concatenate([high, low], 0)
-    by_row = jnp.einsum("kc,grc->gkr", col_mask, parts, preferred_element_type=jnp.float32)
-    picked = jnp.sum(by_row * row_onehot.astype(jnp.float32)[None], axis=-1)
+    by_row = jnp.einsum("kc,grc->grk", col_mask, parts, preferred_element_type=jnp.float32)
+    picked = jnp.sum(by_row * row_onehot.astype(jnp.float32)[None], axis=1)
     return picked[:fields] + picked[fields:]
 
 
@@ -35,16 +35,17 @@
     fields = values.shape[0]
     high, low = split_bf16(values)
     parts = jnp.concatenate([high, low], 0)
-    spread = parts[:, :, None] * row_onehot[None]
-    placed = jnp.einsum("gkr,kc->grc", spread, col_mask, preferred_element_type=jnp.float32)
+    spread = parts[:, None, :] * row_onehot[None]
+    placed = jnp.einsum("grk,kc->grc", spread, col_mask, preferred_element_type=jnp.float32)
     return placed[:fields] + placed[fields:]
 
 
 def rock_kernel(
     rock_ref, source_ref, leak_ref, below_ref, above_ref, left_ref, right_ref, coef_ref, inv_ref,
-    out_ref, low_ref, high_ref, first_ref, last_ref,
+    out_ref, low_ref, high_ref, first_ref, last_ref, table_ref,
 ):
     depth, rows, lanes = rock_ref.shape[1:]
+    tiles = leak_ref.shape[2]
     row = lax.broadcasted_iota(jnp.int32, (rows, lanes), 0)
     lane = lax.broadcasted_iota(jnp.int32, (rows, lanes), 1)
     for z in range(depth):
@@ -60,11 +61,14 @@
             north = jnp.where(lane == lanes - 1, 0.0, pltpu.roll(here, lanes - 1, 1))
             total = coef[0] * down + coef[1] * up + coef[2] * west + coef[3] * east
             total = total + coef[4] * south + coef[5] * north
-            rhs.append(source_ref[f, z] + total + leak_ref[f, z])
+            leak = jnp.concatenate([leak_ref[f, z, j] for j in range(tiles)], axis=1)
+            rhs.append(source_ref[f, z] + total + leak)
         inv = [inv_ref[i, z].astype(jnp.float32) for i in range(4)]
         for f in range(2):
             value = inv[2 * f] * rhs[0] + inv[2 * f + 1] * rhs[1]
             out_ref[f, z] = value
+            for j in range(tiles):
+                table_ref[f, z, j] = value[:, j * 128 : (j + 1) * 128]
             first_ref[f, z] = value[0]
             last_ref[f, z] = value[rows - 1]
             if z == 0:
@@ -84,9 +88,10 @@
             jax.ShapeDtypeStruct((fields, rows, lanes), jnp.float32),
             jax.ShapeDtypeStruct((fields, depth, lanes), jnp.float32),
             jax.ShapeDtypeStruct((fields, depth, lanes), jnp.float32),
+            jax.ShapeDtypeStruct(leak.shape, jnp.float32),
         ),
         in_specs=[vmem] * 9,
-        out_specs=(vmem,) * 5,
+        out_specs=(vmem,) * 6,
         cost_estimate=pl.CostEstimate(
             flops=40 * rock.size, transcendentals=0, bytes_accessed=20 * rock.size
         ),
@@ -130,15 +135,21 @@
     cell_total = rock_state[0].size
     cell_rows = cell_total // 128
     cell_flat = cell_table.reshape(-1)
+    _, depth, rows, lanes = rock_state.shape
+    tiles = lanes // 128
+    cell_z = cell_flat // (rows * lanes)
+    cell_x = (cell_flat // lanes) % rows
+    cell_y = cell_flat % lanes
+    cell_row = (cell_z * tiles + cell_y // 128) * rows + cell_x
     cell_row_onehot = (
-        (cell_flat // 128)[:, None] == lax.broadcasted_iota(jnp.int32, (1, cell_rows), 1)
+        cell_row[None, :] == lax.broadcasted_iota(jnp.int32, (cell_rows, 1), 0)
     ).astype(jnp.bfloat16)
     cell_col_mask = (
-        (cell_flat % 128)[:, None] == lax.broadcasted_iota(jnp.int32, (1, 128), 1)
+        (cell_y % 128)[:, None] == lax.broadcasted_iota(jnp.int32, (1, 128), 1)
     ).astype(jnp.bfloat16)
     segment_flat = arrived_segment.reshape(-1)
     segment_row_onehot = (
-        (segment_flat // segment_width)[:, None] == lax.broadcasted_iota(jnp.int32, (1, blocks), 1)
+        (segment_flat // segment_width)[None, :] == lax.broadcasted_iota(jnp.int32, (blocks, 1), 0)
     ).astype(jnp.bfloat16)
     segment_col_mask = (
         (segment_flat % segment_width)[:, None]
@@ -158,13 +169,14 @@
     backward_plane = [(i + 1, i) for i in range(plane_count - 1)]
     coef_all = jnp.stack([coef_z, upper_z, coef_x, upper_x, coef_y, upper_y])
     rock_now = rock_state
+    rock_table = rock_state.reshape(2, depth, rows, tiles, 128).transpose(0, 1, 3, 2, 4)
+    rock_table = rock_table.reshape(2, cell_rows, 128)
     rock_low, rock_high = rock_now[:, 0], rock_now[:, -1]
     rock_first, rock_last = rock_now[:, :, 0], rock_now[:, :, -1]
     fracture_now = fracture_state
     source_blocks = fracture_source.reshape(2, blocks, segment_width)
     layer_rows = rock_now.shape[2]
     for _ in range(ITERS):
-        rock_table = rock_now.reshape(2, cell_rows, 128)
         rock_picked = pick_values(cell_row_onehot, cell_col_mask, rock_table)
         send_rock = slot_weight_flat[None] * rock_picked
         fracture_table = fracture_now.reshape(2, blocks, segment_width)
@@ -200,12 +212,12 @@
         leak_fracture = place_values(segment_row_onehot, segment_col_mask, got_rock)
         leak_rock = place_values(
             cell_row_onehot, cell_col_mask, slot_weight_flat[None] * got_fracture
-        ).reshape(rock_now.shape)
+        ).reshape(2, depth, tiles, rows, 128)
         fracture_rhs = (fracture_part + leak_fracture).astype(jnp.bfloat16)
         fracture_next = jnp.einsum(
             "bij,fbj->fbi", fracture_inverse, fracture_rhs, preferred_element_type=jnp.float32
         ).reshape(2, -1)
-        rock_now, rock_low, rock_high, rock_first, rock_last = rock_step(
+        rock_now, rock_low, rock_high, rock_first, rock_last, rock_table = rock_step(
             rock_now,
             rock_source,
             leak_rock,
@@ -216,6 +228,7 @@
             coef_all,
             cell_inverse,
         )
+        rock_table = rock_table.reshape(2, cell_rows, 128)
         fracture_now = fracture_next
     return (rock_now, fracture_now)
 

time: 217 us -> 216 us (level)
  local copies, waits for them, and re-layouts: 19.6 us -> 14.5 us
  other arithmetic: 8.76 us -> 13.2 us
    reshape x6 -> x0, local copies, waits for them, and re-layouts: 4.46 us -> none  [the longest x3 2.54 us: shards(): rock_table = rock_now.reshape(2, cell_rows, 128)]
    convert_element_type x9, other arithmetic: 1.65 us -> 4.17 us  [split_bf16(): return (high.astype(jnp.bfloat16), (value - high).astype(jnp.bfloat16))]
where the time goes in v3:
time: 216 us; the launch traced here: 215 us
  starting transfers between devices  144 us (67%)
  matrix products  26.6 us (12%)
  local copies, waits for them, and re-layouts  14.5 us (7%)
  other arithmetic  13.2 us (6%)
  waiting for transfers between devices  9.18 us (4%)
  Pallas kernels  5.51 us (3%)
    all_to_all x3, starting transfers between devices, shards(): lax.all_to_all(send.transpose(1, 0, 2), 'slab', split_axis=0, concat_axis...  35 us
    ppermute x3, starting transfers between devices, shards(): from_right = lax.ppermute(rock_first, 'plane', backward_plane)  29.5 us
    ppermute x3, starting transfers between devices, shards(): lax.ppermute(jnp.concatenate([rock_low, fracture_wide], 1), 'slab', backw...  22 us
    ppermute x2, starting transfers between devices, shifted(): lax.ppermute(value, axis, [(source, source + steps) for source in range(f...  18.2 us
    ppermute x3, starting transfers between devices, shards(): from_left = lax.ppermute(rock_last, 'plane', forward_plane)  17 us
    all_to_all x1, starting transfers between devices, shards(): lax.all_to_all(contact_segment[0], 'slab', split_axis=0, concat_axis=0, t...  16.3 us
    dot_general x6, matrix products, pick_values(): jnp.einsum('kc,grc->grk', col_mask, parts, preferred_element_type=jnp.flo...  14.4 us
    dot_general x6, matrix products, place_values(): jnp.einsum('grk,kc->grc', spread, col_mask, preferred_element_type=jnp.fl...  9.2 us
  transfers between devices with their start and end apart: 18, of which 1 were waited for; matrix products, arithmetic and copies ran while one was open for 20% of the time, Pallas kernels for 0%

profile of v3, /device:TPU:30, one launch (start us, length us, event | category | flops | bytes accessed | tf_op | source)
XLA Modules:
  0.0 214.7 jit_solution(6562651036601751342)
XLA Ops:
  0.7 16.3 %all-to-all-start = ((s32[64,1,128]{2,1,0:T(1,128)}), s32[64,1,128]{2,1,0:T(1,128)S(1)}, u32[]{:S(2)}, u32[]{:S(2)}) async-start(s32[64,1,128]{2,1,0:T(1,128)} %bitcast.260), calls=%async_computation | async-start | bytes 65536 | tf_op jit(solution)/shard_map/all_to_all | solution.py:126
  17.0 1.3 slice_bitcast_fusion.12
  18.3 8.5 %collective-permute-start.5 = (bf16[2,1,512]{2,1,0:T(2,128)(2,1)}, bf16[2,1,512]{2,1,0:T(2,128)(2,1)S(1)}, u32[]{:S(2)}, u32[]{:S(2)}) collective-permute-start(bf16[2,1,512]{2,1,0:T(2,128)(2,1)} %slice_bitcast_fusion.12), channel_id=1, source_target_pairs={{1,0},{2,1},{3,2},{4,3},{5,4},{6,5},{7,6},{9,8},{10,9},{11,10},{12... | collective-permute-start | bytes 6152 | tf_op jit(solution)/shard_map/ppermute | solution.py:17
  27.5 9.7 %collective-permute-start.4 = (bf16[1,8,512]{2,1,0:T(8,128)(2,1)S(1)}, bf16[1,8,512]{2,1,0:T(8,128)(2,1)S(1)}, u32[]{:S(2)}, u32[]{:S(2)}) collective-permute-start(bf16[1,8,512]{2,1,0:T(8,128)(2,1)S(1)} %get-tuple-element.60), channel_id=1, source_target_pairs={{8,0},{16,8},{24,16},{32,24},{40,32},{48,40},{56,48},{64,56},{72,6... | collective-permute-start | bytes 24584 | tf_op jit(solution)/shard_map/ppermute | solution.py:17
  37.2 0.9 fusion.178
  38.7 6.1 %collective-permute-start.2 = (f32[2,2,512]{2,1,0:T(2,128)}, f32[2,2,512]{2,1,0:T(2,128)}, u32[]{:S(2)}, u32[]{:S(2)}) collective-permute-start(f32[2,2,512]{2,1,0:T(2,128)} %bitcast.248), channel_id=1, source_target_pairs={{0,1},{1,2},{2,3},{3,4},{4,5},{5,6},{6,7},{8,9},{9,10},{10,11},{11... | collective-permute-start | bytes 24584 | tf_op jit(solution)/shard_map/ppermute | solution.py:198
  45.4 9.4 %collective-permute-start.3 = (f32[2,2,512]{2,1,0:T(2,128)}, f32[2,2,512]{2,1,0:T(2,128)}, u32[]{:S(2)}, u32[]{:S(2)}) collective-permute-start(f32[2,2,512]{2,1,0:T(2,128)} %bitcast.247), channel_id=1, source_target_pairs={{1,0},{2,1},{3,2},{4,3},{5,4},{6,5},{7,6},{9,8},{10,9},{11,10},{12... | collective-permute-start | bytes 24584 | tf_op jit(solution)/shard_map/ppermute | solution.py:199
  54.7 0.8 slice_bitcast_fusion.6
  56.9 2.0 collective-permute-start.1
  59.6 1.3 reduce-precision_convert_fusion.11
  60.9 0.8 add_select_fusion.6
  61.8 0.9 reduce-precision_convert_fusion.2
  62.6 1.3 fusion.76
  64.1 2.5 %fusion.23 = f32[4,8192]{1,0:T(4,128)S(1)} fusion(f32[64,8192]{1,0:T(8,128)S(1)} %get-tuple-element.65, s32[8192]{0:T(1024)S(1)} %get-tuple-element.63, bf16[2,64,128]{2,1,0:T(8,128)(2,1)S(1)} %get-tuple-element.55, bf16[2,64,128]{2,1,0:T(8,128)(2,1)S(1)} %get-tuple-element.54), kind=kOutput, calls=%fused_computation.19 | convolution fusion | flops 542113792 | bytes 2326528 | tf_op jit(solution)/shard_map/kc,grc->grk/dot_general | solution.py:29
  67.8 2.3 %collective-permute-start = (f32[2,10,512]{2,1,0:T(8,128)S(1)}, f32[2,10,512]{2,1,0:T(8,128)}, u32[]{:S(2)}, u32[]{:S(2)}) collective-permute-start(f32[2,10,512]{2,1,0:T(8,128)S(1)} %get-tuple-element.86), channel_id=1, source_target_pairs={{0,8},{8,16},{16,24},{24,32},{32,40},{40,48},{48,56},{56,64},{64,7... | collective-permute-start | bytes 122888 | tf_op jit(solution)/shard_map/ppermute | solution.py:192
  70.4 2.8 %fusion.51 = f32[4,8192]{1,0:T(4,128)S(1)} fusion(s32[8192]{0:T(1024)S(1)} %get-tuple-element.68, f32[8,8192]{1,0:T(8,128)S(1)} %get-tuple-element.62, bf16[2,8,128]{2,1,0:T(8,128)(2,1)} %get-tuple-element.88, bf16[2,8,128]{2,1,0:T(8,128)(2,1)} %get-tuple-element.87), kind=kOutput, calls=%fused_computation.42 | convolution fusion | flops 68653056 | bytes 434176 | tf_op jit(solution)/shard_map/kc,grc->grk/dot_general | solution.py:29
  74.0 13.6 %all-to-all-start.1 = ((f32[64,4,128]{2,1,0:T(4,128)}), f32[64,4,128]{2,1,0:T(4,128)S(1)}, u32[]{:S(2)}, u32[]{:S(2)}) async-start(f32[64,4,128]{2,1,0:T(4,128)} %maximum_bitcast_fusion), calls=%async_computation.1 | async-start | bytes 262144 | tf_op jit(solution)/shard_map/all_to_all | solution.py:185
  87.6 0.8 slice.352
  89.6 1.4 slice.234.below_ref
  91.0 9.1 %all-to-all-done.1 = f32[64,4,128]{2,1,0:T(4,128)S(1)} async-done(((f32[64,4,128]{2,1,0:T(4,128)}), f32[64,4,128]{2,1,0:T(4,128)S(1)}, u32[]{:S(2)}, u32[]{:S(2)}) %all-to-all-start.1) | async-done | bytes 131104 | tf_op jit(solution)/shard_map/all_to_all | solution.py:185
  100.3 1.3 fusion.20
  101.7 1.5 fusion.4
  104.1 1.8 shard_map.140
  105.9 0.9 reduce-precision_convert_fusion.1
  106.8 2.5 %fusion.26 = f32[4,8192]{1,0:T(4,128)S(1)} fusion(f32[64,8192]{1,0:T(8,128)S(1)} %get-tuple-element.65, s32[8192]{0:T(1024)S(1)} %get-tuple-element.63, bf16[2,64,128]{2,1,0:T(8,128)(2,1)S(1)} %get-tuple-element.49, bf16[2,64,128]{2,1,0:T(8,128)(2,1)S(1)} %get-tuple-element.48), kind=kOutput, calls=%fused_computation.20 | convolution fusion | flops 542113792 | bytes 2326528 | tf_op jit(solution)/shard_map/kc,grc->grk/dot_general | solution.py:29
  109.4 2.1 fusion.54
  112.2 8.1 %all-to-all-start.2 = ((f32[64,4,128]{2,1,0:T(4,128)}), f32[64,4,128]{2,1,0:T(4,128)S(1)}, u32[]{:S(2)}, u32[]{:S(2)}) async-start(f32[64,4,128]{2,1,0:T(4,128)} %maximum_bitcast_fusion.1), calls=%async_computation.2 | async-start | bytes 262144 | tf_op jit(solution)/shard_map/all_to_all | solution.py:185
  120.3 10.0 %collective-permute-start.7 = (f32[2,10,512]{2,1,0:T(8,128)S(1)}, f32[2,10,512]{2,1,0:T(8,128)S(1)}, u32[]{:S(2)}, u32[]{:S(2)}) collective-permute-start(f32[2,10,512]{2,1,0:T(8,128)S(1)} %get-tuple-element.79), channel_id=1, source_target_pairs={{8,0},{16,8},{24,16},{32,24},{40,32},{48,40},{56,48},{64,56},{72,6... | collective-permute-start | bytes 122888 | tf_op jit(solution)/shard_map/ppermute | solution.py:195
  130.3 1.9 collective-permute-start.6
  132.2 5.7 %collective-permute-start.8 = (f32[2,2,512]{2,1,0:T(2,128)}, f32[2,2,512]{2,1,0:T(2,128)S(1)}, u32[]{:S(2)}, u32[]{:S(2)}) collective-permute-start(f32[2,2,512]{2,1,0:T(2,128)} %get-tuple-element.19), channel_id=1, source_target_pairs={{0,1},{1,2},{2,3},{3,4},{4,5},{5,6},{6,7},{8,9},{9,10},{10,11},{11... | collective-permute-start | bytes 24584 | tf_op jit(solution)/shard_map/ppermute | solution.py:198
  138.0 9.9 %collective-permute-start.9 = (f32[2,2,512]{2,1,0:T(2,128)}, f32[2,2,512]{2,1,0:T(2,128)}, u32[]{:S(2)}, u32[]{:S(2)}) collective-permute-start(f32[2,2,512]{2,1,0:T(2,128)} %get-tuple-element.20), channel_id=1, source_target_pairs={{1,0},{2,1},{3,2},{4,3},{5,4},{6,5},{7,6},{9,8},{10,9},{11,10},{12... | collective-permute-start | bytes 24584 | tf_op jit(solution)/shard_map/ppermute | solution.py:199
  147.9 0.8 slice.350
  149.9 1.4 slice.250.below_ref
  151.5 2.3 %fusion.17 = f32[4,8,128]{2,1,0:T(8,128)S(1)} fusion(s32[8192]{0:T(1024)S(1)} %get-tuple-element.68, bf16[4,8192]{1,0:T(4,128)(2,1)S(1)} %pad_maximum_fusion.9, bf16[8,8192]{1,0:T(8,128)(2,1)} %copy-done.10), kind=kOutput, calls=%fused_computation.17 | convolution fusion | flops 68419584 | bytes 245760 | tf_op jit(solution)/shard_map/grk,kc->grc/dot_general | solution.py:39
  153.9 1.5 fusion.2
  155.6 2.1 fusion.57
  159.0 1.8 shard_map.141
  160.8 0.9 reduce-precision_convert_fusion
  161.7 2.5 %fusion.29 = f32[4,8192]{1,0:T(4,128)S(1)} fusion(f32[64,8192]{1,0:T(8,128)S(1)} %get-tuple-element.65, s32[8192]{0:T(1024)S(1)} %get-tuple-element.63, bf16[2,64,128]{2,1,0:T(8,128)(2,1)S(1)} %get-tuple-element.47, bf16[2,64,128]{2,1,0:T(8,128)(2,1)S(1)} %get-tuple-element.46), kind=kOutput, calls=%fused_computation.21 | convolution fusion | flops 542113792 | bytes 2326528 | tf_op jit(solution)/shard_map/kc,grc->grk/dot_general | solution.py:29
  165.0 13.4 %all-to-all-start.3 = ((f32[64,4,128]{2,1,0:T(4,128)}), f32[64,4,128]{2,1,0:T(4,128)S(1)}, u32[]{:S(2)}, u32[]{:S(2)}) async-start(f32[64,4,128]{2,1,0:T(4,128)} %maximum_bitcast_fusion.2), calls=%async_computation.3 | async-start | bytes 262144 | tf_op jit(solution)/shard_map/all_to_all | solution.py:185
  178.4 10.0 %collective-permute-start.11 = (f32[2,10,512]{2,1,0:T(8,128)S(1)}, f32[2,10,512]{2,1,0:T(8,128)S(1)}, u32[]{:S(2)}, u32[]{:S(2)}) collective-permute-start(f32[2,10,512]{2,1,0:T(8,128)S(1)} %get-tuple-element.75), channel_id=1, source_target_pairs={{8,0},{16,8},{24,16},{32,24},{40,32},{48,40},{56,48},{64,56},{72,6... | collective-permute-start | bytes 122888 | tf_op jit(solution)/shard_map/ppermute | solution.py:195
  188.4 1.9 collective-permute-start.10
  190.3 5.2 %collective-permute-start.12 = (f32[2,2,512]{2,1,0:T(2,128)S(1)}, f32[2,2,512]{2,1,0:T(2,128)S(1)}, u32[]{:S(2)}, u32[]{:S(2)}) collective-permute-start(f32[2,2,512]{2,1,0:T(2,128)S(1)} %copy-done.28), channel_id=1, source_target_pairs={{0,1},{1,2},{2,3},{3,4},{4,5},{5,6},{6,7},{8,9},{9,10},{10,11},{11... | collective-permute-start | bytes 24584 | tf_op jit(solution)/shard_map/ppermute | solution.py:198
  195.6 10.2 %collective-permute-start.13 = (f32[2,2,512]{2,1,0:T(2,128)S(1)}, f32[2,2,512]{2,1,0:T(2,128)S(1)}, u32[]{:S(2)}, u32[]{:S(2)}) collective-permute-start(f32[2,2,512]{2,1,0:T(2,128)S(1)} %copy-done.27), channel_id=1, source_target_pairs={{1,0},{2,1},{3,2},{4,3},{5,4},{6,5},{7,6},{9,8},{10,9},{11,10},{12... | collective-permute-start | bytes 24584 | tf_op jit(solution)/shard_map/ppermute | solution.py:199
  207.9 1.3 fusion.14
  209.3 1.5 fusion
  211.4 0.8 convolution_bitcast_fusion
  212.8 1.8 shard_map.142
  (147 shorter events, 16.7 us)
Async XLA Ops:
  0.6 88.0 %copy-start = (bf16[8,3,128,128]{3,2,1,0:T(8,128)(2,1)S(1)}, bf16[8,3,128,128]{3,2,1,0:T(8,128)(2,1)}, u32[]{:S(2)}) copy-start(bf16[8,3,128,128]{3,2,1,0:T(8,128)(2,1)} %param.19) | copy-start | bytes 2359300
  0.6 63.3 %copy-start.26 = (s32[1,64]{1,0:T(1,128)S(1)}, s32[1,64]{1,0:T(1,128)}, u32[]{:S(2)}) copy-start(s32[1,64]{1,0:T(1,128)} %param.25) | copy-start | bytes 772
  0.7 63.3 %copy-start.17 = (f32[1,64,128]{2,1,0:T(8,128)S(1)}, f32[1,64,128]{2,1,0:T(8,128)}, u32[]{:S(2)}) copy-start(f32[1,64,128]{2,1,0:T(8,128)} %param.24) | copy-start | bytes 98308
  0.7 69.6 %all-to-all-start = ((s32[64,1,128]{2,1,0:T(1,128)}), s32[64,1,128]{2,1,0:T(1,128)S(1)}, u32[]{:S(2)}, u32[]{:S(2)}) async-start(s32[64,1,128]{2,1,0:T(1,128)} %bitcast.260), calls=%async_computation | async-start | bytes 65536 | tf_op jit(solution)/shard_map/all_to_all | solution.py:126
  18.3 51.9 %collective-permute-start.5 = (bf16[2,1,512]{2,1,0:T(2,128)(2,1)}, bf16[2,1,512]{2,1,0:T(2,128)(2,1)S(1)}, u32[]{:S(2)}, u32[]{:S(2)}) collective-permute-start(bf16[2,1,512]{2,1,0:T(2,128)(2,1)} %slice_bitcast_fusion.12), channel_id=1, source_target_pairs={{1,0},{2,1},{3,2},{4,3},{5,4},{6,5},{7,6},{9,8},{10,9},{11,10},{12... | collective-permute-start | bytes 6152 | tf_op jit(solution)/shard_map/ppermute | solution.py:17
  27.5 40.3 %collective-permute-start.4 = (bf16[1,8,512]{2,1,0:T(8,128)(2,1)S(1)}, bf16[1,8,512]{2,1,0:T(8,128)(2,1)S(1)}, u32[]{:S(2)}, u32[]{:S(2)}) collective-permute-start(bf16[1,8,512]{2,1,0:T(8,128)(2,1)S(1)} %get-tuple-element.60), channel_id=1, source_target_pairs={{8,0},{16,8},{24,16},{32,24},{40,32},{48,40},{56,48},{64,56},{72,6... | collective-permute-start | bytes 24584 | tf_op jit(solution)/shard_map/ppermute | solution.py:17
  38.7 65.4 %collective-permute-start.2 = (f32[2,2,512]{2,1,0:T(2,128)}, f32[2,2,512]{2,1,0:T(2,128)}, u32[]{:S(2)}, u32[]{:S(2)}) collective-permute-start(f32[2,2,512]{2,1,0:T(2,128)} %bitcast.248), channel_id=1, source_target_pairs={{0,1},{1,2},{2,3},{3,4},{4,5},{5,6},{6,7},{8,9},{9,10},{10,11},{11... | collective-permute-start | bytes 24584 | tf_op jit(solution)/shard_map/ppermute | solution.py:198
  45.4 58.7 %collective-permute-start.3 = (f32[2,2,512]{2,1,0:T(2,128)}, f32[2,2,512]{2,1,0:T(2,128)}, u32[]{:S(2)}, u32[]{:S(2)}) collective-permute-start(f32[2,2,512]{2,1,0:T(2,128)} %bitcast.247), channel_id=1, source_target_pairs={{1,0},{2,1},{3,2},{4,3},{5,4},{6,5},{7,6},{9,8},{10,9},{11,10},{12... | collective-permute-start | bytes 24584 | tf_op jit(solution)/shard_map/ppermute | solution.py:199
  56.9 30.7 %collective-permute-start.1 = (f32[2,10,512]{2,1,0:T(8,128)}, f32[2,10,512]{2,1,0:T(8,128)S(1)}, u32[]{:S(2)}, u32[]{:S(2)}) collective-permute-start(f32[2,10,512]{2,1,0:T(8,128)} %get-tuple-element.85), channel_id=1, source_target_pairs={{8,0},{16,8},{24,16},{32,24},{40,32},{48,40},{56,48},{64,56},{72,6... | collective-permute-start | bytes 122888 | tf_op jit(solution)/shard_map/ppermute | solution.py:195
  64.0 2.5 %copy-start.22 = (s32[8,3]{0,1:T(4,128)S(1)}, s32[8,3]{0,1:T(4,128)}, u32[]{:S(2)}) copy-start(s32[8,3]{0,1:T(4,128)} %param.21) | copy-start | bytes 292
  64.0 6.0 %copy-start.9 = (bf16[3,2,8,512]{3,2,1,0:T(8,128)(2,1)S(1)}, bf16[3,2,8,512]{3,2,1,0:T(8,128)(2,1)}, u32[]{:S(2)}) copy-start(bf16[3,2,8,512]{3,2,1,0:T(8,128)(2,1)} %param.15) | copy-start | bytes 147460
  66.6 22.1 %copy-start.12 = (f32[2,1024]{1,0:T(2,128)S(1)}, f32[2,1024]{1,0:T(2,128)}, u32[]{:S(2)}) copy-start(f32[2,1024]{1,0:T(2,128)} %param.18) | copy-start | bytes 24580
  67.8 19.9 %collective-permute-start = (f32[2,10,512]{2,1,0:T(8,128)S(1)}, f32[2,10,512]{2,1,0:T(8,128)}, u32[]{:S(2)}, u32[]{:S(2)}) collective-permute-start(f32[2,10,512]{2,1,0:T(8,128)S(1)} %get-tuple-element.86), channel_id=1, source_target_pairs={{0,8},{8,16},{16,24},{24,32},{32,40},{40,48},{48,56},{56,64},{64,7... | collective-permute-start | bytes 122888 | tf_op jit(solution)/shard_map/ppermute | solution.py:192
  70.2 18.2 %copy-start.21 = (bf16[1,2,8,128]{3,2,1,0:T(8,128)(2,1)S(1)}, bf16[1,2,8,128]{3,2,1,0:T(8,128)(2,1)}, u32[]{:S(2)}) copy-start(bf16[1,2,8,128]{3,2,1,0:T(8,128)(2,1)} %copy.152) | copy-start | bytes 12292
  70.2 18.2 %copy-start.23 = (s32[8,3]{0,1:T(4,128)S(1)}, s32[8,3]{0,1:T(4,128)}, u32[]{:S(2)}) copy-start(s32[8,3]{0,1:T(4,128)} %fusion.166) | copy-start | bytes 292
  70.3 2.9 %copy-start.6 = (f32[8,8192]{1,0:T(8,128)}, f32[8,8192]{1,0:T(8,128)S(1)}, u32[]{:S(2)}) copy-start(f32[8,8192]{1,0:T(8,128)S(1)} %get-tuple-element.62) | copy-start | bytes 786436
  70.3 31.2 %copy-start.10 = (bf16[8,8192]{1,0:T(8,128)(2,1)}, bf16[8,8192]{1,0:T(8,128)(2,1)S(1)}, u32[]{:S(2)}) copy-start(bf16[8,8192]{1,0:T(8,128)(2,1)S(1)} %get-tuple-element.61) | copy-start | bytes 393220
  74.0 26.1 %all-to-all-start.1 = ((f32[64,4,128]{2,1,0:T(4,128)}), f32[64,4,128]{2,1,0:T(4,128)S(1)}, u32[]{:S(2)}, u32[]{:S(2)}) async-start(f32[64,4,128]{2,1,0:T(4,128)} %maximum_bitcast_fusion), calls=%async_computation.1 | async-start | bytes 262144 | tf_op jit(solution)/shard_map/all_to_all | solution.py:185
  87.6 15.6 %copy-start.5 = (bf16[6,2,8,512]{3,2,1,0:T(8,128)(2,1)}, bf16[6,2,8,512]{3,2,1,0:T(8,128)(2,1)S(1)}, u32[]{:S(2)}) copy-start(bf16[6,2,8,512]{3,2,1,0:T(8,128)(2,1)S(1)} %bitcast_dynamic-update-slice_fusion.coef_ref) | copy-start | bytes 294916
  100.1 1.6 copy-start.2
  101.7 2.1 copy-start.1
  106.8 2.6 %copy-start.7 = (f32[8,8192]{1,0:T(8,128)S(1)}, f32[8,8192]{1,0:T(8,128)}, u32[]{:S(2)}) copy-start(f32[8,8192]{1,0:T(8,128)} %copy-done.6) | copy-start | bytes 786436
  109.3 11.0 %copy-start.13 = (f32[2,8,512]{2,1,0:T(8,128)S(1)}, f32[2,8,512]{2,1,0:T(8,128)}, u32[]{:S(2)}) copy-start(f32[2,8,512]{2,1,0:T(8,128)} %get-tuple-element.18) | copy-start | bytes 98308
  109.3 11.0 %copy-start.14 = (f32[2,8,512]{2,1,0:T(8,128)S(1)}, f32[2,8,512]{2,1,0:T(8,128)}, u32[]{:S(2)}) copy-start(f32[2,8,512]{2,1,0:T(8,128)} %get-tuple-element.17) | copy-start | bytes 98308
  109.3 39.4 %copy-start.24 = (s32[8,3]{0,1:T(4,128)S(1)}, s32[8,3]{0,1:T(4,128)}, u32[]{:S(2)}) copy-start(s32[8,3]{0,1:T(4,128)} %fusion.166) | copy-start | bytes 292
  112.2 39.1 %all-to-all-start.2 = ((f32[64,4,128]{2,1,0:T(4,128)}), f32[64,4,128]{2,1,0:T(4,128)S(1)}, u32[]{:S(2)}, u32[]{:S(2)}) async-start(f32[64,4,128]{2,1,0:T(4,128)} %maximum_bitcast_fusion.1), calls=%async_computation.2 | async-start | bytes 262144 | tf_op jit(solution)/shard_map/all_to_all | solution.py:185
  120.3 27.6 %collective-permute-start.7 = (f32[2,10,512]{2,1,0:T(8,128)S(1)}, f32[2,10,512]{2,1,0:T(8,128)S(1)}, u32[]{:S(2)}, u32[]{:S(2)}) collective-permute-start(f32[2,10,512]{2,1,0:T(8,128)S(1)} %get-tuple-element.79), channel_id=1, source_target_pairs={{8,0},{16,8},{24,16},{32,24},{40,32},{48,40},{56,48},{64,56},{72,6... | collective-permute-start | bytes 122888 | tf_op jit(solution)/shard_map/ppermute | solution.py:195
  130.3 17.6 %collective-permute-start.6 = (f32[2,10,512]{2,1,0:T(8,128)S(1)}, f32[2,10,512]{2,1,0:T(8,128)}, u32[]{:S(2)}, u32[]{:S(2)}) collective-permute-start(f32[2,10,512]{2,1,0:T(8,128)S(1)} %get-tuple-element.80), channel_id=1, source_target_pairs={{0,8},{8,16},{16,24},{24,32},{32,40},{40,48},{48,56},{56,64},{64,7... | collective-permute-start | bytes 122888 | tf_op jit(solution)/shard_map/ppermute | solution.py:192
  132.2 26.1 %collective-permute-start.8 = (f32[2,2,512]{2,1,0:T(2,128)}, f32[2,2,512]{2,1,0:T(2,128)S(1)}, u32[]{:S(2)}, u32[]{:S(2)}) collective-permute-start(f32[2,2,512]{2,1,0:T(2,128)} %get-tuple-element.19), channel_id=1, source_target_pairs={{0,1},{1,2},{2,3},{3,4},{4,5},{5,6},{6,7},{8,9},{9,10},{10,11},{11... | collective-permute-start | bytes 24584 | tf_op jit(solution)/shard_map/ppermute | solution.py:198
  138.0 20.4 %collective-permute-start.9 = (f32[2,2,512]{2,1,0:T(2,128)}, f32[2,2,512]{2,1,0:T(2,128)}, u32[]{:S(2)}, u32[]{:S(2)}) collective-permute-start(f32[2,2,512]{2,1,0:T(2,128)} %get-tuple-element.20), channel_id=1, source_target_pairs={{1,0},{2,1},{3,2},{4,3},{5,4},{6,5},{7,6},{9,8},{10,9},{11,10},{12... | collective-permute-start | bytes 24584 | tf_op jit(solution)/shard_map/ppermute | solution.py:199
  151.3 2.6 %copy-start.3 = (bf16[64,8192]{1,0:T(8,128)(2,1)S(1)}, bf16[64,8192]{1,0:T(8,128)(2,1)}, u32[]{:S(2)}) copy-start(bf16[64,8192]{1,0:T(8,128)(2,1)} %get-tuple-element.66) | copy-start | bytes 3145732
  153.8 1.7 copy-start.8
  158.4 0.6 copy-start.18
  161.7 16.7 %copy-start.15 = (f32[2,8,512]{2,1,0:T(8,128)S(1)}, f32[2,8,512]{2,1,0:T(8,128)}, u32[]{:S(2)}) copy-start(f32[2,8,512]{2,1,0:T(8,128)} %get-tuple-element.24) | copy-start | bytes 98308
  161.7 16.7 %copy-start.16 = (f32[2,8,512]{2,1,0:T(8,128)S(1)}, f32[2,8,512]{2,1,0:T(8,128)}, u32[]{:S(2)}) copy-start(f32[2,8,512]{2,1,0:T(8,128)} %get-tuple-element.23) | copy-start | bytes 98308
  161.7 28.7 %copy-start.28 = (f32[2,2,512]{2,1,0:T(2,128)S(1)}, f32[2,2,512]{2,1,0:T(2,128)}, u32[]{:S(2)}) copy-start(f32[2,2,512]{2,1,0:T(2,128)} %get-tuple-element.25) | copy-start | bytes 24580
  161.7 33.9 %copy-start.27 = (f32[2,2,512]{2,1,0:T(2,128)S(1)}, f32[2,2,512]{2,1,0:T(2,128)}, u32[]{:S(2)}) copy-start(f32[2,2,512]{2,1,0:T(2,128)} %get-tuple-element.26) | copy-start | bytes 24580
  161.7 44.2 %copy-start.25 = (s32[8,3]{0,1:T(4,128)S(1)}, s32[8,3]{0,1:T(4,128)}, u32[]{:S(2)}) copy-start(s32[8,3]{0,1:T(4,128)} %fusion.166) | copy-start | bytes 292
  164.2 43.7 %copy-start.11 = (bf16[8,8192]{1,0:T(8,128)(2,1)S(1)}, bf16[8,8192]{1,0:T(8,128)(2,1)}, u32[]{:S(2)}) copy-start(bf16[8,8192]{1,0:T(8,128)(2,1)} %copy-done.10) | copy-start | bytes 393220
  164.3 45.0 %copy-start.4 = (bf16[64,8192]{1,0:T(8,128)(2,1)S(1)}, bf16[64,8192]{1,0:T(8,128)(2,1)}, u32[]{:S(2)}) copy-start(bf16[64,8192]{1,0:T(8,128)(2,1)} %get-tuple-element.66) | copy-start | bytes 3145732
  165.0 42.7 %all-to-all-start.3 = ((f32[64,4,128]{2,1,0:T(4,128)}), f32[64,4,128]{2,1,0:T(4,128)S(1)}, u32[]{:S(2)}, u32[]{:S(2)}) async-start(f32[64,4,128]{2,1,0:T(4,128)} %maximum_bitcast_fusion.2), calls=%async_computation.3 | async-start | bytes 262144 | tf_op jit(solution)/shard_map/all_to_all | solution.py:185
  178.4 27.4 %collective-permute-start.11 = (f32[2,10,512]{2,1,0:T(8,128)S(1)}, f32[2,10,512]{2,1,0:T(8,128)S(1)}, u32[]{:S(2)}, u32[]{:S(2)}) collective-permute-start(f32[2,10,512]{2,1,0:T(8,128)S(1)} %get-tuple-element.75), channel_id=1, source_target_pairs={{8,0},{16,8},{24,16},{32,24},{40,32},{48,40},{56,48},{64,56},{72,6... | collective-permute-start | bytes 122888 | tf_op jit(solution)/shard_map/ppermute | solution.py:195
  188.4 17.5 %collective-permute-start.10 = (f32[2,10,512]{2,1,0:T(8,128)S(1)}, f32[2,10,512]{2,1,0:T(8,128)S(1)}, u32[]{:S(2)}, u32[]{:S(2)}) collective-permute-start(f32[2,10,512]{2,1,0:T(8,128)S(1)} %get-tuple-element.76), channel_id=1, source_target_pairs={{0,8},{8,16},{16,24},{24,32},{32,40},{40,48},{48,56},{56,64},{64,7... | collective-permute-start | bytes 122888 | tf_op jit(solution)/shard_map/ppermute | solution.py:192
  190.3 21.9 %collective-permute-start.12 = (f32[2,2,512]{2,1,0:T(2,128)S(1)}, f32[2,2,512]{2,1,0:T(2,128)S(1)}, u32[]{:S(2)}, u32[]{:S(2)}) collective-permute-start(f32[2,2,512]{2,1,0:T(2,128)S(1)} %copy-done.28), channel_id=1, source_target_pairs={{0,1},{1,2},{2,3},{3,4},{4,5},{5,6},{6,7},{8,9},{9,10},{10,11},{11... | collective-permute-start | bytes 24584 | tf_op jit(solution)/shard_map/ppermute | solution.py:198
  195.6 16.6 %collective-permute-start.13 = (f32[2,2,512]{2,1,0:T(2,128)S(1)}, f32[2,2,512]{2,1,0:T(2,128)S(1)}, u32[]{:S(2)}, u32[]{:S(2)}) collective-permute-start(f32[2,2,512]{2,1,0:T(2,128)S(1)} %copy-done.27), channel_id=1, source_target_pairs={{1,0},{2,1},{3,2},{4,3},{5,4},{6,5},{7,6},{9,8},{10,9},{11,10},{12... | collective-permute-start | bytes 24584 | tf_op jit(solution)/shard_map/ppermute | solution.py:199
  212.2 0.6 copy-start.19
  212.2 0.6 copy-start.20

commit v4 on v3

--- a/solution.py
+++ b/solution.py
@@ -158,16 +158,10 @@
     coef_z = transmissibility[0]
     coef_x = transmissibility[1]
     coef_y = transmissibility[2]
-    layer_above = shifted(transmissibility[0, :1], "slab", -1)
-    layer_beside = shifted(transmissibility[1, :, :1], "plane", -1)
-    upper_z = jnp.concatenate([coef_z[1:], layer_above], 0)
-    upper_x = jnp.concatenate([coef_x[:, 1:], layer_beside], 1)
-    upper_y = jnp.pad(coef_y[..., 1:], ((0, 0), (0, 0), (0, 1)))
     forward_slab = [(i, i + 1) for i in range(slab_count - 1)]
     backward_slab = [(i + 1, i) for i in range(slab_count - 1)]
     forward_plane = [(i, i + 1) for i in range(plane_count - 1)]
     backward_plane = [(i + 1, i) for i in range(plane_count - 1)]
-    coef_all = jnp.stack([coef_z, upper_z, coef_x, upper_x, coef_y, upper_y])
     rock_now = rock_state
     rock_table = rock_state.reshape(2, depth, rows, tiles, 128).transpose(0, 1, 3, 2, 4)
     rock_table = rock_table.reshape(2, cell_rows, 128)
@@ -176,7 +170,7 @@
     fracture_now = fracture_state
     source_blocks = fracture_source.reshape(2, blocks, segment_width)
     layer_rows = rock_now.shape[2]
-    for _ in range(ITERS):
+    for sweep_index in range(ITERS):
         rock_picked = pick_values(cell_row_onehot, cell_col_mask, rock_table)
         send_rock = slot_weight_flat[None] * rock_picked
         fracture_table = fracture_now.reshape(2, blocks, segment_width)
@@ -189,14 +183,23 @@
         got_fracture = got[2:].reshape(2, -1)
         fracture_low = fracture_now.astype(jnp.bfloat16).reshape(2, blocks, segment_width)
         fracture_wide = fracture_low.astype(jnp.float32).reshape(2, -1, rock_now.shape[-1])
+        from_left = lax.ppermute(rock_last, "plane", forward_plane)
+        from_right = lax.ppermute(rock_first, "plane", backward_plane)
+        if sweep_index == 0:
+            layer_beside = shifted(transmissibility[1, :, :1], "plane", -1)
         from_below = lax.ppermute(
             jnp.concatenate([rock_high, fracture_wide], 1), "slab", forward_slab
         )
         from_above = lax.ppermute(
             jnp.concatenate([rock_low, fracture_wide], 1), "slab", backward_slab
         )
-        from_left = lax.ppermute(rock_last, "plane", forward_plane)
-        from_right = lax.ppermute(rock_first, "plane", backward_plane)
+        if sweep_index == 0:
+            layer_above = shifted(transmissibility[0, :1], "slab", -1)
+        if sweep_index == 0:
+            upper_z = jnp.concatenate([coef_z[1:], layer_above], 0)
+            upper_x = jnp.concatenate([coef_x[:, 1:], layer_beside], 1)
+            upper_y = jnp.pad(coef_y[..., 1:], ((0, 0), (0, 0), (0, 1)))
+            coef_all = jnp.stack([coef_z, upper_z, coef_x, upper_x, coef_y, upper_y])
         fracture_prev = from_below[:, layer_rows:].reshape(fracture_low.shape).astype(jnp.bfloat16)
         fracture_next_part = from_above[:, layer_rows:].reshape(
             fracture_low.shape

time: 216 us -> 216 us (level)
  no operation moved by 1% of the time
where the time goes in v4:
time: 216 us; the launch traced here: 215 us
  starting transfers between devices  144 us (67%)
  matrix products  26.6 us (12%)
  local copies, waits for them, and re-layouts  14.5 us (7%)
  other arithmetic  13.2 us (6%)
  waiting for transfers between devices  9.18 us (4%)
  Pallas kernels  5.51 us (3%)
    all_to_all x3, starting transfers between devices, shards(): lax.all_to_all(send.transpose(1, 0, 2), 'slab', split_axis=0, concat_axis...  35 us
    ppermute x3, starting transfers between devices, shards(): from_right = lax.ppermute(rock_first, 'plane', backward_plane)  29.5 us
    ppermute x3, starting transfers between devices, shards(): lax.ppermute(jnp.concatenate([rock_low, fracture_wide], 1), 'slab', backw...  22 us
    ppermute x2, starting transfers between devices, shifted(): lax.ppermute(value, axis, [(source, source + steps) for source in range(f...  18.2 us
    ppermute x3, starting transfers between devices, shards(): from_left = lax.ppermute(rock_last, 'plane', forward_plane)  17 us
    all_to_all x1, starting transfers between devices, shards(): lax.all_to_all(contact_segment[0], 'slab', split_axis=0, concat_axis=0, t...  16.3 us
    dot_general x6, matrix products, pick_values(): jnp.einsum('kc,grc->grk', col_mask, parts, preferred_element_type=jnp.flo...  14.4 us
    dot_general x6, matrix products, place_values(): jnp.einsum('grk,kc->grc', spread, col_mask, preferred_element_type=jnp.fl...  9.2 us
  transfers between devices with their start and end apart: 18, of which 1 were waited for; matrix products, arithmetic and copies ran while one was open for 20% of the time, Pallas kernels for 0%

profile of v4, /device:TPU:30, one launch (start us, length us, event | category | flops | bytes accessed | tf_op | source)
XLA Modules:
  0.0 214.7 jit_solution(6562651036601751342)
XLA Ops:
  0.7 16.3 %all-to-all-start = ((s32[64,1,128]{2,1,0:T(1,128)}), s32[64,1,128]{2,1,0:T(1,128)S(1)}, u32[]{:S(2)}, u32[]{:S(2)}) async-start(s32[64,1,128]{2,1,0:T(1,128)} %bitcast.260), calls=%async_computation | async-start | bytes 65536 | tf_op jit(solution)/shard_map/all_to_all | solution.py:126
  17.0 1.3 slice_bitcast_fusion.12
  18.3 8.5 %collective-permute-start.5 = (bf16[2,1,512]{2,1,0:T(2,128)(2,1)}, bf16[2,1,512]{2,1,0:T(2,128)(2,1)S(1)}, u32[]{:S(2)}, u32[]{:S(2)}) collective-permute-start(bf16[2,1,512]{2,1,0:T(2,128)(2,1)} %slice_bitcast_fusion.12), channel_id=1, source_target_pairs={{1,0},{2,1},{3,2},{4,3},{5,4},{6,5},{7,6},{9,8},{10,9},{11,10},{12... | collective-permute-start | bytes 6152 | tf_op jit(solution)/shard_map/ppermute | solution.py:17
  27.5 9.7 %collective-permute-start.4 = (bf16[1,8,512]{2,1,0:T(8,128)(2,1)S(1)}, bf16[1,8,512]{2,1,0:T(8,128)(2,1)S(1)}, u32[]{:S(2)}, u32[]{:S(2)}) collective-permute-start(bf16[1,8,512]{2,1,0:T(8,128)(2,1)S(1)} %get-tuple-element.60), channel_id=1, source_target_pairs={{8,0},{16,8},{24,16},{32,24},{40,32},{48,40},{56,48},{64,56},{72,6... | collective-permute-start | bytes 24584 | tf_op jit(solution)/shard_map/ppermute | solution.py:17
  37.2 0.9 fusion.178
  38.7 6.1 %collective-permute-start.2 = (f32[2,2,512]{2,1,0:T(2,128)}, f32[2,2,512]{2,1,0:T(2,128)}, u32[]{:S(2)}, u32[]{:S(2)}) collective-permute-start(f32[2,2,512]{2,1,0:T(2,128)} %bitcast.248), channel_id=1, source_target_pairs={{0,1},{1,2},{2,3},{3,4},{4,5},{5,6},{6,7},{8,9},{9,10},{10,11},{11... | collective-permute-start | bytes 24584 | tf_op jit(solution)/shard_map/ppermute | solution.py:186
  45.4 9.4 %collective-permute-start.3 = (f32[2,2,512]{2,1,0:T(2,128)}, f32[2,2,512]{2,1,0:T(2,128)}, u32[]{:S(2)}, u32[]{:S(2)}) collective-permute-start(f32[2,2,512]{2,1,0:T(2,128)} %bitcast.247), channel_id=1, source_target_pairs={{1,0},{2,1},{3,2},{4,3},{5,4},{6,5},{7,6},{9,8},{10,9},{11,10},{12... | collective-permute-start | bytes 24584 | tf_op jit(solution)/shard_map/ppermute | solution.py:187
  54.7 0.8 slice_bitcast_fusion.6
  56.9 2.0 collective-permute-start.1
  59.6 1.3 reduce-precision_convert_fusion.11
  60.9 0.8 add_select_fusion.6
  61.8 0.9 reduce-precision_convert_fusion.2
  62.6 1.3 fusion.76
  64.1 2.5 %fusion.23 = f32[4,8192]{1,0:T(4,128)S(1)} fusion(f32[64,8192]{1,0:T(8,128)S(1)} %get-tuple-element.65, s32[8192]{0:T(1024)S(1)} %get-tuple-element.63, bf16[2,64,128]{2,1,0:T(8,128)(2,1)S(1)} %get-tuple-element.55, bf16[2,64,128]{2,1,0:T(8,128)(2,1)S(1)} %get-tuple-element.54), kind=kOutput, calls=%fused_computation.19 | convolution fusion | flops 542113792 | bytes 2326528 | tf_op jit(solution)/shard_map/kc,grc->grk/dot_general | solution.py:29
  67.8 2.3 %collective-permute-start = (f32[2,10,512]{2,1,0:T(8,128)S(1)}, f32[2,10,512]{2,1,0:T(8,128)}, u32[]{:S(2)}, u32[]{:S(2)}) collective-permute-start(f32[2,10,512]{2,1,0:T(8,128)S(1)} %get-tuple-element.86), channel_id=1, source_target_pairs={{0,8},{8,16},{16,24},{24,32},{32,40},{40,48},{48,56},{56,64},{64,7... | collective-permute-start | bytes 122888 | tf_op jit(solution)/shard_map/ppermute | solution.py:190
  70.4 2.8 %fusion.51 = f32[4,8192]{1,0:T(4,128)S(1)} fusion(s32[8192]{0:T(1024)S(1)} %get-tuple-element.68, f32[8,8192]{1,0:T(8,128)S(1)} %get-tuple-element.62, bf16[2,8,128]{2,1,0:T(8,128)(2,1)} %get-tuple-element.88, bf16[2,8,128]{2,1,0:T(8,128)(2,1)} %get-tuple-element.87), kind=kOutput, calls=%fused_computation.42 | convolution fusion | flops 68653056 | bytes 434176 | tf_op jit(solution)/shard_map/kc,grc->grk/dot_general | solution.py:29
  74.0 13.6 %all-to-all-start.1 = ((f32[64,4,128]{2,1,0:T(4,128)}), f32[64,4,128]{2,1,0:T(4,128)S(1)}, u32[]{:S(2)}, u32[]{:S(2)}) async-start(f32[64,4,128]{2,1,0:T(4,128)} %maximum_bitcast_fusion), calls=%async_computation.1 | async-start | bytes 262144 | tf_op jit(solution)/shard_map/all_to_all | solution.py:179
  87.6 0.8 slice.352
  89.6 1.4 slice.234.below_ref
  91.0 9.1 %all-to-all-done.1 = f32[64,4,128]{2,1,0:T(4,128)S(1)} async-done(((f32[64,4,128]{2,1,0:T(4,128)}), f32[64,4,128]{2,1,0:T(4,128)S(1)}, u32[]{:S(2)}, u32[]{:S(2)}) %all-to-all-start.1) | async-done | bytes 131104 | tf_op jit(solution)/shard_map/all_to_all | solution.py:179
  100.3 1.3 fusion.20
  101.7 1.5 fusion.4
  104.1 1.8 shard_map.140
  105.9 0.9 reduce-precision_convert_fusion.1
  106.8 2.5 %fusion.26 = f32[4,8192]{1,0:T(4,128)S(1)} fusion(f32[64,8192]{1,0:T(8,128)S(1)} %get-tuple-element.65, s32[8192]{0:T(1024)S(1)} %get-tuple-element.63, bf16[2,64,128]{2,1,0:T(8,128)(2,1)S(1)} %get-tuple-element.49, bf16[2,64,128]{2,1,0:T(8,128)(2,1)S(1)} %get-tuple-element.48), kind=kOutput, calls=%fused_computation.20 | convolution fusion | flops 542113792 | bytes 2326528 | tf_op jit(solution)/shard_map/kc,grc->grk/dot_general | solution.py:29
  109.4 2.1 fusion.54
  112.2 8.1 %all-to-all-start.2 = ((f32[64,4,128]{2,1,0:T(4,128)}), f32[64,4,128]{2,1,0:T(4,128)S(1)}, u32[]{:S(2)}, u32[]{:S(2)}) async-start(f32[64,4,128]{2,1,0:T(4,128)} %maximum_bitcast_fusion.1), calls=%async_computation.2 | async-start | bytes 262144 | tf_op jit(solution)/shard_map/all_to_all | solution.py:179
  120.3 10.0 %collective-permute-start.7 = (f32[2,10,512]{2,1,0:T(8,128)S(1)}, f32[2,10,512]{2,1,0:T(8,128)S(1)}, u32[]{:S(2)}, u32[]{:S(2)}) collective-permute-start(f32[2,10,512]{2,1,0:T(8,128)S(1)} %get-tuple-element.79), channel_id=1, source_target_pairs={{8,0},{16,8},{24,16},{32,24},{40,32},{48,40},{56,48},{64,56},{72,6... | collective-permute-start | bytes 122888 | tf_op jit(solution)/shard_map/ppermute | solution.py:193
  130.3 1.9 collective-permute-start.6
  132.2 5.7 %collective-permute-start.8 = (f32[2,2,512]{2,1,0:T(2,128)}, f32[2,2,512]{2,1,0:T(2,128)S(1)}, u32[]{:S(2)}, u32[]{:S(2)}) collective-permute-start(f32[2,2,512]{2,1,0:T(2,128)} %get-tuple-element.19), channel_id=1, source_target_pairs={{0,1},{1,2},{2,3},{3,4},{4,5},{5,6},{6,7},{8,9},{9,10},{10,11},{11... | collective-permute-start | bytes 24584 | tf_op jit(solution)/shard_map/ppermute | solution.py:186
  138.0 9.9 %collective-permute-start.9 = (f32[2,2,512]{2,1,0:T(2,128)}, f32[2,2,512]{2,1,0:T(2,128)}, u32[]{:S(2)}, u32[]{:S(2)}) collective-permute-start(f32[2,2,512]{2,1,0:T(2,128)} %get-tuple-element.20), channel_id=1, source_target_pairs={{1,0},{2,1},{3,2},{4,3},{5,4},{6,5},{7,6},{9,8},{10,9},{11,10},{12... | collective-permute-start | bytes 24584 | tf_op jit(solution)/shard_map/ppermute | solution.py:187
  147.9 0.8 slice.350
  149.9 1.4 slice.250.below_ref
  151.5 2.3 %fusion.17 = f32[4,8,128]{2,1,0:T(8,128)S(1)} fusion(s32[8192]{0:T(1024)S(1)} %get-tuple-element.68, bf16[4,8192]{1,0:T(4,128)(2,1)S(1)} %pad_maximum_fusion.9, bf16[8,8192]{1,0:T(8,128)(2,1)} %copy-done.10), kind=kOutput, calls=%fused_computation.17 | convolution fusion | flops 68419584 | bytes 245760 | tf_op jit(solution)/shard_map/grk,kc->grc/dot_general | solution.py:39
  153.9 1.5 fusion.2
  155.6 2.1 fusion.57
  159.0 1.8 shard_map.141
  160.8 0.9 reduce-precision_convert_fusion
  161.7 2.5 %fusion.29 = f32[4,8192]{1,0:T(4,128)S(1)} fusion(f32[64,8192]{1,0:T(8,128)S(1)} %get-tuple-element.65, s32[8192]{0:T(1024)S(1)} %get-tuple-element.63, bf16[2,64,128]{2,1,0:T(8,128)(2,1)S(1)} %get-tuple-element.47, bf16[2,64,128]{2,1,0:T(8,128)(2,1)S(1)} %get-tuple-element.46), kind=kOutput, calls=%fused_computation.21 | convolution fusion | flops 542113792 | bytes 2326528 | tf_op jit(solution)/shard_map/kc,grc->grk/dot_general | solution.py:29
  165.0 13.4 %all-to-all-start.3 = ((f32[64,4,128]{2,1,0:T(4,128)}), f32[64,4,128]{2,1,0:T(4,128)S(1)}, u32[]{:S(2)}, u32[]{:S(2)}) async-start(f32[64,4,128]{2,1,0:T(4,128)} %maximum_bitcast_fusion.2), calls=%async_computation.3 | async-start | bytes 262144 | tf_op jit(solution)/shard_map/all_to_all | solution.py:179
  178.4 10.0 %collective-permute-start.11 = (f32[2,10,512]{2,1,0:T(8,128)S(1)}, f32[2,10,512]{2,1,0:T(8,128)S(1)}, u32[]{:S(2)}, u32[]{:S(2)}) collective-permute-start(f32[2,10,512]{2,1,0:T(8,128)S(1)} %get-tuple-element.75), channel_id=1, source_target_pairs={{8,0},{16,8},{24,16},{32,24},{40,32},{48,40},{56,48},{64,56},{72,6... | collective-permute-start | bytes 122888 | tf_op jit(solution)/shard_map/ppermute | solution.py:193
  188.4 1.9 collective-permute-start.10
  190.3 5.2 %collective-permute-start.12 = (f32[2,2,512]{2,1,0:T(2,128)S(1)}, f32[2,2,512]{2,1,0:T(2,128)S(1)}, u32[]{:S(2)}, u32[]{:S(2)}) collective-permute-start(f32[2,2,512]{2,1,0:T(2,128)S(1)} %copy-done.28), channel_id=1, source_target_pairs={{0,1},{1,2},{2,3},{3,4},{4,5},{5,6},{6,7},{8,9},{9,10},{10,11},{11... | collective-permute-start | bytes 24584 | tf_op jit(solution)/shard_map/ppermute | solution.py:186
  195.6 10.2 %collective-permute-start.13 = (f32[2,2,512]{2,1,0:T(2,128)S(1)}, f32[2,2,512]{2,1,0:T(2,128)S(1)}, u32[]{:S(2)}, u32[]{:S(2)}) collective-permute-start(f32[2,2,512]{2,1,0:T(2,128)S(1)} %copy-done.27), channel_id=1, source_target_pairs={{1,0},{2,1},{3,2},{4,3},{5,4},{6,5},{7,6},{9,8},{10,9},{11,10},{12... | collective-permute-start | bytes 24584 | tf_op jit(solution)/shard_map/ppermute | solution.py:187
  207.9 1.3 fusion.14
  209.3 1.5 fusion
  211.4 0.8 convolution_bitcast_fusion
  212.8 1.8 shard_map.142
  (147 shorter events, 16.7 us)
Async XLA Ops:
  0.6 88.0 %copy-start = (bf16[8,3,128,128]{3,2,1,0:T(8,128)(2,1)S(1)}, bf16[8,3,128,128]{3,2,1,0:T(8,128)(2,1)}, u32[]{:S(2)}) copy-start(bf16[8,3,128,128]{3,2,1,0:T(8,128)(2,1)} %param.19) | copy-start | bytes 2359300
  0.6 63.3 %copy-start.26 = (s32[1,64]{1,0:T(1,128)S(1)}, s32[1,64]{1,0:T(1,128)}, u32[]{:S(2)}) copy-start(s32[1,64]{1,0:T(1,128)} %param.25) | copy-start | bytes 772
  0.7 63.3 %copy-start.17 = (f32[1,64,128]{2,1,0:T(8,128)S(1)}, f32[1,64,128]{2,1,0:T(8,128)}, u32[]{:S(2)}) copy-start(f32[1,64,128]{2,1,0:T(8,128)} %param.24) | copy-start | bytes 98308
  0.7 69.6 %all-to-all-start = ((s32[64,1,128]{2,1,0:T(1,128)}), s32[64,1,128]{2,1,0:T(1,128)S(1)}, u32[]{:S(2)}, u32[]{:S(2)}) async-start(s32[64,1,128]{2,1,0:T(1,128)} %bitcast.260), calls=%async_computation | async-start | bytes 65536 | tf_op jit(solution)/shard_map/all_to_all | solution.py:126
  18.3 51.9 %collective-permute-start.5 = (bf16[2,1,512]{2,1,0:T(2,128)(2,1)}, bf16[2,1,512]{2,1,0:T(2,128)(2,1)S(1)}, u32[]{:S(2)}, u32[]{:S(2)}) collective-permute-start(bf16[2,1,512]{2,1,0:T(2,128)(2,1)} %slice_bitcast_fusion.12), channel_id=1, source_target_pairs={{1,0},{2,1},{3,2},{4,3},{5,4},{6,5},{7,6},{9,8},{10,9},{11,10},{12... | collective-permute-start | bytes 6152 | tf_op jit(solution)/shard_map/ppermute | solution.py:17
  27.5 40.3 %collective-permute-start.4 = (bf16[1,8,512]{2,1,0:T(8,128)(2,1)S(1)}, bf16[1,8,512]{2,1,0:T(8,128)(2,1)S(1)}, u32[]{:S(2)}, u32[]{:S(2)}) collective-permute-start(bf16[1,8,512]{2,1,0:T(8,128)(2,1)S(1)} %get-tuple-element.60), channel_id=1, source_target_pairs={{8,0},{16,8},{24,16},{32,24},{40,32},{48,40},{56,48},{64,56},{72,6... | collective-permute-start | bytes 24584 | tf_op jit(solution)/shard_map/ppermute | solution.py:17
  38.7 65.4 %collective-permute-start.2 = (f32[2,2,512]{2,1,0:T(2,128)}, f32[2,2,512]{2,1,0:T(2,128)}, u32[]{:S(2)}, u32[]{:S(2)}) collective-permute-start(f32[2,2,512]{2,1,0:T(2,128)} %bitcast.248), channel_id=1, source_target_pairs={{0,1},{1,2},{2,3},{3,4},{4,5},{5,6},{6,7},{8,9},{9,10},{10,11},{11... | collective-permute-start | bytes 24584 | tf_op jit(solution)/shard_map/ppermute | solution.py:186
  45.4 58.7 %collective-permute-start.3 = (f32[2,2,512]{2,1,0:T(2,128)}, f32[2,2,512]{2,1,0:T(2,128)}, u32[]{:S(2)}, u32[]{:S(2)}) collective-permute-start(f32[2,2,512]{2,1,0:T(2,128)} %bitcast.247), channel_id=1, source_target_pairs={{1,0},{2,1},{3,2},{4,3},{5,4},{6,5},{7,6},{9,8},{10,9},{11,10},{12... | collective-permute-start | bytes 24584 | tf_op jit(solution)/shard_map/ppermute | solution.py:187
  56.9 30.7 %collective-permute-start.1 = (f32[2,10,512]{2,1,0:T(8,128)}, f32[2,10,512]{2,1,0:T(8,128)S(1)}, u32[]{:S(2)}, u32[]{:S(2)}) collective-permute-start(f32[2,10,512]{2,1,0:T(8,128)} %get-tuple-element.85), channel_id=1, source_target_pairs={{8,0},{16,8},{24,16},{32,24},{40,32},{48,40},{56,48},{64,56},{72,6... | collective-permute-start | bytes 122888 | tf_op jit(solution)/shard_map/ppermute | solution.py:193
  64.0 2.5 %copy-start.22 = (s32[8,3]{0,1:T(4,128)S(1)}, s32[8,3]{0,1:T(4,128)}, u32[]{:S(2)}) copy-start(s32[8,3]{0,1:T(4,128)} %param.21) | copy-start | bytes 292
  64.0 6.0 %copy-start.9 = (bf16[3,2,8,512]{3,2,1,0:T(8,128)(2,1)S(1)}, bf16[3,2,8,512]{3,2,1,0:T(8,128)(2,1)}, u32[]{:S(2)}) copy-start(bf16[3,2,8,512]{3,2,1,0:T(8,128)(2,1)} %param.15) | copy-start | bytes 147460
  66.6 22.1 %copy-start.12 = (f32[2,1024]{1,0:T(2,128)S(1)}, f32[2,1024]{1,0:T(2,128)}, u32[]{:S(2)}) copy-start(f32[2,1024]{1,0:T(2,128)} %param.18) | copy-start | bytes 24580
  67.8 19.9 %collective-permute-start = (f32[2,10,512]{2,1,0:T(8,128)S(1)}, f32[2,10,512]{2,1,0:T(8,128)}, u32[]{:S(2)}, u32[]{:S(2)}) collective-permute-start(f32[2,10,512]{2,1,0:T(8,128)S(1)} %get-tuple-element.86), channel_id=1, source_target_pairs={{0,8},{8,16},{16,24},{24,32},{32,40},{40,48},{48,56},{56,64},{64,7... | collective-permute-start | bytes 122888 | tf_op jit(solution)/shard_map/ppermute | solution.py:190
  70.2 18.2 %copy-start.21 = (bf16[1,2,8,128]{3,2,1,0:T(8,128)(2,1)S(1)}, bf16[1,2,8,128]{3,2,1,0:T(8,128)(2,1)}, u32[]{:S(2)}) copy-start(bf16[1,2,8,128]{3,2,1,0:T(8,128)(2,1)} %copy.152) | copy-start | bytes 12292
  70.2 18.2 %copy-start.23 = (s32[8,3]{0,1:T(4,128)S(1)}, s32[8,3]{0,1:T(4,128)}, u32[]{:S(2)}) copy-start(s32[8,3]{0,1:T(4,128)} %fusion.166) | copy-start | bytes 292
  70.3 2.9 %copy-start.6 = (f32[8,8192]{1,0:T(8,128)}, f32[8,8192]{1,0:T(8,128)S(1)}, u32[]{:S(2)}) copy-start(f32[8,8192]{1,0:T(8,128)S(1)} %get-tuple-element.62) | copy-start | bytes 786436
  70.3 31.2 %copy-start.10 = (bf16[8,8192]{1,0:T(8,128)(2,1)}, bf16[8,8192]{1,0:T(8,128)(2,1)S(1)}, u32[]{:S(2)}) copy-start(bf16[8,8192]{1,0:T(8,128)(2,1)S(1)} %get-tuple-element.61) | copy-start | bytes 393220
  74.0 26.1 %all-to-all-start.1 = ((f32[64,4,128]{2,1,0:T(4,128)}), f32[64,4,128]{2,1,0:T(4,128)S(1)}, u32[]{:S(2)}, u32[]{:S(2)}) async-start(f32[64,4,128]{2,1,0:T(4,128)} %maximum_bitcast_fusion), calls=%async_computation.1 | async-start | bytes 262144 | tf_op jit(solution)/shard_map/all_to_all | solution.py:179
  87.6 15.6 %copy-start.5 = (bf16[6,2,8,512]{3,2,1,0:T(8,128)(2,1)}, bf16[6,2,8,512]{3,2,1,0:T(8,128)(2,1)S(1)}, u32[]{:S(2)}) copy-start(bf16[6,2,8,512]{3,2,1,0:T(8,128)(2,1)S(1)} %bitcast_dynamic-update-slice_fusion.coef_ref) | copy-start | bytes 294916
  100.1 1.6 copy-start.2
  101.7 2.1 copy-start.1
  106.8 2.6 %copy-start.7 = (f32[8,8192]{1,0:T(8,128)S(1)}, f32[8,8192]{1,0:T(8,128)}, u32[]{:S(2)}) copy-start(f32[8,8192]{1,0:T(8,128)} %copy-done.6) | copy-start | bytes 786436
  109.3 11.0 %copy-start.13 = (f32[2,8,512]{2,1,0:T(8,128)S(1)}, f32[2,8,512]{2,1,0:T(8,128)}, u32[]{:S(2)}) copy-start(f32[2,8,512]{2,1,0:T(8,128)} %get-tuple-element.18) | copy-start | bytes 98308
  109.3 11.0 %copy-start.14 = (f32[2,8,512]{2,1,0:T(8,128)S(1)}, f32[2,8,512]{2,1,0:T(8,128)}, u32[]{:S(2)}) copy-start(f32[2,8,512]{2,1,0:T(8,128)} %get-tuple-element.17) | copy-start | bytes 98308
  109.3 39.4 %copy-start.24 = (s32[8,3]{0,1:T(4,128)S(1)}, s32[8,3]{0,1:T(4,128)}, u32[]{:S(2)}) copy-start(s32[8,3]{0,1:T(4,128)} %fusion.166) | copy-start | bytes 292
  112.2 39.1 %all-to-all-start.2 = ((f32[64,4,128]{2,1,0:T(4,128)}), f32[64,4,128]{2,1,0:T(4,128)S(1)}, u32[]{:S(2)}, u32[]{:S(2)}) async-start(f32[64,4,128]{2,1,0:T(4,128)} %maximum_bitcast_fusion.1), calls=%async_computation.2 | async-start | bytes 262144 | tf_op jit(solution)/shard_map/all_to_all | solution.py:179
  120.3 27.6 %collective-permute-start.7 = (f32[2,10,512]{2,1,0:T(8,128)S(1)}, f32[2,10,512]{2,1,0:T(8,128)S(1)}, u32[]{:S(2)}, u32[]{:S(2)}) collective-permute-start(f32[2,10,512]{2,1,0:T(8,128)S(1)} %get-tuple-element.79), channel_id=1, source_target_pairs={{8,0},{16,8},{24,16},{32,24},{40,32},{48,40},{56,48},{64,56},{72,6... | collective-permute-start | bytes 122888 | tf_op jit(solution)/shard_map/ppermute | solution.py:193
  130.3 17.6 %collective-permute-start.6 = (f32[2,10,512]{2,1,0:T(8,128)S(1)}, f32[2,10,512]{2,1,0:T(8,128)}, u32[]{:S(2)}, u32[]{:S(2)}) collective-permute-start(f32[2,10,512]{2,1,0:T(8,128)S(1)} %get-tuple-element.80), channel_id=1, source_target_pairs={{0,8},{8,16},{16,24},{24,32},{32,40},{40,48},{48,56},{56,64},{64,7... | collective-permute-start | bytes 122888 | tf_op jit(solution)/shard_map/ppermute | solution.py:190
  132.2 26.1 %collective-permute-start.8 = (f32[2,2,512]{2,1,0:T(2,128)}, f32[2,2,512]{2,1,0:T(2,128)S(1)}, u32[]{:S(2)}, u32[]{:S(2)}) collective-permute-start(f32[2,2,512]{2,1,0:T(2,128)} %get-tuple-element.19), channel_id=1, source_target_pairs={{0,1},{1,2},{2,3},{3,4},{4,5},{5,6},{6,7},{8,9},{9,10},{10,11},{11... | collective-permute-start | bytes 24584 | tf_op jit(solution)/shard_map/ppermute | solution.py:186
  138.0 20.4 %collective-permute-start.9 = (f32[2,2,512]{2,1,0:T(2,128)}, f32[2,2,512]{2,1,0:T(2,128)}, u32[]{:S(2)}, u32[]{:S(2)}) collective-permute-start(f32[2,2,512]{2,1,0:T(2,128)} %get-tuple-element.20), channel_id=1, source_target_pairs={{1,0},{2,1},{3,2},{4,3},{5,4},{6,5},{7,6},{9,8},{10,9},{11,10},{12... | collective-permute-start | bytes 24584 | tf_op jit(solution)/shard_map/ppermute | solution.py:187
  151.3 2.6 %copy-start.3 = (bf16[64,8192]{1,0:T(8,128)(2,1)S(1)}, bf16[64,8192]{1,0:T(8,128)(2,1)}, u32[]{:S(2)}) copy-start(bf16[64,8192]{1,0:T(8,128)(2,1)} %get-tuple-element.66) | copy-start | bytes 3145732
  153.8 1.7 copy-start.8
  158.4 0.6 copy-start.18
  161.7 16.7 %copy-start.15 = (f32[2,8,512]{2,1,0:T(8,128)S(1)}, f32[2,8,512]{2,1,0:T(8,128)}, u32[]{:S(2)}) copy-start(f32[2,8,512]{2,1,0:T(8,128)} %get-tuple-element.24) | copy-start | bytes 98308
  161.7 16.7 %copy-start.16 = (f32[2,8,512]{2,1,0:T(8,128)S(1)}, f32[2,8,512]{2,1,0:T(8,128)}, u32[]{:S(2)}) copy-start(f32[2,8,512]{2,1,0:T(8,128)} %get-tuple-element.23) | copy-start | bytes 98308
  161.7 28.7 %copy-start.28 = (f32[2,2,512]{2,1,0:T(2,128)S(1)}, f32[2,2,512]{2,1,0:T(2,128)}, u32[]{:S(2)}) copy-start(f32[2,2,512]{2,1,0:T(2,128)} %get-tuple-element.25) | copy-start | bytes 24580
  161.7 33.9 %copy-start.27 = (f32[2,2,512]{2,1,0:T(2,128)S(1)}, f32[2,2,512]{2,1,0:T(2,128)}, u32[]{:S(2)}) copy-start(f32[2,2,512]{2,1,0:T(2,128)} %get-tuple-element.26) | copy-start | bytes 24580
  161.7 44.2 %copy-start.25 = (s32[8,3]{0,1:T(4,128)S(1)}, s32[8,3]{0,1:T(4,128)}, u32[]{:S(2)}) copy-start(s32[8,3]{0,1:T(4,128)} %fusion.166) | copy-start | bytes 292
  164.2 43.7 %copy-start.11 = (bf16[8,8192]{1,0:T(8,128)(2,1)S(1)}, bf16[8,8192]{1,0:T(8,128)(2,1)}, u32[]{:S(2)}) copy-start(bf16[8,8192]{1,0:T(8,128)(2,1)} %copy-done.10) | copy-start | bytes 393220
  164.3 45.0 %copy-start.4 = (bf16[64,8192]{1,0:T(8,128)(2,1)S(1)}, bf16[64,8192]{1,0:T(8,128)(2,1)}, u32[]{:S(2)}) copy-start(bf16[64,8192]{1,0:T(8,128)(2,1)} %get-tuple-element.66) | copy-start | bytes 3145732
  165.0 42.7 %all-to-all-start.3 = ((f32[64,4,128]{2,1,0:T(4,128)}), f32[64,4,128]{2,1,0:T(4,128)S(1)}, u32[]{:S(2)}, u32[]{:S(2)}) async-start(f32[64,4,128]{2,1,0:T(4,128)} %maximum_bitcast_fusion.2), calls=%async_computation.3 | async-start | bytes 262144 | tf_op jit(solution)/shard_map/all_to_all | solution.py:179
  178.4 27.4 %collective-permute-start.11 = (f32[2,10,512]{2,1,0:T(8,128)S(1)}, f32[2,10,512]{2,1,0:T(8,128)S(1)}, u32[]{:S(2)}, u32[]{:S(2)}) collective-permute-start(f32[2,10,512]{2,1,0:T(8,128)S(1)} %get-tuple-element.75), channel_id=1, source_target_pairs={{8,0},{16,8},{24,16},{32,24},{40,32},{48,40},{56,48},{64,56},{72,6... | collective-permute-start | bytes 122888 | tf_op jit(solution)/shard_map/ppermute | solution.py:193
  188.4 17.5 %collective-permute-start.10 = (f32[2,10,512]{2,1,0:T(8,128)S(1)}, f32[2,10,512]{2,1,0:T(8,128)S(1)}, u32[]{:S(2)}, u32[]{:S(2)}) collective-permute-start(f32[2,10,512]{2,1,0:T(8,128)S(1)} %get-tuple-element.76), channel_id=1, source_target_pairs={{0,8},{8,16},{16,24},{24,32},{32,40},{40,48},{48,56},{56,64},{64,7... | collective-permute-start | bytes 122888 | tf_op jit(solution)/shard_map/ppermute | solution.py:190
  190.3 21.9 %collective-permute-start.12 = (f32[2,2,512]{2,1,0:T(2,128)S(1)}, f32[2,2,512]{2,1,0:T(2,128)S(1)}, u32[]{:S(2)}, u32[]{:S(2)}) collective-permute-start(f32[2,2,512]{2,1,0:T(2,128)S(1)} %copy-done.28), channel_id=1, source_target_pairs={{0,1},{1,2},{2,3},{3,4},{4,5},{5,6},{6,7},{8,9},{9,10},{10,11},{11... | collective-permute-start | bytes 24584 | tf_op jit(solution)/shard_map/ppermute | solution.py:186
  195.6 16.6 %collective-permute-start.13 = (f32[2,2,512]{2,1,0:T(2,128)S(1)}, f32[2,2,512]{2,1,0:T(2,128)S(1)}, u32[]{:S(2)}, u32[]{:S(2)}) collective-permute-start(f32[2,2,512]{2,1,0:T(2,128)S(1)} %copy-done.27), channel_id=1, source_target_pairs={{1,0},{2,1},{3,2},{4,3},{5,4},{6,5},{7,6},{9,8},{10,9},{11,10},{12... | collective-permute-start | bytes 24584 | tf_op jit(solution)/shard_map/ppermute | solution.py:187
  212.2 0.6 copy-start.19
  212.2 0.6 copy-start.20

commit v5 on v4

--- a/solution.py
+++ b/solution.py
@@ -53,8 +53,8 @@
         rhs = []
         for f in range(2):
             here = rock_ref[f, z]
-            down = below_ref[f] if z == 0 else rock_ref[f, z - 1]
-            up = above_ref[f] if z == depth - 1 else rock_ref[f, z + 1]
+            down = below_ref[f, :rows] if z == 0 else rock_ref[f, z - 1]
+            up = above_ref[f, :rows] if z == depth - 1 else rock_ref[f, z + 1]
             west = jnp.where(row == 0, left_ref[f, z][None, :], pltpu.roll(here, 1, 0))
             east = jnp.where(row == rows - 1, right_ref[f, z][None, :], pltpu.roll(here, rows - 1, 0))
             south = jnp.where(lane == 0, 0.0, pltpu.roll(here, 1, 1))
@@ -183,19 +183,17 @@
         got_fracture = got[2:].reshape(2, -1)
         fracture_low = fracture_now.astype(jnp.bfloat16).reshape(2, blocks, segment_width)
         fracture_wide = fracture_low.astype(jnp.float32).reshape(2, -1, rock_now.shape[-1])
+        from_below = lax.ppermute(
+            jnp.concatenate([rock_high, fracture_wide], 1), "slab", forward_slab
+        )
+        from_above = lax.ppermute(
+            jnp.concatenate([rock_low, fracture_wide], 1), "slab", backward_slab
+        )
         from_left = lax.ppermute(rock_last, "plane", forward_plane)
         from_right = lax.ppermute(rock_first, "plane", backward_plane)
         if sweep_index == 0:
+            layer_above = shifted(transmissibility[0, :1], "slab", -1)
             layer_beside = shifted(transmissibility[1, :, :1], "plane", -1)
-        from_below = lax.ppermute(
-            jnp.concatenate([rock_high, fracture_wide], 1), "slab", forward_slab
-        )
-        from_above = lax.ppermute(
-            jnp.concatenate([rock_low, fracture_wide], 1), "slab", backward_slab
-        )
-        if sweep_index == 0:
-            layer_above = shifted(transmissibility[0, :1], "slab", -1)
-        if sweep_index == 0:
             upper_z = jnp.concatenate([coef_z[1:], layer_above], 0)
             upper_x = jnp.concatenate([coef_x[:, 1:], layer_beside], 1)
             upper_y = jnp.pad(coef_y[..., 1:], ((0, 0), (0, 0), (0, 1)))
@@ -224,8 +222,8 @@
             rock_now,
             rock_source,
             leak_rock,
-            from_below[:, :layer_rows],
-            from_above[:, :layer_rows],
+            from_below,
+            from_above,
             from_left,
             from_right,
             coef_all,

time: 216 us -> 212 us (0.981)
  local copies, waits for them, and re-layouts: 14.5 us -> 8.82 us
    slice x6 -> x0, local copies, waits for them, and re-layouts: 5.2 us -> none  [the longest x3 3.34 us: shards(): from_below[:, :layer_rows]]
  transfers between devices with their start and end apart: 18 -> 18, of which waited for: 1 -> 1; matrix products, arithmetic and copies ran while one was open for 20% -> 18% of each run, Pallas kernels for 0% -> 0%
where the time goes in v5:
time: 212 us; the launch traced here: 210 us
  starting transfers between devices  144 us (68%)
  matrix products  26.4 us (12%)
  other arithmetic  12.7 us (6%)
  waiting for transfers between devices  11.1 us (5%)
  local copies, waits for them, and re-layouts  8.82 us (4%)
  Pallas kernels  5.62 us (3%)
    all_to_all x3, starting transfers between devices, shards(): lax.all_to_all(send.transpose(1, 0, 2), 'slab', split_axis=0, concat_axis...  35 us
    ppermute x3, starting transfers between devices, shards(): from_right = lax.ppermute(rock_first, 'plane', backward_plane)  29.5 us
    ppermute x3, starting transfers between devices, shards(): lax.ppermute(jnp.concatenate([rock_low, fracture_wide], 1), 'slab', backw...  22 us
    ppermute x2, starting transfers between devices, shifted(): lax.ppermute(value, axis, [(source, source + steps) for source in range(f...  18.2 us
    ppermute x3, starting transfers between devices, shards(): from_left = lax.ppermute(rock_last, 'plane', forward_plane)  17 us
    all_to_all x1, starting transfers between devices, shards(): lax.all_to_all(contact_segment[0], 'slab', split_axis=0, concat_axis=0, t...  16.3 us
    dot_general x6, matrix products, pick_values(): jnp.einsum('kc,grc->grk', col_mask, parts, preferred_element_type=jnp.flo...  13.6 us
    all_to_all x3, waiting for transfers between devices, shards(): lax.all_to_all(send.transpose(1, 0, 2), 'slab', split_axis=0, concat_axis...  11.1 us
  transfers between devices with their start and end apart: 18, of which 1 were waited for; matrix products, arithmetic and copies ran while one was open for 18% of the time, Pallas kernels for 0%

profile of v5, /device:TPU:30, one launch (start us, length us, event | category | flops | bytes accessed | tf_op | source)
XLA Modules:
  0.0 210.4 jit_solution(4464963848262953670)
XLA Ops:
  0.7 16.3 %all-to-all-start = ((s32[64,1,128]{2,1,0:T(1,128)}), s32[64,1,128]{2,1,0:T(1,128)S(1)}, u32[]{:S(2)}, u32[]{:S(2)}) async-start(s32[64,1,128]{2,1,0:T(1,128)} %bitcast.260), calls=%async_computation | async-start | bytes 65536 | tf_op jit(solution)/shard_map/all_to_all | solution.py:126
  17.0 0.7 slice_bitcast_fusion.12
  17.7 8.5 %collective-permute-start.5 = (bf16[2,1,512]{2,1,0:T(2,128)(2,1)S(1)}, bf16[2,1,512]{2,1,0:T(2,128)(2,1)S(1)}, u32[]{:S(2)}, u32[]{:S(2)}) collective-permute-start(bf16[2,1,512]{2,1,0:T(2,128)(2,1)S(1)} %slice_bitcast_fusion.12), channel_id=1, source_target_pairs={{1,0},{2,1},{3,2},{4,3},{5,4},{6,5},{7,6},{9,8},{10,9},{11,10},{12... | collective-permute-start | bytes 6152 | tf_op jit(solution)/shard_map/ppermute | solution.py:17
  26.9 9.7 %collective-permute-start.4 = (bf16[1,8,512]{2,1,0:T(8,128)(2,1)S(1)}, bf16[1,8,512]{2,1,0:T(8,128)(2,1)S(1)}, u32[]{:S(2)}, u32[]{:S(2)}) collective-permute-start(bf16[1,8,512]{2,1,0:T(8,128)(2,1)S(1)} %get-tuple-element.60), channel_id=1, source_target_pairs={{8,0},{16,8},{24,16},{32,24},{40,32},{48,40},{56,48},{64,56},{72,6... | collective-permute-start | bytes 24584 | tf_op jit(solution)/shard_map/ppermute | solution.py:17
  36.6 0.9 fusion.178
  38.1 6.1 %collective-permute-start.2 = (f32[2,2,512]{2,1,0:T(2,128)}, f32[2,2,512]{2,1,0:T(2,128)}, u32[]{:S(2)}, u32[]{:S(2)}) collective-permute-start(f32[2,2,512]{2,1,0:T(2,128)} %bitcast.248), channel_id=1, source_target_pairs={{0,1},{1,2},{2,3},{3,4},{4,5},{5,6},{6,7},{8,9},{9,10},{10,11},{11... | collective-permute-start | bytes 24584 | tf_op jit(solution)/shard_map/ppermute | solution.py:192
  44.8 9.4 %collective-permute-start.3 = (f32[2,2,512]{2,1,0:T(2,128)}, f32[2,2,512]{2,1,0:T(2,128)}, u32[]{:S(2)}, u32[]{:S(2)}) collective-permute-start(f32[2,2,512]{2,1,0:T(2,128)} %bitcast.247), channel_id=1, source_target_pairs={{1,0},{2,1},{3,2},{4,3},{5,4},{6,5},{7,6},{9,8},{10,9},{11,10},{12... | collective-permute-start | bytes 24584 | tf_op jit(solution)/shard_map/ppermute | solution.py:193
  54.2 0.8 slice_bitcast_fusion.6
  56.3 2.0 collective-permute-start.1
  58.3 0.7 slice_dynamic-update-slice_fusion
  59.8 0.8 add_select_fusion.6
  60.6 0.9 reduce-precision_convert_fusion.2
  61.5 1.3 fusion.76
  62.9 2.5 %fusion.23 = f32[4,8192]{1,0:T(4,128)S(1)} fusion(f32[64,8192]{1,0:T(8,128)S(1)} %get-tuple-element.65, s32[8192]{0:T(1024)S(1)} %get-tuple-element.63, bf16[2,64,128]{2,1,0:T(8,128)(2,1)S(1)} %get-tuple-element.55, bf16[2,64,128]{2,1,0:T(8,128)(2,1)S(1)} %get-tuple-element.54), kind=kOutput, calls=%fused_computation.19 | convolution fusion | flops 542113792 | bytes 2326528 | tf_op jit(solution)/shard_map/kc,grc->grk/dot_general | solution.py:29
  65.4 2.3 %collective-permute-start = (f32[2,10,512]{2,1,0:T(8,128)}, f32[2,10,512]{2,1,0:T(8,128)}, u32[]{:S(2)}, u32[]{:S(2)}) collective-permute-start(f32[2,10,512]{2,1,0:T(8,128)} %get-tuple-element.86), channel_id=1, source_target_pairs={{0,8},{8,16},{16,24},{24,32},{32,40},{40,48},{48,56},{56,64},{64,7... | collective-permute-start | bytes 122888 | tf_op jit(solution)/shard_map/ppermute | solution.py:186
  68.6 2.1 fusion.51
  71.5 13.6 %all-to-all-start.1 = ((f32[64,4,128]{2,1,0:T(4,128)}), f32[64,4,128]{2,1,0:T(4,128)S(1)}, u32[]{:S(2)}, u32[]{:S(2)}) async-start(f32[64,4,128]{2,1,0:T(4,128)} %maximum_bitcast_fusion), calls=%async_computation.1 | async-start | bytes 262144 | tf_op jit(solution)/shard_map/all_to_all | solution.py:179
  85.2 0.8 slice.322
  86.6 11.1 %all-to-all-done.1 = f32[64,4,128]{2,1,0:T(4,128)S(1)} async-done(((f32[64,4,128]{2,1,0:T(4,128)}), f32[64,4,128]{2,1,0:T(4,128)S(1)}, u32[]{:S(2)}, u32[]{:S(2)}) %all-to-all-start.1) | async-done | bytes 131104 | tf_op jit(solution)/shard_map/all_to_all | solution.py:179
  97.8 1.3 fusion.20
  99.2 1.5 fusion.4
  101.7 1.9 shard_map.140
  103.5 0.9 reduce-precision_convert_fusion.1
  104.4 2.5 %fusion.26 = f32[4,8192]{1,0:T(4,128)S(1)} fusion(f32[64,8192]{1,0:T(8,128)S(1)} %get-tuple-element.65, s32[8192]{0:T(1024)S(1)} %get-tuple-element.63, bf16[2,64,128]{2,1,0:T(8,128)(2,1)S(1)} %get-tuple-element.49, bf16[2,64,128]{2,1,0:T(8,128)(2,1)S(1)} %get-tuple-element.48), kind=kOutput, calls=%fused_computation.20 | convolution fusion | flops 542113792 | bytes 2326528 | tf_op jit(solution)/shard_map/kc,grc->grk/dot_general | solution.py:29
  107.0 2.1 fusion.54
  109.8 8.1 %all-to-all-start.2 = ((f32[64,4,128]{2,1,0:T(4,128)}), f32[64,4,128]{2,1,0:T(4,128)S(1)}, u32[]{:S(2)}, u32[]{:S(2)}) async-start(f32[64,4,128]{2,1,0:T(4,128)} %maximum_bitcast_fusion.1), calls=%async_computation.2 | async-start | bytes 262144 | tf_op jit(solution)/shard_map/all_to_all | solution.py:179
  118.5 10.0 %collective-permute-start.7 = (f32[2,10,512]{2,1,0:T(8,128)S(1)}, f32[2,10,512]{2,1,0:T(8,128)S(1)}, u32[]{:S(2)}, u32[]{:S(2)}) collective-permute-start(f32[2,10,512]{2,1,0:T(8,128)S(1)} %get-tuple-element.79), channel_id=1, source_target_pairs={{8,0},{16,8},{24,16},{32,24},{40,32},{48,40},{56,48},{64,56},{72,6... | collective-permute-start | bytes 122888 | tf_op jit(solution)/shard_map/ppermute | solution.py:189
  128.5 1.9 collective-permute-start.6
  130.5 5.7 %collective-permute-start.8 = (f32[2,2,512]{2,1,0:T(2,128)}, f32[2,2,512]{2,1,0:T(2,128)}, u32[]{:S(2)}, u32[]{:S(2)}) collective-permute-start(f32[2,2,512]{2,1,0:T(2,128)} %get-tuple-element.19), channel_id=1, source_target_pairs={{0,1},{1,2},{2,3},{3,4},{4,5},{5,6},{6,7},{8,9},{9,10},{10,11},{11... | collective-permute-start | bytes 24584 | tf_op jit(solution)/shard_map/ppermute | solution.py:192
  136.2 9.9 %collective-permute-start.9 = (f32[2,2,512]{2,1,0:T(2,128)}, f32[2,2,512]{2,1,0:T(2,128)}, u32[]{:S(2)}, u32[]{:S(2)}) collective-permute-start(f32[2,2,512]{2,1,0:T(2,128)} %get-tuple-element.20), channel_id=1, source_target_pairs={{1,0},{2,1},{3,2},{4,3},{5,4},{6,5},{7,6},{9,8},{10,9},{11,10},{12... | collective-permute-start | bytes 24584 | tf_op jit(solution)/shard_map/ppermute | solution.py:193
  146.2 0.8 slice.320
  147.5 0.9 fusion.61
  149.0 2.1 %fusion.17 = f32[4,8,128]{2,1,0:T(8,128)S(1)} fusion(s32[8192]{0:T(1024)} %copy-done.16, bf16[4,8192]{1,0:T(4,128)(2,1)S(1)} %pad_maximum_fusion.9, bf16[8,8192]{1,0:T(8,128)(2,1)S(1)} %get-tuple-element.61), kind=kOutput, calls=%fused_computation.17 | convolution fusion | flops 68419584 | bytes 245760 | tf_op jit(solution)/shard_map/grk,kc->grc/dot_general | solution.py:39
  151.2 1.5 fusion.2
  153.0 2.1 fusion.57
  155.8 1.9 shard_map.141
  157.7 0.9 reduce-precision_convert_fusion
  158.6 2.5 %fusion.29 = f32[4,8192]{1,0:T(4,128)S(1)} fusion(f32[64,8192]{1,0:T(8,128)S(1)} %get-tuple-element.65, s32[8192]{0:T(1024)S(1)} %get-tuple-element.63, bf16[2,64,128]{2,1,0:T(8,128)(2,1)S(1)} %get-tuple-element.47, bf16[2,64,128]{2,1,0:T(8,128)(2,1)S(1)} %get-tuple-element.46), kind=kOutput, calls=%fused_computation.21 | convolution fusion | flops 542113792 | bytes 2326528 | tf_op jit(solution)/shard_map/kc,grc->grk/dot_general | solution.py:29
  161.1 0.7 maximum_bitcast_fusion.2
  161.9 13.4 %all-to-all-start.3 = ((f32[64,4,128]{2,1,0:T(4,128)}), f32[64,4,128]{2,1,0:T(4,128)S(1)}, u32[]{:S(2)}, u32[]{:S(2)}) async-start(f32[64,4,128]{2,1,0:T(4,128)} %maximum_bitcast_fusion.2), calls=%async_computation.3 | async-start | bytes 262144 | tf_op jit(solution)/shard_map/all_to_all | solution.py:179
  175.3 10.0 %collective-permute-start.11 = (f32[2,10,512]{2,1,0:T(8,128)S(1)}, f32[2,10,512]{2,1,0:T(8,128)S(1)}, u32[]{:S(2)}, u32[]{:S(2)}) collective-permute-start(f32[2,10,512]{2,1,0:T(8,128)S(1)} %get-tuple-element.75), channel_id=1, source_target_pairs={{8,0},{16,8},{24,16},{32,24},{40,32},{48,40},{56,48},{64,56},{72,6... | collective-permute-start | bytes 122888 | tf_op jit(solution)/shard_map/ppermute | solution.py:189
  185.3 1.9 collective-permute-start.10
  187.2 5.2 %collective-permute-start.12 = (f32[2,2,512]{2,1,0:T(2,128)S(1)}, f32[2,2,512]{2,1,0:T(2,128)S(1)}, u32[]{:S(2)}, u32[]{:S(2)}) collective-permute-start(f32[2,2,512]{2,1,0:T(2,128)S(1)} %copy-done.32), channel_id=1, source_target_pairs={{0,1},{1,2},{2,3},{3,4},{4,5},{5,6},{6,7},{8,9},{9,10},{10,11},{11... | collective-permute-start | bytes 24584 | tf_op jit(solution)/shard_map/ppermute | solution.py:192
  192.5 10.2 %collective-permute-start.13 = (f32[2,2,512]{2,1,0:T(2,128)S(1)}, f32[2,2,512]{2,1,0:T(2,128)S(1)}, u32[]{:S(2)}, u32[]{:S(2)}) collective-permute-start(f32[2,2,512]{2,1,0:T(2,128)S(1)} %copy-done.31), channel_id=1, source_target_pairs={{1,0},{2,1},{3,2},{4,3},{5,4},{6,5},{7,6},{9,8},{10,9},{11,10},{12... | collective-permute-start | bytes 24584 | tf_op jit(solution)/shard_map/ppermute | solution.py:193
  203.6 1.3 fusion.14
  205.0 1.5 fusion
  207.1 0.8 convolution_bitcast_fusion
  208.5 1.9 shard_map.142
  (149 shorter events, 13.4 us)
Async XLA Ops:
  0.6 85.5 %copy-start = (bf16[8,3,128,128]{3,2,1,0:T(8,128)(2,1)S(1)}, bf16[8,3,128,128]{3,2,1,0:T(8,128)(2,1)}, u32[]{:S(2)}) copy-start(bf16[8,3,128,128]{3,2,1,0:T(8,128)(2,1)} %param.19) | copy-start | bytes 2359300
  0.6 62.1 %copy-start.30 = (s32[1,64]{1,0:T(1,128)S(1)}, s32[1,64]{1,0:T(1,128)}, u32[]{:S(2)}) copy-start(s32[1,64]{1,0:T(1,128)} %param.25) | copy-start | bytes 772
  0.7 62.1 %copy-start.23 = (f32[1,64,128]{2,1,0:T(8,128)S(1)}, f32[1,64,128]{2,1,0:T(8,128)}, u32[]{:S(2)}) copy-start(f32[1,64,128]{2,1,0:T(8,128)} %param.24) | copy-start | bytes 98308
  0.7 67.9 %all-to-all-start = ((s32[64,1,128]{2,1,0:T(1,128)}), s32[64,1,128]{2,1,0:T(1,128)S(1)}, u32[]{:S(2)}, u32[]{:S(2)}) async-start(s32[64,1,128]{2,1,0:T(1,128)} %bitcast.260), calls=%async_computation | async-start | bytes 65536 | tf_op jit(solution)/shard_map/all_to_all | solution.py:126
  17.7 50.8 %collective-permute-start.5 = (bf16[2,1,512]{2,1,0:T(2,128)(2,1)S(1)}, bf16[2,1,512]{2,1,0:T(2,128)(2,1)S(1)}, u32[]{:S(2)}, u32[]{:S(2)}) collective-permute-start(bf16[2,1,512]{2,1,0:T(2,128)(2,1)S(1)} %slice_bitcast_fusion.12), channel_id=1, source_target_pairs={{1,0},{2,1},{3,2},{4,3},{5,4},{6,5},{7,6},{9,8},{10,9},{11,10},{12... | collective-permute-start | bytes 6152 | tf_op jit(solution)/shard_map/ppermute | solution.py:17
  26.9 38.6 %collective-permute-start.4 = (bf16[1,8,512]{2,1,0:T(8,128)(2,1)S(1)}, bf16[1,8,512]{2,1,0:T(8,128)(2,1)S(1)}, u32[]{:S(2)}, u32[]{:S(2)}) collective-permute-start(bf16[1,8,512]{2,1,0:T(8,128)(2,1)S(1)} %get-tuple-element.60), channel_id=1, source_target_pairs={{8,0},{16,8},{24,16},{32,24},{40,32},{48,40},{56,48},{64,56},{72,6... | collective-permute-start | bytes 24584 | tf_op jit(solution)/shard_map/ppermute | solution.py:17
  38.1 63.5 %collective-permute-start.2 = (f32[2,2,512]{2,1,0:T(2,128)}, f32[2,2,512]{2,1,0:T(2,128)}, u32[]{:S(2)}, u32[]{:S(2)}) collective-permute-start(f32[2,2,512]{2,1,0:T(2,128)} %bitcast.248), channel_id=1, source_target_pairs={{0,1},{1,2},{2,3},{3,4},{4,5},{5,6},{6,7},{8,9},{9,10},{10,11},{11... | collective-permute-start | bytes 24584 | tf_op jit(solution)/shard_map/ppermute | solution.py:192
  44.8 56.9 %collective-permute-start.3 = (f32[2,2,512]{2,1,0:T(2,128)}, f32[2,2,512]{2,1,0:T(2,128)}, u32[]{:S(2)}, u32[]{:S(2)}) collective-permute-start(f32[2,2,512]{2,1,0:T(2,128)} %bitcast.247), channel_id=1, source_target_pairs={{1,0},{2,1},{3,2},{4,3},{5,4},{6,5},{7,6},{9,8},{10,9},{11,10},{12... | collective-permute-start | bytes 24584 | tf_op jit(solution)/shard_map/ppermute | solution.py:193
  56.3 28.8 %collective-permute-start.1 = (f32[2,10,512]{2,1,0:T(8,128)}, f32[2,10,512]{2,1,0:T(8,128)S(1)}, u32[]{:S(2)}, u32[]{:S(2)}) collective-permute-start(f32[2,10,512]{2,1,0:T(8,128)} %get-tuple-element.85), channel_id=1, source_target_pairs={{8,0},{16,8},{24,16},{32,24},{40,32},{48,40},{56,48},{64,56},{72,6... | collective-permute-start | bytes 122888 | tf_op jit(solution)/shard_map/ppermute | solution.py:189
  62.9 2.5 %copy-start.27 = (s32[8,3]{0,1:T(4,128)S(1)}, s32[8,3]{0,1:T(4,128)}, u32[]{:S(2)}) copy-start(s32[8,3]{0,1:T(4,128)} %param.21) | copy-start | bytes 292
  62.9 4.9 %copy-start.9 = (bf16[3,2,8,512]{3,2,1,0:T(8,128)(2,1)S(1)}, bf16[3,2,8,512]{3,2,1,0:T(8,128)(2,1)}, u32[]{:S(2)}) copy-start(bf16[3,2,8,512]{3,2,1,0:T(8,128)(2,1)} %param.15) | copy-start | bytes 147460
  65.4 20.8 %copy-start.14 = (f32[2,1024]{1,0:T(2,128)S(1)}, f32[2,1024]{1,0:T(2,128)}, u32[]{:S(2)}) copy-start(f32[2,1024]{1,0:T(2,128)} %param.18) | copy-start | bytes 24580
  65.4 21.1 %copy-start.28 = (s32[8,3]{0,1:T(4,128)}, s32[8,3]{0,1:T(4,128)S(1)}, u32[]{:S(2)}) copy-start(s32[8,3]{0,1:T(4,128)S(1)} %fusion.166) | copy-start | bytes 292
  65.4 19.7 %collective-permute-start = (f32[2,10,512]{2,1,0:T(8,128)}, f32[2,10,512]{2,1,0:T(8,128)}, u32[]{:S(2)}, u32[]{:S(2)}) collective-permute-start(f32[2,10,512]{2,1,0:T(8,128)} %get-tuple-element.86), channel_id=1, source_target_pairs={{0,8},{8,16},{16,24},{24,32},{32,40},{40,48},{48,56},{56,64},{64,7... | collective-permute-start | bytes 122888 | tf_op jit(solution)/shard_map/ppermute | solution.py:186
  68.6 38.4 %copy-start.16 = (s32[8192]{0:T(1024)}, s32[8192]{0:T(1024)S(1)}, u32[]{:S(2)}) copy-start(s32[8192]{0:T(1024)S(1)} %get-tuple-element.68) | copy-start | bytes 98308
  68.6 16.5 %copy-start.15 = (bf16[2,8,511]{2,1,0:T(8,128)(2,1)S(1)}, bf16[2,8,511]{2,1,0:T(8,128)(2,1)}, u32[]{:S(2)}) copy-start(bf16[2,8,511]{2,1,0:T(8,128)(2,1)} %slice.211) | copy-start | bytes 49060
  68.6 2.2 %copy-start.6 = (f32[8,8192]{1,0:T(8,128)}, f32[8,8192]{1,0:T(8,128)S(1)}, u32[]{:S(2)}) copy-start(f32[8,8192]{1,0:T(8,128)S(1)} %get-tuple-element.62) | copy-start | bytes 786436
  71.5 26.1 %all-to-all-start.1 = ((f32[64,4,128]{2,1,0:T(4,128)}), f32[64,4,128]{2,1,0:T(4,128)S(1)}, u32[]{:S(2)}, u32[]{:S(2)}) async-start(f32[64,4,128]{2,1,0:T(4,128)} %maximum_bitcast_fusion), calls=%async_computation.1 | async-start | bytes 262144 | tf_op jit(solution)/shard_map/all_to_all | solution.py:179
  85.1 15.6 %copy-start.5 = (bf16[6,2,8,512]{3,2,1,0:T(8,128)(2,1)}, bf16[6,2,8,512]{3,2,1,0:T(8,128)(2,1)S(1)}, u32[]{:S(2)}) copy-start(bf16[6,2,8,512]{3,2,1,0:T(8,128)(2,1)S(1)} %bitcast_dynamic-update-slice_fusion.coef_ref) | copy-start | bytes 294916
  85.1 15.6 %copy-start.10 = (f32[2,10,512]{2,1,0:T(8,128)}, f32[2,10,512]{2,1,0:T(8,128)S(1)}, u32[]{:S(2)}) copy-start(f32[2,10,512]{2,1,0:T(8,128)S(1)} %collective-permute-done.1.above_ref) | copy-start | bytes 122884
  99.2 2.1 %copy-start.1 = (bf16[8,128,128]{2,1,0:T(8,128)(2,1)S(1)}, bf16[8,128,128]{2,1,0:T(8,128)(2,1)}, u32[]{:S(2)}) copy-start(bf16[8,128,128]{2,1,0:T(8,128)(2,1)} %param.20) | copy-start | bytes 786436
  101.6 1.9 copy-start.24
  104.4 2.6 %copy-start.7 = (f32[8,8192]{1,0:T(8,128)S(1)}, f32[8,8192]{1,0:T(8,128)}, u32[]{:S(2)}) copy-start(f32[8,8192]{1,0:T(8,128)} %copy-done.6) | copy-start | bytes 786436
  106.9 11.0 %copy-start.19 = (f32[2,8,512]{2,1,0:T(8,128)S(1)}, f32[2,8,512]{2,1,0:T(8,128)}, u32[]{:S(2)}) copy-start(f32[2,8,512]{2,1,0:T(8,128)} %get-tuple-element.18) | copy-start | bytes 98308
  106.9 11.0 %copy-start.20 = (f32[2,8,512]{2,1,0:T(8,128)S(1)}, f32[2,8,512]{2,1,0:T(8,128)}, u32[]{:S(2)}) copy-start(f32[2,8,512]{2,1,0:T(8,128)} %get-tuple-element.17) | copy-start | bytes 98308
  109.8 39.0 %all-to-all-start.2 = ((f32[64,4,128]{2,1,0:T(4,128)}), f32[64,4,128]{2,1,0:T(4,128)S(1)}, u32[]{:S(2)}, u32[]{:S(2)}) async-start(f32[64,4,128]{2,1,0:T(4,128)} %maximum_bitcast_fusion.1), calls=%async_computation.2 | async-start | bytes 262144 | tf_op jit(solution)/shard_map/all_to_all | solution.py:179
  118.5 27.6 %collective-permute-start.7 = (f32[2,10,512]{2,1,0:T(8,128)S(1)}, f32[2,10,512]{2,1,0:T(8,128)S(1)}, u32[]{:S(2)}, u32[]{:S(2)}) collective-permute-start(f32[2,10,512]{2,1,0:T(8,128)S(1)} %get-tuple-element.79), channel_id=1, source_target_pairs={{8,0},{16,8},{24,16},{32,24},{40,32},{48,40},{56,48},{64,56},{72,6... | collective-permute-start | bytes 122888 | tf_op jit(solution)/shard_map/ppermute | solution.py:189
  128.5 17.6 %collective-permute-start.6 = (f32[2,10,512]{2,1,0:T(8,128)}, f32[2,10,512]{2,1,0:T(8,128)}, u32[]{:S(2)}, u32[]{:S(2)}) collective-permute-start(f32[2,10,512]{2,1,0:T(8,128)} %get-tuple-element.80), channel_id=1, source_target_pairs={{0,8},{8,16},{16,24},{24,32},{32,40},{40,48},{48,56},{56,64},{64,7... | collective-permute-start | bytes 122888 | tf_op jit(solution)/shard_map/ppermute | solution.py:186
  130.5 25.3 %collective-permute-start.8 = (f32[2,2,512]{2,1,0:T(2,128)}, f32[2,2,512]{2,1,0:T(2,128)}, u32[]{:S(2)}, u32[]{:S(2)}) collective-permute-start(f32[2,2,512]{2,1,0:T(2,128)} %get-tuple-element.19), channel_id=1, source_target_pairs={{0,1},{1,2},{2,3},{3,4},{4,5},{5,6},{6,7},{8,9},{9,10},{10,11},{11... | collective-permute-start | bytes 24584 | tf_op jit(solution)/shard_map/ppermute | solution.py:192
  136.2 19.6 %collective-permute-start.9 = (f32[2,2,512]{2,1,0:T(2,128)}, f32[2,2,512]{2,1,0:T(2,128)}, u32[]{:S(2)}, u32[]{:S(2)}) collective-permute-start(f32[2,2,512]{2,1,0:T(2,128)} %get-tuple-element.20), channel_id=1, source_target_pairs={{1,0},{2,1},{3,2},{4,3},{5,4},{6,5},{7,6},{9,8},{10,9},{11,10},{12... | collective-permute-start | bytes 24584 | tf_op jit(solution)/shard_map/ppermute | solution.py:193
  146.1 6.6 %copy-start.11 = (f32[2,10,512]{2,1,0:T(8,128)}, f32[2,10,512]{2,1,0:T(8,128)S(1)}, u32[]{:S(2)}) copy-start(f32[2,10,512]{2,1,0:T(8,128)S(1)} %collective-permute-done.7.above_ref) | copy-start | bytes 122884
  148.8 2.4 %copy-start.3 = (bf16[64,8192]{1,0:T(8,128)(2,1)S(1)}, bf16[64,8192]{1,0:T(8,128)(2,1)}, u32[]{:S(2)}) copy-start(bf16[64,8192]{1,0:T(8,128)(2,1)} %get-tuple-element.66) | copy-start | bytes 3145732
  151.2 1.7 copy-start.8
  151.2 1.7 copy-start.17
  158.5 16.7 %copy-start.21 = (f32[2,8,512]{2,1,0:T(8,128)S(1)}, f32[2,8,512]{2,1,0:T(8,128)}, u32[]{:S(2)}) copy-start(f32[2,8,512]{2,1,0:T(8,128)} %get-tuple-element.24) | copy-start | bytes 98308
  158.5 16.7 %copy-start.22 = (f32[2,8,512]{2,1,0:T(8,128)S(1)}, f32[2,8,512]{2,1,0:T(8,128)}, u32[]{:S(2)}) copy-start(f32[2,8,512]{2,1,0:T(8,128)} %get-tuple-element.23) | copy-start | bytes 98308
  158.5 28.7 %copy-start.32 = (f32[2,2,512]{2,1,0:T(2,128)S(1)}, f32[2,2,512]{2,1,0:T(2,128)}, u32[]{:S(2)}) copy-start(f32[2,2,512]{2,1,0:T(2,128)} %get-tuple-element.25) | copy-start | bytes 24580
  158.6 33.9 %copy-start.31 = (f32[2,2,512]{2,1,0:T(2,128)S(1)}, f32[2,2,512]{2,1,0:T(2,128)}, u32[]{:S(2)}) copy-start(f32[2,2,512]{2,1,0:T(2,128)} %get-tuple-element.26) | copy-start | bytes 24580
  158.6 44.2 %copy-start.29 = (s32[8,3]{0,1:T(4,128)S(1)}, s32[8,3]{0,1:T(4,128)}, u32[]{:S(2)}) copy-start(s32[8,3]{0,1:T(4,128)} %copy-done.28) | copy-start | bytes 292
  161.1 42.5 %copy-start.18 = (s32[8192]{0:T(1024)S(1)}, s32[8192]{0:T(1024)}, u32[]{:S(2)}) copy-start(s32[8192]{0:T(1024)} %copy-done.16) | copy-start | bytes 98308
  161.1 43.8 %copy-start.4 = (bf16[64,8192]{1,0:T(8,128)(2,1)S(1)}, bf16[64,8192]{1,0:T(8,128)(2,1)}, u32[]{:S(2)}) copy-start(bf16[64,8192]{1,0:T(8,128)(2,1)} %get-tuple-element.66) | copy-start | bytes 3145732
  161.9 41.5 %all-to-all-start.3 = ((f32[64,4,128]{2,1,0:T(4,128)}), f32[64,4,128]{2,1,0:T(4,128)S(1)}, u32[]{:S(2)}, u32[]{:S(2)}) async-start(f32[64,4,128]{2,1,0:T(4,128)} %maximum_bitcast_fusion.2), calls=%async_computation.3 | async-start | bytes 262144 | tf_op jit(solution)/shard_map/all_to_all | solution.py:179
  175.3 27.4 %collective-permute-start.11 = (f32[2,10,512]{2,1,0:T(8,128)S(1)}, f32[2,10,512]{2,1,0:T(8,128)S(1)}, u32[]{:S(2)}, u32[]{:S(2)}) collective-permute-start(f32[2,10,512]{2,1,0:T(8,128)S(1)} %get-tuple-element.75), channel_id=1, source_target_pairs={{8,0},{16,8},{24,16},{32,24},{40,32},{48,40},{56,48},{64,56},{72,6... | collective-permute-start | bytes 122888 | tf_op jit(solution)/shard_map/ppermute | solution.py:189
  185.3 17.5 %collective-permute-start.10 = (f32[2,10,512]{2,1,0:T(8,128)S(1)}, f32[2,10,512]{2,1,0:T(8,128)S(1)}, u32[]{:S(2)}, u32[]{:S(2)}) collective-permute-start(f32[2,10,512]{2,1,0:T(8,128)S(1)} %get-tuple-element.76), channel_id=1, source_target_pairs={{0,8},{8,16},{16,24},{24,32},{32,40},{40,48},{48,56},{56,64},{64,7... | collective-permute-start | bytes 122888 | tf_op jit(solution)/shard_map/ppermute | solution.py:186
  187.2 20.7 %collective-permute-start.12 = (f32[2,2,512]{2,1,0:T(2,128)S(1)}, f32[2,2,512]{2,1,0:T(2,128)S(1)}, u32[]{:S(2)}, u32[]{:S(2)}) collective-permute-start(f32[2,2,512]{2,1,0:T(2,128)S(1)} %copy-done.32), channel_id=1, source_target_pairs={{0,1},{1,2},{2,3},{3,4},{4,5},{5,6},{6,7},{8,9},{9,10},{10,11},{11... | collective-permute-start | bytes 24584 | tf_op jit(solution)/shard_map/ppermute | solution.py:192
  192.5 15.5 %collective-permute-start.13 = (f32[2,2,512]{2,1,0:T(2,128)S(1)}, f32[2,2,512]{2,1,0:T(2,128)S(1)}, u32[]{:S(2)}, u32[]{:S(2)}) collective-permute-start(f32[2,2,512]{2,1,0:T(2,128)S(1)} %copy-done.31), channel_id=1, source_target_pairs={{1,0},{2,1},{3,2},{4,3},{5,4},{6,5},{7,6},{9,8},{10,9},{11,10},{12... | collective-permute-start | bytes 24584 | tf_op jit(solution)/shard_map/ppermute | solution.py:193
  202.7 3.7 %copy-start.12 = (f32[2,10,512]{2,1,0:T(8,128)}, f32[2,10,512]{2,1,0:T(8,128)S(1)}, u32[]{:S(2)}) copy-start(f32[2,10,512]{2,1,0:T(8,128)S(1)} %collective-permute-done.11.above_ref) | copy-start | bytes 122884
  202.8 3.7 %copy-start.13 = (f32[2,10,512]{2,1,0:T(8,128)}, f32[2,10,512]{2,1,0:T(8,128)S(1)}, u32[]{:S(2)}) copy-start(f32[2,10,512]{2,1,0:T(8,128)S(1)} %collective-permute-done.10.below_ref) | copy-start | bytes 122884
  (3 other events, 2.7 us)

commit v6 on v5

--- a/solution.py
+++ b/solution.py
@@ -42,7 +42,7 @@
 
 def rock_kernel(
     rock_ref, source_ref, leak_ref, below_ref, above_ref, left_ref, right_ref, coef_ref, inv_ref,
-    out_ref, low_ref, high_ref, first_ref, last_ref, table_ref,
+    fracture_ref, out_ref, low_ref, high_ref, first_ref, last_ref, table_ref,
 ):
     depth, rows, lanes = rock_ref.shape[1:]
     tiles = leak_ref.shape[2]
@@ -72,31 +72,34 @@
             first_ref[f, z] = value[0]
             last_ref[f, z] = value[rows - 1]
             if z == 0:
-                low_ref[f] = value
+                low_ref[f, :rows] = value
+                low_ref[f, rows:] = fracture_ref[f]
             if z == depth - 1:
-                high_ref[f] = value
-
-
-def rock_step(rock, source, leak, below, above, left, right, coef, inverse):
+                high_ref[f, :rows] = value
+                high_ref[f, rows:] = fracture_ref[f]
+
+
+def rock_step(rock, source, leak, below, above, left, right, coef, inverse, fracture):
     fields, depth, rows, lanes = rock.shape
+    halo_rows = rows + fracture.shape[1]
     vmem = pl.BlockSpec(memory_space=pltpu.VMEM)
     return pl.pallas_call(
         rock_kernel,
         out_shape=(
             jax.ShapeDtypeStruct(rock.shape, jnp.float32),
-            jax.ShapeDtypeStruct((fields, rows, lanes), jnp.float32),
-            jax.ShapeDtypeStruct((fields, rows, lanes), jnp.float32),
+            jax.ShapeDtypeStruct((fields, halo_rows, lanes), jnp.float32),
+            jax.ShapeDtypeStruct((fields, halo_rows, lanes), jnp.float32),
             jax.ShapeDtypeStruct((fields, depth, lanes), jnp.float32),
             jax.ShapeDtypeStruct((fields, depth, lanes), jnp.float32),
             jax.ShapeDtypeStruct(leak.shape, jnp.float32),
         ),
-        in_specs=[vmem] * 9,
+        in_specs=[vmem] * 10,
         out_specs=(vmem,) * 6,
         cost_estimate=pl.CostEstimate(
             flops=40 * rock.size, transcendentals=0, bytes_accessed=20 * rock.size
         ),
         interpret=INTERPRET,
-    )(rock, source, leak, below, above, left, right, coef, inverse)
+    )(rock, source, leak, below, above, left, right, coef, inverse, fracture)
 
 
 def shards(
@@ -165,7 +168,10 @@
     rock_now = rock_state
     rock_table = rock_state.reshape(2, depth, rows, tiles, 128).transpose(0, 1, 3, 2, 4)
     rock_table = rock_table.reshape(2, cell_rows, 128)
-    rock_low, rock_high = rock_now[:, 0], rock_now[:, -1]
+    fracture_start = fracture_state.astype(jnp.bfloat16).astype(jnp.float32)
+    fracture_start = fracture_start.reshape(2, -1, rock_state.shape[-1])
+    rock_low = jnp.concatenate([rock_now[:, 0], fracture_start], 1)
+    rock_high = jnp.concatenate([rock_now[:, -1], fracture_start], 1)
     rock_first, rock_last = rock_now[:, :, 0], rock_now[:, :, -1]
     fracture_now = fracture_state
     source_blocks = fracture_source.reshape(2, blocks, segment_width)
@@ -183,12 +189,8 @@
         got_fracture = got[2:].reshape(2, -1)
         fracture_low = fracture_now.astype(jnp.bfloat16).reshape(2, blocks, segment_width)
         fracture_wide = fracture_low.astype(jnp.float32).reshape(2, -1, rock_now.shape[-1])
-        from_below = lax.ppermute(
-            jnp.concatenate([rock_high, fracture_wide], 1), "slab", forward_slab
-        )
-        from_above = lax.ppermute(
-            jnp.concatenate([rock_low, fracture_wide], 1), "slab", backward_slab
-        )
+        from_below = lax.ppermute(rock_high, "slab", forward_slab)
+        from_above = lax.ppermute(rock_low, "slab", backward_slab)
         from_left = lax.ppermute(rock_last, "plane", forward_plane)
         from_right = lax.ppermute(rock_first, "plane", backward_plane)
         if sweep_index == 0:
@@ -228,6 +230,7 @@
             from_right,
             coef_all,
             cell_inverse,
+            fracture_next.astype(jnp.bfloat16).astype(jnp.float32).reshape(fracture_wide.shape),
         )
         rock_table = rock_table.reshape(2, cell_rows, 128)
         fracture_now = fracture_next

time: 212 us -> 208 us (0.981)
  the two profiles are of different devices: /device:TPU:30 before, /device:TPU:14 now
where the time goes in v6:
time: 208 us; the launch traced here: 207 us
  starting transfers between devices  138 us (66%)
  matrix products  26.4 us (13%)
  other arithmetic  12.1 us (6%)
  waiting for transfers between devices  12 us (6%)
  local copies, waits for them, and re-layouts  11.2 us (5%)
  Pallas kernels  5.71 us (3%)
    ppermute x3, starting transfers between devices, shards(): from_right = lax.ppermute(rock_first, 'plane', backward_plane)  29.5 us
    all_to_all x3, starting transfers between devices, shards(): lax.all_to_all(send.transpose(1, 0, 2), 'slab', split_axis=0, concat_axis...  26.6 us
    ppermute x3, starting transfers between devices, shards(): from_above = lax.ppermute(rock_low, 'slab', backward_slab)  24.1 us
    ppermute x2, starting transfers between devices, shifted(): lax.ppermute(value, axis, [(source, source + steps) for source in range(f...  17.9 us
    ppermute x3, starting transfers between devices, shards(): from_left = lax.ppermute(rock_last, 'plane', forward_plane)  17 us
    all_to_all x1, starting transfers between devices, shards(): lax.all_to_all(contact_segment[0], 'slab', split_axis=0, concat_axis=0, t...  16.3 us
    dot_general x6, matrix products, pick_values(): jnp.einsum('kc,grc->grk', col_mask, parts, preferred_element_type=jnp.flo...  13.6 us
    all_to_all x3, waiting for transfers between devices, shards(): lax.all_to_all(send.transpose(1, 0, 2), 'slab', split_axis=0, concat_axis...  11.9 us
  transfers between devices with their start and end apart: 18, of which 1 were waited for; matrix products, arithmetic and copies ran while one was open for 19% of the time, Pallas kernels for 0%

profile of v6, /device:TPU:14, one launch (start us, length us, event | category | flops | bytes accessed | tf_op | source)
XLA Modules:
  0.0 206.6 jit_solution(13923422412765561073)
XLA Ops:
  0.7 16.3 %all-to-all-start = ((s32[64,1,128]{2,1,0:T(1,128)}), s32[64,1,128]{2,1,0:T(1,128)S(1)}, u32[]{:S(2)}, u32[]{:S(2)}) async-start(s32[64,1,128]{2,1,0:T(1,128)} %bitcast.262), calls=%async_computation | async-start | bytes 65536 | tf_op jit(solution)/shard_map/all_to_all | solution.py:129
  17.0 0.7 slice_bitcast_fusion.12
  17.7 8.5 %collective-permute-start.5 = (bf16[2,1,512]{2,1,0:T(2,128)(2,1)S(1)}, bf16[2,1,512]{2,1,0:T(2,128)(2,1)S(1)}, u32[]{:S(2)}, u32[]{:S(2)}) collective-permute-start(bf16[2,1,512]{2,1,0:T(2,128)(2,1)S(1)} %slice_bitcast_fusion.12), channel_id=1, source_target_pairs={{1,0},{2,1},{3,2},{4,3},{5,4},{6,5},{7,6},{9,8},{10,9},{11,10},{12... | collective-permute-start | bytes 6152 | tf_op jit(solution)/shard_map/ppermute | solution.py:17
  26.9 9.4 %collective-permute-start.4 = (bf16[1,8,512]{2,1,0:T(8,128)(2,1)S(1)}, bf16[1,8,512]{2,1,0:T(8,128)(2,1)S(1)}, u32[]{:S(2)}, u32[]{:S(2)}) collective-permute-start(bf16[1,8,512]{2,1,0:T(8,128)(2,1)S(1)} %get-tuple-element.60), channel_id=1, source_target_pairs={{8,0},{16,8},{24,16},{32,24},{40,32},{48,40},{56,48},{64,56},{72,6... | collective-permute-start | bytes 24584 | tf_op jit(solution)/shard_map/ppermute | solution.py:17
  36.3 0.9 fusion.180
  37.9 6.1 %collective-permute-start.2 = (f32[2,2,512]{2,1,0:T(2,128)}, f32[2,2,512]{2,1,0:T(2,128)}, u32[]{:S(2)}, u32[]{:S(2)}) collective-permute-start(f32[2,2,512]{2,1,0:T(2,128)} %bitcast.250), channel_id=1, source_target_pairs={{0,1},{1,2},{2,3},{3,4},{4,5},{5,6},{6,7},{8,9},{9,10},{10,11},{11... | collective-permute-start | bytes 24584 | tf_op jit(solution)/shard_map/ppermute | solution.py:194
  44.5 9.4 %collective-permute-start.3 = (f32[2,2,512]{2,1,0:T(2,128)}, f32[2,2,512]{2,1,0:T(2,128)}, u32[]{:S(2)}, u32[]{:S(2)}) collective-permute-start(f32[2,2,512]{2,1,0:T(2,128)} %bitcast.249), channel_id=1, source_target_pairs={{1,0},{2,1},{3,2},{4,3},{5,4},{6,5},{7,6},{9,8},{10,9},{11,10},{12... | collective-permute-start | bytes 24584 | tf_op jit(solution)/shard_map/ppermute | solution.py:195
  53.9 0.8 slice_bitcast_fusion.6
  56.1 2.0 collective-permute-start.1
  58.1 0.7 slice_dynamic-update-slice_fusion
  59.5 0.8 add_select_fusion.6
  60.3 0.9 reduce-precision_convert_fusion.2
  61.2 1.3 fusion.76
  62.6 2.5 %fusion.23 = f32[4,8192]{1,0:T(4,128)S(1)} fusion(f32[64,8192]{1,0:T(8,128)S(1)} %get-tuple-element.65, s32[8192]{0:T(1024)S(1)} %get-tuple-element.63, bf16[2,64,128]{2,1,0:T(8,128)(2,1)S(1)} %get-tuple-element.55, bf16[2,64,128]{2,1,0:T(8,128)(2,1)S(1)} %get-tuple-element.54), kind=kOutput, calls=%fused_computation.19 | convolution fusion | flops 542113792 | bytes 2326528 | tf_op jit(solution)/shard_map/kc,grc->grk/dot_general | solution.py:29
  65.2 2.3 %collective-permute-start = (f32[2,10,512]{2,1,0:T(8,128)}, f32[2,10,512]{2,1,0:T(8,128)}, u32[]{:S(2)}, u32[]{:S(2)}) collective-permute-start(f32[2,10,512]{2,1,0:T(8,128)} %get-tuple-element.82), channel_id=1, source_target_pairs={{0,8},{8,16},{16,24},{24,32},{32,40},{40,48},{48,56},{56,64},{64,7... | collective-permute-start | bytes 122888 | tf_op jit(solution)/shard_map/ppermute | solution.py:192
  68.4 2.1 fusion.51
  71.3 13.9 %all-to-all-start.1 = ((f32[64,4,128]{2,1,0:T(4,128)}), f32[64,4,128]{2,1,0:T(4,128)S(1)}, u32[]{:S(2)}, u32[]{:S(2)}) async-start(f32[64,4,128]{2,1,0:T(4,128)} %maximum_bitcast_fusion), calls=%async_computation.1 | async-start | bytes 262144 | tf_op jit(solution)/shard_map/all_to_all | solution.py:185
  85.2 0.8 slice.322
  86.6 11.9 %all-to-all-done.1 = f32[64,4,128]{2,1,0:T(4,128)S(1)} async-done(((f32[64,4,128]{2,1,0:T(4,128)}), f32[64,4,128]{2,1,0:T(4,128)S(1)}, u32[]{:S(2)}, u32[]{:S(2)}) %all-to-all-start.1) | async-done | bytes 131104 | tf_op jit(solution)/shard_map/all_to_all | solution.py:185
  98.7 1.3 fusion.20
  100.1 1.5 fusion.4
  103.1 1.9 shard_map.140
  105.0 0.9 reduce-precision_convert_fusion.1
  105.8 2.5 %fusion.26 = f32[4,8192]{1,0:T(4,128)S(1)} fusion(f32[64,8192]{1,0:T(8,128)S(1)} %get-tuple-element.65, s32[8192]{0:T(1024)S(1)} %get-tuple-element.63, bf16[2,64,128]{2,1,0:T(8,128)(2,1)S(1)} %get-tuple-element.49, bf16[2,64,128]{2,1,0:T(8,128)(2,1)S(1)} %get-tuple-element.48), kind=kOutput, calls=%fused_computation.20 | convolution fusion | flops 542113792 | bytes 2326528 | tf_op jit(solution)/shard_map/kc,grc->grk/dot_general | solution.py:29
  108.4 2.1 %fusion.54 = f32[4,8192]{1,0:T(4,128)S(1)} fusion(s32[8192]{0:T(1024)S(1)} %get-tuple-element.68, f32[8,8192]{1,0:T(8,128)S(1)} %copy-done.7, bf16[2,8,128]{2,1,0:T(8,128)(2,1)S(1)} %get-tuple-element.78, bf16[2,8,128]{2,1,0:T(8,128)(2,1)S(1)} %get-tuple-element.77), kind=kOutput, calls=%fused_computation.43 | convolution fusion | flops 68653056 | bytes 434176 | tf_op jit(solution)/shard_map/kc,grc->grk/dot_general | solution.py:29
  110.5 0.7 maximum_bitcast_fusion.1
  111.3 7.2 %all-to-all-start.2 = ((f32[64,4,128]{2,1,0:T(4,128)}), f32[64,4,128]{2,1,0:T(4,128)S(1)}, u32[]{:S(2)}, u32[]{:S(2)}) async-start(f32[64,4,128]{2,1,0:T(4,128)} %maximum_bitcast_fusion.1), calls=%async_computation.2 | async-start | bytes 262144 | tf_op jit(solution)/shard_map/all_to_all | solution.py:185
  118.5 2.0 collective-permute-start.6
  120.5 11.0 %collective-permute-start.7 = (f32[2,10,512]{2,1,0:T(8,128)}, f32[2,10,512]{2,1,0:T(8,128)}, u32[]{:S(2)}, u32[]{:S(2)}) collective-permute-start(f32[2,10,512]{2,1,0:T(8,128)} %get-tuple-element.18), channel_id=1, source_target_pairs={{8,0},{16,8},{24,16},{32,24},{40,32},{48,40},{56,48},{64,56},{72,6... | collective-permute-start | bytes 122888 | tf_op jit(solution)/shard_map/ppermute | solution.py:193
  131.6 5.7 %collective-permute-start.8 = (f32[2,2,512]{2,1,0:T(2,128)}, f32[2,2,512]{2,1,0:T(2,128)}, u32[]{:S(2)}, u32[]{:S(2)}) collective-permute-start(f32[2,2,512]{2,1,0:T(2,128)} %get-tuple-element.19), channel_id=1, source_target_pairs={{0,1},{1,2},{2,3},{3,4},{4,5},{5,6},{6,7},{8,9},{9,10},{10,11},{11... | collective-permute-start | bytes 24584 | tf_op jit(solution)/shard_map/ppermute | solution.py:194
  137.3 9.9 %collective-permute-start.9 = (f32[2,2,512]{2,1,0:T(2,128)}, f32[2,2,512]{2,1,0:T(2,128)}, u32[]{:S(2)}, u32[]{:S(2)}) collective-permute-start(f32[2,2,512]{2,1,0:T(2,128)} %get-tuple-element.20), channel_id=1, source_target_pairs={{1,0},{2,1},{3,2},{4,3},{5,4},{6,5},{7,6},{9,8},{10,9},{11,10},{12... | collective-permute-start | bytes 24584 | tf_op jit(solution)/shard_map/ppermute | solution.py:195
  147.9 0.8 slice.319
  149.2 0.9 fusion.61
  150.7 2.1 %fusion.17 = f32[4,8,128]{2,1,0:T(8,128)S(1)} fusion(s32[8192]{0:T(1024)} %copy-done.16, bf16[4,8192]{1,0:T(4,128)(2,1)S(1)} %pad_maximum_fusion.5, bf16[8,8192]{1,0:T(8,128)(2,1)S(1)} %get-tuple-element.61), kind=kOutput, calls=%fused_computation.17 | convolution fusion | flops 68419584 | bytes 245760 | tf_op jit(solution)/shard_map/grk,kc->grc/dot_general | solution.py:39
  153.1 2.1 fusion.57
  155.3 1.5 fusion.2
  158.1 1.9 shard_map.141
  160.0 0.9 reduce-precision_convert_fusion
  160.9 2.5 %fusion.29 = f32[4,8192]{1,0:T(4,128)S(1)} fusion(f32[64,8192]{1,0:T(8,128)S(1)} %get-tuple-element.65, s32[8192]{0:T(1024)S(1)} %get-tuple-element.63, bf16[2,64,128]{2,1,0:T(8,128)(2,1)S(1)} %get-tuple-element.47, bf16[2,64,128]{2,1,0:T(8,128)(2,1)S(1)} %get-tuple-element.46), kind=kOutput, calls=%fused_computation.21 | convolution fusion | flops 542113792 | bytes 2326528 | tf_op jit(solution)/shard_map/kc,grc->grk/dot_general | solution.py:29
  164.1 5.6 %all-to-all-start.3 = ((f32[64,4,128]{2,1,0:T(4,128)}), f32[64,4,128]{2,1,0:T(4,128)S(1)}, u32[]{:S(2)}, u32[]{:S(2)}) async-start(f32[64,4,128]{2,1,0:T(4,128)} %maximum_bitcast_fusion.2), calls=%async_computation.3 | async-start | bytes 262144 | tf_op jit(solution)/shard_map/all_to_all | solution.py:185
  169.7 2.0 collective-permute-start.10
  171.7 11.0 %collective-permute-start.11 = (f32[2,10,512]{2,1,0:T(8,128)S(1)}, f32[2,10,512]{2,1,0:T(8,128)S(1)}, u32[]{:S(2)}, u32[]{:S(2)}) collective-permute-start(f32[2,10,512]{2,1,0:T(8,128)S(1)} %copy-done.26), channel_id=1, source_target_pairs={{8,0},{16,8},{24,16},{32,24},{40,32},{48,40},{56,48},{64,56},{72,6... | collective-permute-start | bytes 122888 | tf_op jit(solution)/shard_map/ppermute | solution.py:193
  182.8 5.2 %collective-permute-start.12 = (f32[2,2,512]{2,1,0:T(2,128)}, f32[2,2,512]{2,1,0:T(2,128)S(1)}, u32[]{:S(2)}, u32[]{:S(2)}) collective-permute-start(f32[2,2,512]{2,1,0:T(2,128)} %get-tuple-element.25), channel_id=1, source_target_pairs={{0,1},{1,2},{2,3},{3,4},{4,5},{5,6},{6,7},{8,9},{9,10},{10,11},{11... | collective-permute-start | bytes 24584 | tf_op jit(solution)/shard_map/ppermute | solution.py:194
  188.0 10.2 %collective-permute-start.13 = (f32[2,2,512]{2,1,0:T(2,128)}, f32[2,2,512]{2,1,0:T(2,128)S(1)}, u32[]{:S(2)}, u32[]{:S(2)}) collective-permute-start(f32[2,2,512]{2,1,0:T(2,128)} %get-tuple-element.26), channel_id=1, source_target_pairs={{1,0},{2,1},{3,2},{4,3},{5,4},{6,5},{7,6},{9,8},{10,9},{11,10},{12... | collective-permute-start | bytes 24584 | tf_op jit(solution)/shard_map/ppermute | solution.py:195
  199.1 1.3 fusion.14
  200.5 1.5 fusion
  202.0 0.8 fusion.157
  204.7 1.9 shard_map.142
  (137 shorter events, 15.1 us)
Async XLA Ops:
  0.6 85.6 %copy-start = (bf16[8,3,128,128]{3,2,1,0:T(8,128)(2,1)S(1)}, bf16[8,3,128,128]{3,2,1,0:T(8,128)(2,1)}, u32[]{:S(2)}) copy-start(bf16[8,3,128,128]{3,2,1,0:T(8,128)(2,1)} %param.19) | copy-start | bytes 2359300
  0.6 61.9 %copy-start.25 = (s32[1,64]{1,0:T(1,128)S(1)}, s32[1,64]{1,0:T(1,128)}, u32[]{:S(2)}) copy-start(s32[1,64]{1,0:T(1,128)} %param.25) | copy-start | bytes 772
  0.7 61.9 %copy-start.19 = (f32[1,64,128]{2,1,0:T(8,128)S(1)}, f32[1,64,128]{2,1,0:T(8,128)}, u32[]{:S(2)}) copy-start(f32[1,64,128]{2,1,0:T(8,128)} %param.24) | copy-start | bytes 98308
  0.7 67.6 %all-to-all-start = ((s32[64,1,128]{2,1,0:T(1,128)}), s32[64,1,128]{2,1,0:T(1,128)S(1)}, u32[]{:S(2)}, u32[]{:S(2)}) async-start(s32[64,1,128]{2,1,0:T(1,128)} %bitcast.262), calls=%async_computation | async-start | bytes 65536 | tf_op jit(solution)/shard_map/all_to_all | solution.py:129
  17.7 50.5 %collective-permute-start.5 = (bf16[2,1,512]{2,1,0:T(2,128)(2,1)S(1)}, bf16[2,1,512]{2,1,0:T(2,128)(2,1)S(1)}, u32[]{:S(2)}, u32[]{:S(2)}) collective-permute-start(bf16[2,1,512]{2,1,0:T(2,128)(2,1)S(1)} %slice_bitcast_fusion.12), channel_id=1, source_target_pairs={{1,0},{2,1},{3,2},{4,3},{5,4},{6,5},{7,6},{9,8},{10,9},{11,10},{12... | collective-permute-start | bytes 6152 | tf_op jit(solution)/shard_map/ppermute | solution.py:17
  26.9 38.3 %collective-permute-start.4 = (bf16[1,8,512]{2,1,0:T(8,128)(2,1)S(1)}, bf16[1,8,512]{2,1,0:T(8,128)(2,1)S(1)}, u32[]{:S(2)}, u32[]{:S(2)}) collective-permute-start(bf16[1,8,512]{2,1,0:T(8,128)(2,1)S(1)} %get-tuple-element.60), channel_id=1, source_target_pairs={{8,0},{16,8},{24,16},{32,24},{40,32},{48,40},{56,48},{64,56},{72,6... | collective-permute-start | bytes 24584 | tf_op jit(solution)/shard_map/ppermute | solution.py:17
  37.9 65.2 %collective-permute-start.2 = (f32[2,2,512]{2,1,0:T(2,128)}, f32[2,2,512]{2,1,0:T(2,128)}, u32[]{:S(2)}, u32[]{:S(2)}) collective-permute-start(f32[2,2,512]{2,1,0:T(2,128)} %bitcast.250), channel_id=1, source_target_pairs={{0,1},{1,2},{2,3},{3,4},{4,5},{5,6},{6,7},{8,9},{9,10},{10,11},{11... | collective-permute-start | bytes 24584 | tf_op jit(solution)/shard_map/ppermute | solution.py:194
  44.5 58.6 %collective-permute-start.3 = (f32[2,2,512]{2,1,0:T(2,128)}, f32[2,2,512]{2,1,0:T(2,128)}, u32[]{:S(2)}, u32[]{:S(2)}) collective-permute-start(f32[2,2,512]{2,1,0:T(2,128)} %bitcast.249), channel_id=1, source_target_pairs={{1,0},{2,1},{3,2},{4,3},{5,4},{6,5},{7,6},{9,8},{10,9},{11,10},{12... | collective-permute-start | bytes 24584 | tf_op jit(solution)/shard_map/ppermute | solution.py:195
  56.1 29.1 %collective-permute-start.1 = (f32[2,10,512]{2,1,0:T(8,128)}, f32[2,10,512]{2,1,0:T(8,128)S(1)}, u32[]{:S(2)}, u32[]{:S(2)}) collective-permute-start(f32[2,10,512]{2,1,0:T(8,128)} %get-tuple-element.81), channel_id=1, source_target_pairs={{8,0},{16,8},{24,16},{32,24},{40,32},{48,40},{56,48},{64,56},{72,6... | collective-permute-start | bytes 122888 | tf_op jit(solution)/shard_map/ppermute | solution.py:193
  62.6 2.5 %copy-start.22 = (s32[8,3]{0,1:T(4,128)S(1)}, s32[8,3]{0,1:T(4,128)}, u32[]{:S(2)}) copy-start(s32[8,3]{0,1:T(4,128)} %param.21) | copy-start | bytes 292
  62.6 4.9 %copy-start.9 = (bf16[3,2,8,512]{3,2,1,0:T(8,128)(2,1)S(1)}, bf16[3,2,8,512]{3,2,1,0:T(8,128)(2,1)}, u32[]{:S(2)}) copy-start(bf16[3,2,8,512]{3,2,1,0:T(8,128)(2,1)} %param.15) | copy-start | bytes 147460
  65.1 21.1 %copy-start.14 = (f32[2,1024]{1,0:T(2,128)S(1)}, f32[2,1024]{1,0:T(2,128)}, u32[]{:S(2)}) copy-start(f32[2,1024]{1,0:T(2,128)} %param.18) | copy-start | bytes 24580
  65.2 21.4 %copy-start.23 = (s32[8,3]{0,1:T(4,128)}, s32[8,3]{0,1:T(4,128)S(1)}, u32[]{:S(2)}) copy-start(s32[8,3]{0,1:T(4,128)S(1)} %fusion.168) | copy-start | bytes 292
  65.2 20.0 %collective-permute-start = (f32[2,10,512]{2,1,0:T(8,128)}, f32[2,10,512]{2,1,0:T(8,128)}, u32[]{:S(2)}, u32[]{:S(2)}) collective-permute-start(f32[2,10,512]{2,1,0:T(8,128)} %get-tuple-element.82), channel_id=1, source_target_pairs={{0,8},{8,16},{16,24},{24,32},{32,40},{40,48},{48,56},{56,64},{64,7... | collective-permute-start | bytes 122888 | tf_op jit(solution)/shard_map/ppermute | solution.py:192
  68.3 40.1 %copy-start.16 = (s32[8192]{0:T(1024)}, s32[8192]{0:T(1024)S(1)}, u32[]{:S(2)}) copy-start(s32[8192]{0:T(1024)S(1)} %get-tuple-element.68) | copy-start | bytes 98308
  68.3 16.8 %copy-start.15 = (bf16[2,8,511]{2,1,0:T(8,128)(2,1)S(1)}, bf16[2,8,511]{2,1,0:T(8,128)(2,1)}, u32[]{:S(2)}) copy-start(bf16[2,8,511]{2,1,0:T(8,128)(2,1)} %slice.211) | copy-start | bytes 49060
  68.4 2.2 %copy-start.6 = (f32[8,8192]{1,0:T(8,128)}, f32[8,8192]{1,0:T(8,128)S(1)}, u32[]{:S(2)}) copy-start(f32[8,8192]{1,0:T(8,128)S(1)} %get-tuple-element.62) | copy-start | bytes 786436
  71.3 27.2 %all-to-all-start.1 = ((f32[64,4,128]{2,1,0:T(4,128)}), f32[64,4,128]{2,1,0:T(4,128)S(1)}, u32[]{:S(2)}, u32[]{:S(2)}) async-start(f32[64,4,128]{2,1,0:T(4,128)} %maximum_bitcast_fusion), calls=%async_computation.1 | async-start | bytes 262144 | tf_op jit(solution)/shard_map/all_to_all | solution.py:185
  85.1 16.4 %copy-start.5 = (bf16[6,2,8,512]{3,2,1,0:T(8,128)(2,1)}, bf16[6,2,8,512]{3,2,1,0:T(8,128)(2,1)S(1)}, u32[]{:S(2)}) copy-start(bf16[6,2,8,512]{3,2,1,0:T(8,128)(2,1)S(1)} %bitcast_dynamic-update-slice_fusion.coef_ref) | copy-start | bytes 294916
  85.2 16.4 %copy-start.10 = (f32[2,10,512]{2,1,0:T(8,128)}, f32[2,10,512]{2,1,0:T(8,128)S(1)}, u32[]{:S(2)}) copy-start(f32[2,10,512]{2,1,0:T(8,128)S(1)} %collective-permute-done.1.above_ref) | copy-start | bytes 122884
  98.5 1.6 copy-start.2
  100.1 2.1 %copy-start.1 = (bf16[8,128,128]{2,1,0:T(8,128)(2,1)S(1)}, bf16[8,128,128]{2,1,0:T(8,128)(2,1)}, u32[]{:S(2)}) copy-start(bf16[8,128,128]{2,1,0:T(8,128)(2,1)} %param.20) | copy-start | bytes 786436
  105.8 2.6 %copy-start.7 = (f32[8,8192]{1,0:T(8,128)S(1)}, f32[8,8192]{1,0:T(8,128)}, u32[]{:S(2)}) copy-start(f32[8,8192]{1,0:T(8,128)} %copy-done.6) | copy-start | bytes 786436
  111.3 39.2 %all-to-all-start.2 = ((f32[64,4,128]{2,1,0:T(4,128)}), f32[64,4,128]{2,1,0:T(4,128)S(1)}, u32[]{:S(2)}, u32[]{:S(2)}) async-start(f32[64,4,128]{2,1,0:T(4,128)} %maximum_bitcast_fusion.1), calls=%async_computation.2 | async-start | bytes 262144 | tf_op jit(solution)/shard_map/all_to_all | solution.py:185
  118.5 28.7 %collective-permute-start.6 = (f32[2,10,512]{2,1,0:T(8,128)}, f32[2,10,512]{2,1,0:T(8,128)S(1)}, u32[]{:S(2)}, u32[]{:S(2)}) collective-permute-start(f32[2,10,512]{2,1,0:T(8,128)} %get-tuple-element.17), channel_id=1, source_target_pairs={{0,8},{8,16},{16,24},{24,32},{32,40},{40,48},{48,56},{56,64},{64,7... | collective-permute-start | bytes 122888 | tf_op jit(solution)/shard_map/ppermute | solution.py:192
  120.5 27.3 %collective-permute-start.7 = (f32[2,10,512]{2,1,0:T(8,128)}, f32[2,10,512]{2,1,0:T(8,128)}, u32[]{:S(2)}, u32[]{:S(2)}) collective-permute-start(f32[2,10,512]{2,1,0:T(8,128)} %get-tuple-element.18), channel_id=1, source_target_pairs={{8,0},{16,8},{24,16},{32,24},{40,32},{48,40},{56,48},{64,56},{72,6... | collective-permute-start | bytes 122888 | tf_op jit(solution)/shard_map/ppermute | solution.py:193
  131.6 26.5 %collective-permute-start.8 = (f32[2,2,512]{2,1,0:T(2,128)}, f32[2,2,512]{2,1,0:T(2,128)}, u32[]{:S(2)}, u32[]{:S(2)}) collective-permute-start(f32[2,2,512]{2,1,0:T(2,128)} %get-tuple-element.19), channel_id=1, source_target_pairs={{0,1},{1,2},{2,3},{3,4},{4,5},{5,6},{6,7},{8,9},{9,10},{10,11},{11... | collective-permute-start | bytes 24584 | tf_op jit(solution)/shard_map/ppermute | solution.py:194
  137.3 20.7 %collective-permute-start.9 = (f32[2,2,512]{2,1,0:T(2,128)}, f32[2,2,512]{2,1,0:T(2,128)}, u32[]{:S(2)}, u32[]{:S(2)}) collective-permute-start(f32[2,2,512]{2,1,0:T(2,128)} %get-tuple-element.20), channel_id=1, source_target_pairs={{1,0},{2,1},{3,2},{4,3},{5,4},{6,5},{7,6},{9,8},{10,9},{11,10},{12... | collective-permute-start | bytes 24584 | tf_op jit(solution)/shard_map/ppermute | solution.py:195
  147.2 7.9 %copy-start.11 = (f32[2,10,512]{2,1,0:T(8,128)}, f32[2,10,512]{2,1,0:T(8,128)S(1)}, u32[]{:S(2)}) copy-start(f32[2,10,512]{2,1,0:T(8,128)S(1)} %collective-permute-done.6.below_ref) | copy-start | bytes 122884
  150.5 2.6 %copy-start.8 = (f32[8,8192]{1,0:T(8,128)S(1)}, f32[8,8192]{1,0:T(8,128)}, u32[]{:S(2)}) copy-start(f32[8,8192]{1,0:T(8,128)} %copy-done.6) | copy-start | bytes 786436
  150.5 2.6 %copy-start.17 = (s32[8192]{0:T(1024)S(1)}, s32[8192]{0:T(1024)}, u32[]{:S(2)}) copy-start(s32[8192]{0:T(1024)} %copy-done.16) | copy-start | bytes 98308
  150.7 4.6 %copy-start.3 = (bf16[64,8192]{1,0:T(8,128)(2,1)S(1)}, bf16[64,8192]{1,0:T(8,128)(2,1)}, u32[]{:S(2)}) copy-start(bf16[64,8192]{1,0:T(8,128)(2,1)} %get-tuple-element.66) | copy-start | bytes 3145732
  160.8 10.9 %copy-start.26 = (f32[2,10,512]{2,1,0:T(8,128)S(1)}, f32[2,10,512]{2,1,0:T(8,128)}, u32[]{:S(2)}) copy-start(f32[2,10,512]{2,1,0:T(8,128)} %get-tuple-element.24) | copy-start | bytes 122884
  160.8 37.5 %copy-start.24 = (s32[8,3]{0,1:T(4,128)S(1)}, s32[8,3]{0,1:T(4,128)}, u32[]{:S(2)}) copy-start(s32[8,3]{0,1:T(4,128)} %copy-done.23) | copy-start | bytes 292
  163.3 35.8 %copy-start.18 = (s32[8192]{0:T(1024)S(1)}, s32[8192]{0:T(1024)}, u32[]{:S(2)}) copy-start(s32[8192]{0:T(1024)} %copy-done.16) | copy-start | bytes 98308
  163.3 37.2 %copy-start.4 = (bf16[64,8192]{1,0:T(8,128)(2,1)S(1)}, bf16[64,8192]{1,0:T(8,128)(2,1)}, u32[]{:S(2)}) copy-start(bf16[64,8192]{1,0:T(8,128)(2,1)} %get-tuple-element.66) | copy-start | bytes 3145732
  164.1 34.8 %all-to-all-start.3 = ((f32[64,4,128]{2,1,0:T(4,128)}), f32[64,4,128]{2,1,0:T(4,128)S(1)}, u32[]{:S(2)}, u32[]{:S(2)}) async-start(f32[64,4,128]{2,1,0:T(4,128)} %maximum_bitcast_fusion.2), calls=%async_computation.3 | async-start | bytes 262144 | tf_op jit(solution)/shard_map/all_to_all | solution.py:185
  169.7 28.6 %collective-permute-start.10 = (f32[2,10,512]{2,1,0:T(8,128)}, f32[2,10,512]{2,1,0:T(8,128)S(1)}, u32[]{:S(2)}, u32[]{:S(2)}) collective-permute-start(f32[2,10,512]{2,1,0:T(8,128)} %get-tuple-element.23), channel_id=1, source_target_pairs={{0,8},{8,16},{16,24},{24,32},{32,40},{40,48},{48,56},{56,64},{64,7... | collective-permute-start | bytes 122888 | tf_op jit(solution)/shard_map/ppermute | solution.py:192
  171.7 26.6 %collective-permute-start.11 = (f32[2,10,512]{2,1,0:T(8,128)S(1)}, f32[2,10,512]{2,1,0:T(8,128)S(1)}, u32[]{:S(2)}, u32[]{:S(2)}) collective-permute-start(f32[2,10,512]{2,1,0:T(8,128)S(1)} %copy-done.26), channel_id=1, source_target_pairs={{8,0},{16,8},{24,16},{32,24},{40,32},{48,40},{56,48},{64,56},{72,6... | collective-permute-start | bytes 122888 | tf_op jit(solution)/shard_map/ppermute | solution.py:193
  182.8 21.3 %collective-permute-start.12 = (f32[2,2,512]{2,1,0:T(2,128)}, f32[2,2,512]{2,1,0:T(2,128)S(1)}, u32[]{:S(2)}, u32[]{:S(2)}) collective-permute-start(f32[2,2,512]{2,1,0:T(2,128)} %get-tuple-element.25), channel_id=1, source_target_pairs={{0,1},{1,2},{2,3},{3,4},{4,5},{5,6},{6,7},{8,9},{9,10},{10,11},{11... | collective-permute-start | bytes 24584 | tf_op jit(solution)/shard_map/ppermute | solution.py:194
  188.0 16.1 %collective-permute-start.13 = (f32[2,2,512]{2,1,0:T(2,128)}, f32[2,2,512]{2,1,0:T(2,128)S(1)}, u32[]{:S(2)}, u32[]{:S(2)}) collective-permute-start(f32[2,2,512]{2,1,0:T(2,128)} %get-tuple-element.26), channel_id=1, source_target_pairs={{1,0},{2,1},{3,2},{4,3},{5,4},{6,5},{7,6},{9,8},{10,9},{11,10},{12... | collective-permute-start | bytes 24584 | tf_op jit(solution)/shard_map/ppermute | solution.py:195
  198.3 3.7 %copy-start.12 = (f32[2,10,512]{2,1,0:T(8,128)}, f32[2,10,512]{2,1,0:T(8,128)S(1)}, u32[]{:S(2)}) copy-start(f32[2,10,512]{2,1,0:T(8,128)S(1)} %collective-permute-done.10.below_ref) | copy-start | bytes 122884
  198.3 3.7 %copy-start.13 = (f32[2,10,512]{2,1,0:T(8,128)}, f32[2,10,512]{2,1,0:T(8,128)S(1)}, u32[]{:S(2)}) copy-start(f32[2,10,512]{2,1,0:T(8,128)S(1)} %collective-permute-done.11.above_ref) | copy-start | bytes 122884
  204.1 0.6 copy-start.20
  204.1 0.6 copy-start.21

commit v7 on v6

--- a/solution.py
+++ b/solution.py
@@ -23,9 +23,12 @@
 
 
 def pick_values(row_onehot, col_mask, table):
-    fields = table.shape[0]
     high, low = split_bf16(table)
-    parts = jnp.concatenate([high, low], 0)
+    return pick_parts(row_onehot, col_mask, jnp.concatenate([high, low], 0))
+
+
+def pick_parts(row_onehot, col_mask, parts):
+    fields = parts.shape[0] // 2
     by_row = jnp.einsum("kc,grc->grk", col_mask, parts, preferred_element_type=jnp.float32)
     picked = jnp.sum(by_row * row_onehot.astype(jnp.float32)[None], axis=1)
     return picked[:fields] + picked[fields:]
@@ -44,7 +47,7 @@
     rock_ref, source_ref, leak_ref, below_ref, above_ref, left_ref, right_ref, coef_ref, inv_ref,
     fracture_ref, out_ref, low_ref, high_ref, first_ref, last_ref, table_ref,
 ):
-    depth, rows, lanes = rock_ref.shape[1:]
+    fields, depth, rows, lanes = rock_ref.shape
     tiles = leak_ref.shape[2]
     row = lax.broadcasted_iota(jnp.int32, (rows, lanes), 0)
     lane = lax.broadcasted_iota(jnp.int32, (rows, lanes), 1)
@@ -67,8 +70,11 @@
         for f in range(2):
             value = inv[2 * f] * rhs[0] + inv[2 * f + 1] * rhs[1]
             out_ref[f, z] = value
+            high = value.astype(jnp.bfloat16)
+            low = (value - high.astype(jnp.float32)).astype(jnp.bfloat16)
             for j in range(tiles):
-                table_ref[f, z, j] = value[:, j * 128 : (j + 1) * 128]
+                table_ref[f, z, j] = high[:, j * 128 : (j + 1) * 128]
+                table_ref[fields + f, z, j] = low[:, j * 128 : (j + 1) * 128]
             first_ref[f, z] = value[0]
             last_ref[f, z] = value[rows - 1]
             if z == 0:
@@ -91,7 +97,7 @@
             jax.ShapeDtypeStruct((fields, halo_rows, lanes), jnp.float32),
             jax.ShapeDtypeStruct((fields, depth, lanes), jnp.float32),
             jax.ShapeDtypeStruct((fields, depth, lanes), jnp.float32),
-            jax.ShapeDtypeStruct(leak.shape, jnp.float32),
+            jax.ShapeDtypeStruct((2 * fields,) + leak.shape[1:], jnp.bfloat16),
         ),
         in_specs=[vmem] * 10,
         out_specs=(vmem,) * 6,
@@ -168,6 +174,8 @@
     rock_now = rock_state
     rock_table = rock_state.reshape(2, depth, rows, tiles, 128).transpose(0, 1, 3, 2, 4)
     rock_table = rock_table.reshape(2, cell_rows, 128)
+    rock_high_part, rock_low_part = split_bf16(rock_table)
+    rock_parts = jnp.concatenate([rock_high_part, rock_low_part], 0)
     fracture_start = fracture_state.astype(jnp.bfloat16).astype(jnp.float32)
     fracture_start = fracture_start.reshape(2, -1, rock_state.shape[-1])
     rock_low = jnp.concatenate([rock_now[:, 0], fracture_start], 1)
@@ -177,7 +185,7 @@
     source_blocks = fracture_source.reshape(2, blocks, segment_width)
     layer_rows = rock_now.shape[2]
     for sweep_index in range(ITERS):
-        rock_picked = pick_values(cell_row_onehot, cell_col_mask, rock_table)
+        rock_picked = pick_parts(cell_row_onehot, cell_col_mask, rock_parts)
         send_rock = slot_weight_flat[None] * rock_picked
         fracture_table = fracture_now.reshape(2, blocks, segment_width)
         send_fracture = pick_values(segment_row_onehot, segment_col_mask, fracture_table)
@@ -232,7 +240,7 @@
             cell_inverse,
             fracture_next.astype(jnp.bfloat16).astype(jnp.float32).reshape(fracture_wide.shape),
         )
-        rock_table = rock_table.reshape(2, cell_rows, 128)
+        rock_parts = rock_table.reshape(4, cell_rows, 128)
         fracture_now = fracture_next
     return (rock_now, fracture_now)
 

time: 208 us -> 208 us (level)
  no operation moved by 1% of the time
where the time goes in v7:
time: 208 us; the launch traced here: 207 us
  starting transfers between devices  138 us (66%)
  matrix products  28.1 us (14%)
  waiting for transfers between devices  12 us (6%)
  local copies, waits for them, and re-layouts  11.2 us (5%)
  other arithmetic  10.3 us (5%)
  Pallas kernels  5.69 us (3%)
    ppermute x3, starting transfers between devices, shards(): from_right = lax.ppermute(rock_first, 'plane', backward_plane)  29.5 us
    all_to_all x3, starting transfers between devices, shards(): lax.all_to_all(send.transpose(1, 0, 2), 'slab', split_axis=0, concat_axis...  26.6 us
    ppermute x3, starting transfers between devices, shards(): from_above = lax.ppermute(rock_low, 'slab', backward_slab)  24.1 us
    ppermute x2, starting transfers between devices, shifted(): lax.ppermute(value, axis, [(source, source + steps) for source in range(f...  17.9 us
    ppermute x3, starting transfers between devices, shards(): from_left = lax.ppermute(rock_last, 'plane', forward_plane)  17 us
    all_to_all x1, starting transfers between devices, shards(): lax.all_to_all(contact_segment[0], 'slab', split_axis=0, concat_axis=0, t...  16.3 us
    dot_general x6, matrix products, pick_parts(): jnp.einsum('kc,grc->grk', col_mask, parts, preferred_element_type=jnp.flo...  15.4 us
    all_to_all x3, waiting for transfers between devices, shards(): lax.all_to_all(send.transpose(1, 0, 2), 'slab', split_axis=0, concat_axis...  11.9 us
  transfers between devices with their start and end apart: 18, of which 1 were waited for; matrix products, arithmetic and copies ran while one was open for 19% of the time, Pallas kernels for 0%

profile of v7, /device:TPU:14, one launch (start us, length us, event | category | flops | bytes accessed | tf_op | source)
XLA Modules:
  0.0 206.6 jit_solution(16598561856705987197)
XLA Ops:
  0.7 16.3 %all-to-all-start = ((s32[64,1,128]{2,1,0:T(1,128)}), s32[64,1,128]{2,1,0:T(1,128)S(1)}, u32[]{:S(2)}, u32[]{:S(2)}) async-start(s32[64,1,128]{2,1,0:T(1,128)} %bitcast.262), calls=%async_computation | async-start | bytes 65536 | tf_op jit(solution)/shard_map/all_to_all | solution.py:135
  17.0 0.7 slice_bitcast_fusion.12
  17.7 8.5 %collective-permute-start.5 = (bf16[2,1,512]{2,1,0:T(2,128)(2,1)S(1)}, bf16[2,1,512]{2,1,0:T(2,128)(2,1)S(1)}, u32[]{:S(2)}, u32[]{:S(2)}) collective-permute-start(bf16[2,1,512]{2,1,0:T(2,128)(2,1)S(1)} %slice_bitcast_fusion.12), channel_id=1, source_target_pairs={{1,0},{2,1},{3,2},{4,3},{5,4},{6,5},{7,6},{9,8},{10,9},{11,10},{12... | collective-permute-start | bytes 6152 | tf_op jit(solution)/shard_map/ppermute | solution.py:17
  26.2 0.7 slice_bitcast_fusion.11
  26.9 9.4 %collective-permute-start.4 = (bf16[1,8,512]{2,1,0:T(8,128)(2,1)S(1)}, bf16[1,8,512]{2,1,0:T(8,128)(2,1)S(1)}, u32[]{:S(2)}, u32[]{:S(2)}) collective-permute-start(bf16[1,8,512]{2,1,0:T(8,128)(2,1)S(1)} %get-tuple-element.56), channel_id=1, source_target_pairs={{8,0},{16,8},{24,16},{32,24},{40,32},{48,40},{56,48},{64,56},{72,6... | collective-permute-start | bytes 24584 | tf_op jit(solution)/shard_map/ppermute | solution.py:17
  36.3 0.9 fusion.170
  37.9 6.1 %collective-permute-start.2 = (f32[2,2,512]{2,1,0:T(2,128)}, f32[2,2,512]{2,1,0:T(2,128)}, u32[]{:S(2)}, u32[]{:S(2)}) collective-permute-start(f32[2,2,512]{2,1,0:T(2,128)} %bitcast.248), channel_id=1, source_target_pairs={{0,1},{1,2},{2,3},{3,4},{4,5},{5,6},{6,7},{8,9},{9,10},{10,11},{11... | collective-permute-start | bytes 24584 | tf_op jit(solution)/shard_map/ppermute | solution.py:202
  44.5 9.4 %collective-permute-start.3 = (f32[2,2,512]{2,1,0:T(2,128)}, f32[2,2,512]{2,1,0:T(2,128)}, u32[]{:S(2)}, u32[]{:S(2)}) collective-permute-start(f32[2,2,512]{2,1,0:T(2,128)} %bitcast.247), channel_id=1, source_target_pairs={{1,0},{2,1},{3,2},{4,3},{5,4},{6,5},{7,6},{9,8},{10,9},{11,10},{12... | collective-permute-start | bytes 24584 | tf_op jit(solution)/shard_map/ppermute | solution.py:203
  53.9 0.8 slice_bitcast_fusion.6
  56.1 2.0 collective-permute-start.1
  58.1 0.7 slice_dynamic-update-slice_fusion
  59.5 0.8 add_select_fusion.6
  60.3 0.9 reduce-precision_convert_fusion
  61.2 1.3 fusion.76
  62.6 2.5 %fusion.23 = f32[4,8192]{1,0:T(4,128)S(1)} fusion(f32[64,8192]{1,0:T(8,128)S(1)} %get-tuple-element.61, s32[8192]{0:T(1024)S(1)} %get-tuple-element.59, bf16[2,64,128]{2,1,0:T(8,128)(2,1)S(1)} %get-tuple-element.51, bf16[2,64,128]{2,1,0:T(8,128)(2,1)S(1)} %get-tuple-element.50), kind=kOutput, calls=%fused_computation.19 | convolution fusion | flops 542113792 | bytes 2326528 | tf_op jit(solution)/shard_map/kc,grc->grk/dot_general | solution.py:32
  65.2 2.3 %collective-permute-start = (f32[2,10,512]{2,1,0:T(8,128)}, f32[2,10,512]{2,1,0:T(8,128)}, u32[]{:S(2)}, u32[]{:S(2)}) collective-permute-start(f32[2,10,512]{2,1,0:T(8,128)} %get-tuple-element.78), channel_id=1, source_target_pairs={{0,8},{8,16},{16,24},{24,32},{32,40},{40,48},{48,56},{56,64},{64,7... | collective-permute-start | bytes 122888 | tf_op jit(solution)/shard_map/ppermute | solution.py:200
  68.4 2.1 fusion.51
  70.6 0.7 maximum_bitcast_fusion
  71.3 13.8 %all-to-all-start.1 = ((f32[64,4,128]{2,1,0:T(4,128)}), f32[64,4,128]{2,1,0:T(4,128)S(1)}, u32[]{:S(2)}, u32[]{:S(2)}) async-start(f32[64,4,128]{2,1,0:T(4,128)} %maximum_bitcast_fusion), calls=%async_computation.1 | async-start | bytes 262144 | tf_op jit(solution)/shard_map/all_to_all | solution.py:193
  85.2 0.8 slice.322
  86.6 11.9 %all-to-all-done.1 = f32[64,4,128]{2,1,0:T(4,128)S(1)} async-done(((f32[64,4,128]{2,1,0:T(4,128)}), f32[64,4,128]{2,1,0:T(4,128)S(1)}, u32[]{:S(2)}, u32[]{:S(2)}) %all-to-all-start.1) | async-done | bytes 131104 | tf_op jit(solution)/shard_map/all_to_all | solution.py:193
  98.7 1.3 fusion.20
  100.1 1.5 fusion.4
  103.1 1.9 shard_map.140
  105.0 3.4 %fusion.26 = f32[4,8192]{1,0:T(4,128)S(1)} fusion(f32[64,8192]{1,0:T(8,128)S(1)} %get-tuple-element.61, bf16[4,64,128]{2,1,0:T(8,128)(2,1)} %bitcast.261, s32[8192]{0:T(1024)S(1)} %get-tuple-element.59), kind=kOutput, calls=%fused_computation.20 | convolution fusion | flops 542081024 | bytes 2326528 | tf_op jit(solution)/shard_map/kc,grc->grk/dot_general | solution.py:32
  108.4 2.1 fusion.54
  110.5 0.7 maximum_bitcast_fusion.1
  111.3 7.2 %all-to-all-start.2 = ((f32[64,4,128]{2,1,0:T(4,128)}), f32[64,4,128]{2,1,0:T(4,128)S(1)}, u32[]{:S(2)}, u32[]{:S(2)}) async-start(f32[64,4,128]{2,1,0:T(4,128)} %maximum_bitcast_fusion.1), calls=%async_computation.2 | async-start | bytes 262144 | tf_op jit(solution)/shard_map/all_to_all | solution.py:193
  118.5 2.0 collective-permute-start.6
  120.5 11.0 %collective-permute-start.7 = (f32[2,10,512]{2,1,0:T(8,128)}, f32[2,10,512]{2,1,0:T(8,128)}, u32[]{:S(2)}, u32[]{:S(2)}) collective-permute-start(f32[2,10,512]{2,1,0:T(8,128)} %get-tuple-element.18), channel_id=1, source_target_pairs={{8,0},{16,8},{24,16},{32,24},{40,32},{48,40},{56,48},{64,56},{72,6... | collective-permute-start | bytes 122888 | tf_op jit(solution)/shard_map/ppermute | solution.py:201
  131.6 5.7 %collective-permute-start.8 = (f32[2,2,512]{2,1,0:T(2,128)}, f32[2,2,512]{2,1,0:T(2,128)}, u32[]{:S(2)}, u32[]{:S(2)}) collective-permute-start(f32[2,2,512]{2,1,0:T(2,128)} %get-tuple-element.19), channel_id=1, source_target_pairs={{0,1},{1,2},{2,3},{3,4},{4,5},{5,6},{6,7},{8,9},{9,10},{10,11},{11... | collective-permute-start | bytes 24584 | tf_op jit(solution)/shard_map/ppermute | solution.py:202
  137.3 9.9 %collective-permute-start.9 = (f32[2,2,512]{2,1,0:T(2,128)}, f32[2,2,512]{2,1,0:T(2,128)}, u32[]{:S(2)}, u32[]{:S(2)}) collective-permute-start(f32[2,2,512]{2,1,0:T(2,128)} %get-tuple-element.20), channel_id=1, source_target_pairs={{1,0},{2,1},{3,2},{4,3},{5,4},{6,5},{7,6},{9,8},{10,9},{11,10},{12... | collective-permute-start | bytes 24584 | tf_op jit(solution)/shard_map/ppermute | solution.py:203
  147.9 0.8 slice.319
  149.3 0.9 fusion.61
  150.7 2.1 %fusion.17 = f32[4,8,128]{2,1,0:T(8,128)S(1)} fusion(s32[8192]{0:T(1024)} %copy-done.16, bf16[4,8192]{1,0:T(4,128)(2,1)S(1)} %pad_maximum_fusion.5, bf16[8,8192]{1,0:T(8,128)(2,1)S(1)} %get-tuple-element.57), kind=kOutput, calls=%fused_computation.17 | convolution fusion | flops 68419584 | bytes 245760 | tf_op jit(solution)/shard_map/grk,kc->grc/dot_general | solution.py:42
  153.1 2.1 fusion.57
  155.4 1.5 fusion.2
  158.1 1.9 shard_map.141
  160.0 3.3 %fusion.29 = f32[4,8192]{1,0:T(4,128)S(1)} fusion(f32[64,8192]{1,0:T(8,128)S(1)} %get-tuple-element.61, bf16[4,64,128]{2,1,0:T(8,128)(2,1)} %bitcast.260, s32[8192]{0:T(1024)S(1)} %get-tuple-element.59), kind=kOutput, calls=%fused_computation.21 | convolution fusion | flops 542081024 | bytes 2326528 | tf_op jit(solution)/shard_map/kc,grc->grk/dot_general | solution.py:32
  164.2 5.6 %all-to-all-start.3 = ((f32[64,4,128]{2,1,0:T(4,128)}), f32[64,4,128]{2,1,0:T(4,128)S(1)}, u32[]{:S(2)}, u32[]{:S(2)}) async-start(f32[64,4,128]{2,1,0:T(4,128)} %maximum_bitcast_fusion.2), calls=%async_computation.3 | async-start | bytes 262144 | tf_op jit(solution)/shard_map/all_to_all | solution.py:193
  169.7 2.0 collective-permute-start.10
  171.8 11.0 %collective-permute-start.11 = (f32[2,10,512]{2,1,0:T(8,128)S(1)}, f32[2,10,512]{2,1,0:T(8,128)S(1)}, u32[]{:S(2)}, u32[]{:S(2)}) collective-permute-start(f32[2,10,512]{2,1,0:T(8,128)S(1)} %copy-done.26), channel_id=1, source_target_pairs={{8,0},{16,8},{24,16},{32,24},{40,32},{48,40},{56,48},{64,56},{72,6... | collective-permute-start | bytes 122888 | tf_op jit(solution)/shard_map/ppermute | solution.py:201
  182.8 5.2 %collective-permute-start.12 = (f32[2,2,512]{2,1,0:T(2,128)S(1)}, f32[2,2,512]{2,1,0:T(2,128)S(1)}, u32[]{:S(2)}, u32[]{:S(2)}) collective-permute-start(f32[2,2,512]{2,1,0:T(2,128)S(1)} %copy-done.28), channel_id=1, source_target_pairs={{0,1},{1,2},{2,3},{3,4},{4,5},{5,6},{6,7},{8,9},{9,10},{10,11},{11... | collective-permute-start | bytes 24584 | tf_op jit(solution)/shard_map/ppermute | solution.py:202
  188.1 10.2 %collective-permute-start.13 = (f32[2,2,512]{2,1,0:T(2,128)S(1)}, f32[2,2,512]{2,1,0:T(2,128)S(1)}, u32[]{:S(2)}, u32[]{:S(2)}) collective-permute-start(f32[2,2,512]{2,1,0:T(2,128)S(1)} %copy-done.27), channel_id=1, source_target_pairs={{1,0},{2,1},{3,2},{4,3},{5,4},{6,5},{7,6},{9,8},{10,9},{11,10},{12... | collective-permute-start | bytes 24584 | tf_op jit(solution)/shard_map/ppermute | solution.py:203
  199.2 1.3 fusion.14
  200.6 1.5 fusion
  202.0 0.8 fusion.149
  204.7 1.9 shard_map.142
  (139 shorter events, 13.7 us)
Async XLA Ops:
  0.6 85.6 %copy-start = (bf16[8,3,128,128]{3,2,1,0:T(8,128)(2,1)S(1)}, bf16[8,3,128,128]{3,2,1,0:T(8,128)(2,1)}, u32[]{:S(2)}) copy-start(bf16[8,3,128,128]{3,2,1,0:T(8,128)(2,1)} %param.19) | copy-start | bytes 2359300
  0.6 61.9 %copy-start.25 = (s32[1,64]{1,0:T(1,128)S(1)}, s32[1,64]{1,0:T(1,128)}, u32[]{:S(2)}) copy-start(s32[1,64]{1,0:T(1,128)} %param.25) | copy-start | bytes 772
  0.7 61.9 %copy-start.19 = (f32[1,64,128]{2,1,0:T(8,128)S(1)}, f32[1,64,128]{2,1,0:T(8,128)}, u32[]{:S(2)}) copy-start(f32[1,64,128]{2,1,0:T(8,128)} %param.24) | copy-start | bytes 98308
  0.7 67.6 %all-to-all-start = ((s32[64,1,128]{2,1,0:T(1,128)}), s32[64,1,128]{2,1,0:T(1,128)S(1)}, u32[]{:S(2)}, u32[]{:S(2)}) async-start(s32[64,1,128]{2,1,0:T(1,128)} %bitcast.262), calls=%async_computation | async-start | bytes 65536 | tf_op jit(solution)/shard_map/all_to_all | solution.py:135
  17.7 50.5 %collective-permute-start.5 = (bf16[2,1,512]{2,1,0:T(2,128)(2,1)S(1)}, bf16[2,1,512]{2,1,0:T(2,128)(2,1)S(1)}, u32[]{:S(2)}, u32[]{:S(2)}) collective-permute-start(bf16[2,1,512]{2,1,0:T(2,128)(2,1)S(1)} %slice_bitcast_fusion.12), channel_id=1, source_target_pairs={{1,0},{2,1},{3,2},{4,3},{5,4},{6,5},{7,6},{9,8},{10,9},{11,10},{12... | collective-permute-start | bytes 6152 | tf_op jit(solution)/shard_map/ppermute | solution.py:17
  26.9 38.3 %collective-permute-start.4 = (bf16[1,8,512]{2,1,0:T(8,128)(2,1)S(1)}, bf16[1,8,512]{2,1,0:T(8,128)(2,1)S(1)}, u32[]{:S(2)}, u32[]{:S(2)}) collective-permute-start(bf16[1,8,512]{2,1,0:T(8,128)(2,1)S(1)} %get-tuple-element.56), channel_id=1, source_target_pairs={{8,0},{16,8},{24,16},{32,24},{40,32},{48,40},{56,48},{64,56},{72,6... | collective-permute-start | bytes 24584 | tf_op jit(solution)/shard_map/ppermute | solution.py:17
  37.9 65.2 %collective-permute-start.2 = (f32[2,2,512]{2,1,0:T(2,128)}, f32[2,2,512]{2,1,0:T(2,128)}, u32[]{:S(2)}, u32[]{:S(2)}) collective-permute-start(f32[2,2,512]{2,1,0:T(2,128)} %bitcast.248), channel_id=1, source_target_pairs={{0,1},{1,2},{2,3},{3,4},{4,5},{5,6},{6,7},{8,9},{9,10},{10,11},{11... | collective-permute-start | bytes 24584 | tf_op jit(solution)/shard_map/ppermute | solution.py:202
  44.5 58.5 %collective-permute-start.3 = (f32[2,2,512]{2,1,0:T(2,128)}, f32[2,2,512]{2,1,0:T(2,128)}, u32[]{:S(2)}, u32[]{:S(2)}) collective-permute-start(f32[2,2,512]{2,1,0:T(2,128)} %bitcast.247), channel_id=1, source_target_pairs={{1,0},{2,1},{3,2},{4,3},{5,4},{6,5},{7,6},{9,8},{10,9},{11,10},{12... | collective-permute-start | bytes 24584 | tf_op jit(solution)/shard_map/ppermute | solution.py:203
  56.1 29.1 %collective-permute-start.1 = (f32[2,10,512]{2,1,0:T(8,128)}, f32[2,10,512]{2,1,0:T(8,128)S(1)}, u32[]{:S(2)}, u32[]{:S(2)}) collective-permute-start(f32[2,10,512]{2,1,0:T(8,128)} %get-tuple-element.77), channel_id=1, source_target_pairs={{8,0},{16,8},{24,16},{32,24},{40,32},{48,40},{56,48},{64,56},{72,6... | collective-permute-start | bytes 122888 | tf_op jit(solution)/shard_map/ppermute | solution.py:201
  62.6 2.5 %copy-start.22 = (s32[8,3]{0,1:T(4,128)S(1)}, s32[8,3]{0,1:T(4,128)}, u32[]{:S(2)}) copy-start(s32[8,3]{0,1:T(4,128)} %param.21) | copy-start | bytes 292
  62.6 4.9 %copy-start.9 = (bf16[3,2,8,512]{3,2,1,0:T(8,128)(2,1)S(1)}, bf16[3,2,8,512]{3,2,1,0:T(8,128)(2,1)}, u32[]{:S(2)}) copy-start(bf16[3,2,8,512]{3,2,1,0:T(8,128)(2,1)} %param.15) | copy-start | bytes 147460
  65.1 21.1 %copy-start.14 = (f32[2,1024]{1,0:T(2,128)S(1)}, f32[2,1024]{1,0:T(2,128)}, u32[]{:S(2)}) copy-start(f32[2,1024]{1,0:T(2,128)} %param.18) | copy-start | bytes 24580
  65.1 21.4 %copy-start.23 = (s32[8,3]{0,1:T(4,128)}, s32[8,3]{0,1:T(4,128)S(1)}, u32[]{:S(2)}) copy-start(s32[8,3]{0,1:T(4,128)S(1)} %fusion.160) | copy-start | bytes 292
  65.2 20.0 %collective-permute-start = (f32[2,10,512]{2,1,0:T(8,128)}, f32[2,10,512]{2,1,0:T(8,128)}, u32[]{:S(2)}, u32[]{:S(2)}) collective-permute-start(f32[2,10,512]{2,1,0:T(8,128)} %get-tuple-element.78), channel_id=1, source_target_pairs={{0,8},{8,16},{16,24},{24,32},{32,40},{40,48},{48,56},{56,64},{64,7... | collective-permute-start | bytes 122888 | tf_op jit(solution)/shard_map/ppermute | solution.py:200
  68.3 40.1 %copy-start.16 = (s32[8192]{0:T(1024)}, s32[8192]{0:T(1024)S(1)}, u32[]{:S(2)}) copy-start(s32[8192]{0:T(1024)S(1)} %get-tuple-element.64) | copy-start | bytes 98308
  68.3 16.8 %copy-start.15 = (bf16[2,8,511]{2,1,0:T(8,128)(2,1)S(1)}, bf16[2,8,511]{2,1,0:T(8,128)(2,1)}, u32[]{:S(2)}) copy-start(bf16[2,8,511]{2,1,0:T(8,128)(2,1)} %slice.211) | copy-start | bytes 49060
  68.4 2.2 %copy-start.6 = (f32[8,8192]{1,0:T(8,128)}, f32[8,8192]{1,0:T(8,128)S(1)}, u32[]{:S(2)}) copy-start(f32[8,8192]{1,0:T(8,128)S(1)} %get-tuple-element.58) | copy-start | bytes 786436
  71.3 27.2 %all-to-all-start.1 = ((f32[64,4,128]{2,1,0:T(4,128)}), f32[64,4,128]{2,1,0:T(4,128)S(1)}, u32[]{:S(2)}, u32[]{:S(2)}) async-start(f32[64,4,128]{2,1,0:T(4,128)} %maximum_bitcast_fusion), calls=%async_computation.1 | async-start | bytes 262144 | tf_op jit(solution)/shard_map/all_to_all | solution.py:193
  85.1 16.4 %copy-start.5 = (bf16[6,2,8,512]{3,2,1,0:T(8,128)(2,1)}, bf16[6,2,8,512]{3,2,1,0:T(8,128)(2,1)S(1)}, u32[]{:S(2)}) copy-start(bf16[6,2,8,512]{3,2,1,0:T(8,128)(2,1)S(1)} %bitcast_dynamic-update-slice_fusion.coef_ref) | copy-start | bytes 294916
  85.2 16.4 %copy-start.10 = (f32[2,10,512]{2,1,0:T(8,128)}, f32[2,10,512]{2,1,0:T(8,128)S(1)}, u32[]{:S(2)}) copy-start(f32[2,10,512]{2,1,0:T(8,128)S(1)} %collective-permute-done.1.above_ref) | copy-start | bytes 122884
  98.5 1.6 copy-start.2
  100.0 2.1 %copy-start.1 = (bf16[8,128,128]{2,1,0:T(8,128)(2,1)S(1)}, bf16[8,128,128]{2,1,0:T(8,128)(2,1)}, u32[]{:S(2)}) copy-start(bf16[8,128,128]{2,1,0:T(8,128)(2,1)} %param.20) | copy-start | bytes 786436
  105.0 3.5 %copy-start.7 = (f32[8,8192]{1,0:T(8,128)S(1)}, f32[8,8192]{1,0:T(8,128)}, u32[]{:S(2)}) copy-start(f32[8,8192]{1,0:T(8,128)} %copy-done.6) | copy-start | bytes 786436
  111.3 39.2 %all-to-all-start.2 = ((f32[64,4,128]{2,1,0:T(4,128)}), f32[64,4,128]{2,1,0:T(4,128)S(1)}, u32[]{:S(2)}, u32[]{:S(2)}) async-start(f32[64,4,128]{2,1,0:T(4,128)} %maximum_bitcast_fusion.1), calls=%async_computation.2 | async-start | bytes 262144 | tf_op jit(solution)/shard_map/all_to_all | solution.py:193
  118.5 28.7 %collective-permute-start.6 = (f32[2,10,512]{2,1,0:T(8,128)}, f32[2,10,512]{2,1,0:T(8,128)S(1)}, u32[]{:S(2)}, u32[]{:S(2)}) collective-permute-start(f32[2,10,512]{2,1,0:T(8,128)} %get-tuple-element.17), channel_id=1, source_target_pairs={{0,8},{8,16},{16,24},{24,32},{32,40},{40,48},{48,56},{56,64},{64,7... | collective-permute-start | bytes 122888 | tf_op jit(solution)/shard_map/ppermute | solution.py:200
  120.5 27.3 %collective-permute-start.7 = (f32[2,10,512]{2,1,0:T(8,128)}, f32[2,10,512]{2,1,0:T(8,128)}, u32[]{:S(2)}, u32[]{:S(2)}) collective-permute-start(f32[2,10,512]{2,1,0:T(8,128)} %get-tuple-element.18), channel_id=1, source_target_pairs={{8,0},{16,8},{24,16},{32,24},{40,32},{48,40},{56,48},{64,56},{72,6... | collective-permute-start | bytes 122888 | tf_op jit(solution)/shard_map/ppermute | solution.py:201
  131.6 26.5 %collective-permute-start.8 = (f32[2,2,512]{2,1,0:T(2,128)}, f32[2,2,512]{2,1,0:T(2,128)}, u32[]{:S(2)}, u32[]{:S(2)}) collective-permute-start(f32[2,2,512]{2,1,0:T(2,128)} %get-tuple-element.19), channel_id=1, source_target_pairs={{0,1},{1,2},{2,3},{3,4},{4,5},{5,6},{6,7},{8,9},{9,10},{10,11},{11... | collective-permute-start | bytes 24584 | tf_op jit(solution)/shard_map/ppermute | solution.py:202
  137.3 20.7 %collective-permute-start.9 = (f32[2,2,512]{2,1,0:T(2,128)}, f32[2,2,512]{2,1,0:T(2,128)}, u32[]{:S(2)}, u32[]{:S(2)}) collective-permute-start(f32[2,2,512]{2,1,0:T(2,128)} %get-tuple-element.20), channel_id=1, source_target_pairs={{1,0},{2,1},{3,2},{4,3},{5,4},{6,5},{7,6},{9,8},{10,9},{11,10},{12... | collective-permute-start | bytes 24584 | tf_op jit(solution)/shard_map/ppermute | solution.py:203
  147.3 7.9 %copy-start.11 = (f32[2,10,512]{2,1,0:T(8,128)}, f32[2,10,512]{2,1,0:T(8,128)S(1)}, u32[]{:S(2)}) copy-start(f32[2,10,512]{2,1,0:T(8,128)S(1)} %collective-permute-done.6.below_ref) | copy-start | bytes 122884
  150.5 2.6 %copy-start.8 = (f32[8,8192]{1,0:T(8,128)S(1)}, f32[8,8192]{1,0:T(8,128)}, u32[]{:S(2)}) copy-start(f32[8,8192]{1,0:T(8,128)} %copy-done.6) | copy-start | bytes 786436
  150.5 2.6 %copy-start.17 = (s32[8192]{0:T(1024)S(1)}, s32[8192]{0:T(1024)}, u32[]{:S(2)}) copy-start(s32[8192]{0:T(1024)} %copy-done.16) | copy-start | bytes 98308
  150.7 4.6 %copy-start.3 = (bf16[64,8192]{1,0:T(8,128)(2,1)S(1)}, bf16[64,8192]{1,0:T(8,128)(2,1)}, u32[]{:S(2)}) copy-start(bf16[64,8192]{1,0:T(8,128)(2,1)} %get-tuple-element.62) | copy-start | bytes 3145732
  160.0 11.8 %copy-start.26 = (f32[2,10,512]{2,1,0:T(8,128)S(1)}, f32[2,10,512]{2,1,0:T(8,128)}, u32[]{:S(2)}) copy-start(f32[2,10,512]{2,1,0:T(8,128)} %get-tuple-element.24) | copy-start | bytes 122884
  160.0 22.8 %copy-start.28 = (f32[2,2,512]{2,1,0:T(2,128)S(1)}, f32[2,2,512]{2,1,0:T(2,128)}, u32[]{:S(2)}) copy-start(f32[2,2,512]{2,1,0:T(2,128)} %get-tuple-element.25) | copy-start | bytes 24580
  160.0 28.1 %copy-start.27 = (f32[2,2,512]{2,1,0:T(2,128)S(1)}, f32[2,2,512]{2,1,0:T(2,128)}, u32[]{:S(2)}) copy-start(f32[2,2,512]{2,1,0:T(2,128)} %get-tuple-element.26) | copy-start | bytes 24580
  160.0 38.4 %copy-start.24 = (s32[8,3]{0,1:T(4,128)S(1)}, s32[8,3]{0,1:T(4,128)}, u32[]{:S(2)}) copy-start(s32[8,3]{0,1:T(4,128)} %copy-done.23) | copy-start | bytes 292
  163.4 35.8 %copy-start.18 = (s32[8192]{0:T(1024)S(1)}, s32[8192]{0:T(1024)}, u32[]{:S(2)}) copy-start(s32[8192]{0:T(1024)} %copy-done.16) | copy-start | bytes 98308
  163.4 37.2 %copy-start.4 = (bf16[64,8192]{1,0:T(8,128)(2,1)S(1)}, bf16[64,8192]{1,0:T(8,128)(2,1)}, u32[]{:S(2)}) copy-start(bf16[64,8192]{1,0:T(8,128)(2,1)} %get-tuple-element.62) | copy-start | bytes 3145732
  164.2 34.8 %all-to-all-start.3 = ((f32[64,4,128]{2,1,0:T(4,128)}), f32[64,4,128]{2,1,0:T(4,128)S(1)}, u32[]{:S(2)}, u32[]{:S(2)}) async-start(f32[64,4,128]{2,1,0:T(4,128)} %maximum_bitcast_fusion.2), calls=%async_computation.3 | async-start | bytes 262144 | tf_op jit(solution)/shard_map/all_to_all | solution.py:193
  169.7 28.6 %collective-permute-start.10 = (f32[2,10,512]{2,1,0:T(8,128)}, f32[2,10,512]{2,1,0:T(8,128)S(1)}, u32[]{:S(2)}, u32[]{:S(2)}) collective-permute-start(f32[2,10,512]{2,1,0:T(8,128)} %get-tuple-element.23), channel_id=1, source_target_pairs={{0,8},{8,16},{16,24},{24,32},{32,40},{40,48},{48,56},{56,64},{64,7... | collective-permute-start | bytes 122888 | tf_op jit(solution)/shard_map/ppermute | solution.py:200
  171.8 26.6 %collective-permute-start.11 = (f32[2,10,512]{2,1,0:T(8,128)S(1)}, f32[2,10,512]{2,1,0:T(8,128)S(1)}, u32[]{:S(2)}, u32[]{:S(2)}) collective-permute-start(f32[2,10,512]{2,1,0:T(8,128)S(1)} %copy-done.26), channel_id=1, source_target_pairs={{8,0},{16,8},{24,16},{32,24},{40,32},{48,40},{56,48},{64,56},{72,6... | collective-permute-start | bytes 122888 | tf_op jit(solution)/shard_map/ppermute | solution.py:201
  182.8 21.3 %collective-permute-start.12 = (f32[2,2,512]{2,1,0:T(2,128)S(1)}, f32[2,2,512]{2,1,0:T(2,128)S(1)}, u32[]{:S(2)}, u32[]{:S(2)}) collective-permute-start(f32[2,2,512]{2,1,0:T(2,128)S(1)} %copy-done.28), channel_id=1, source_target_pairs={{0,1},{1,2},{2,3},{3,4},{4,5},{5,6},{6,7},{8,9},{9,10},{10,11},{11... | collective-permute-start | bytes 24584 | tf_op jit(solution)/shard_map/ppermute | solution.py:202
  188.1 16.1 %collective-permute-start.13 = (f32[2,2,512]{2,1,0:T(2,128)S(1)}, f32[2,2,512]{2,1,0:T(2,128)S(1)}, u32[]{:S(2)}, u32[]{:S(2)}) collective-permute-start(f32[2,2,512]{2,1,0:T(2,128)S(1)} %copy-done.27), channel_id=1, source_target_pairs={{1,0},{2,1},{3,2},{4,3},{5,4},{6,5},{7,6},{9,8},{10,9},{11,10},{12... | collective-permute-start | bytes 24584 | tf_op jit(solution)/shard_map/ppermute | solution.py:203
  198.3 3.7 %copy-start.12 = (f32[2,10,512]{2,1,0:T(8,128)}, f32[2,10,512]{2,1,0:T(8,128)S(1)}, u32[]{:S(2)}) copy-start(f32[2,10,512]{2,1,0:T(8,128)S(1)} %collective-permute-done.10.below_ref) | copy-start | bytes 122884
  198.4 3.7 %copy-start.13 = (f32[2,10,512]{2,1,0:T(8,128)}, f32[2,10,512]{2,1,0:T(8,128)S(1)}, u32[]{:S(2)}) copy-start(f32[2,10,512]{2,1,0:T(8,128)S(1)} %collective-permute-done.11.above_ref) | copy-start | bytes 122884
  204.1 0.6 copy-start.20
  204.2 0.6 copy-start.21

commit v8 on v7

--- a/solution.py
+++ b/solution.py
@@ -25,6 +25,11 @@
 def pick_values(row_onehot, col_mask, table):
     high, low = split_bf16(table)
     return pick_parts(row_onehot, col_mask, jnp.concatenate([high, low], 0))
+
+
+def pick_joined(row_onehot, col_mask, parts):
+    by_row = jnp.einsum("kc,frc->frk", col_mask, parts, preferred_element_type=jnp.float32)
+    return jnp.sum(by_row * row_onehot.astype(jnp.float32)[None], axis=1)
 
 
 def pick_parts(row_onehot, col_mask, parts):
@@ -47,7 +52,7 @@
     rock_ref, source_ref, leak_ref, below_ref, above_ref, left_ref, right_ref, coef_ref, inv_ref,
     fracture_ref, out_ref, low_ref, high_ref, first_ref, last_ref, table_ref,
 ):
-    fields, depth, rows, lanes = rock_ref.shape
+    _, depth, rows, lanes = rock_ref.shape
     tiles = leak_ref.shape[2]
     row = lax.broadcasted_iota(jnp.int32, (rows, lanes), 0)
     lane = lax.broadcasted_iota(jnp.int32, (rows, lanes), 1)
@@ -73,8 +78,8 @@
             high = value.astype(jnp.bfloat16)
             low = (value - high.astype(jnp.float32)).astype(jnp.bfloat16)
             for j in range(tiles):
-                table_ref[f, z, j] = high[:, j * 128 : (j + 1) * 128]
-                table_ref[fields + f, z, j] = low[:, j * 128 : (j + 1) * 128]
+                table_ref[f, z, j, :, :128] = high[:, j * 128 : (j + 1) * 128]
+                table_ref[f, z, j, :, 128:] = low[:, j * 128 : (j + 1) * 128]
             first_ref[f, z] = value[0]
             last_ref[f, z] = value[rows - 1]
             if z == 0:
@@ -97,7 +102,7 @@
             jax.ShapeDtypeStruct((fields, halo_rows, lanes), jnp.float32),
             jax.ShapeDtypeStruct((fields, depth, lanes), jnp.float32),
             jax.ShapeDtypeStruct((fields, depth, lanes), jnp.float32),
-            jax.ShapeDtypeStruct((2 * fields,) + leak.shape[1:], jnp.bfloat16),
+            jax.ShapeDtypeStruct(leak.shape[:-1] + (2 * leak.shape[-1],), jnp.bfloat16),
         ),
         in_specs=[vmem] * 10,
         out_specs=(vmem,) * 6,
@@ -175,7 +180,8 @@
     rock_table = rock_state.reshape(2, depth, rows, tiles, 128).transpose(0, 1, 3, 2, 4)
     rock_table = rock_table.reshape(2, cell_rows, 128)
     rock_high_part, rock_low_part = split_bf16(rock_table)
-    rock_parts = jnp.concatenate([rock_high_part, rock_low_part], 0)
+    rock_parts = jnp.concatenate([rock_high_part, rock_low_part], 2)
+    cell_col_pair = jnp.concatenate([cell_col_mask, cell_col_mask], 1)
     fracture_start = fracture_state.astype(jnp.bfloat16).astype(jnp.float32)
     fracture_start = fracture_start.reshape(2, -1, rock_state.shape[-1])
     rock_low = jnp.concatenate([rock_now[:, 0], fracture_start], 1)
@@ -185,7 +191,7 @@
     source_blocks = fracture_source.reshape(2, blocks, segment_width)
     layer_rows = rock_now.shape[2]
     for sweep_index in range(ITERS):
-        rock_picked = pick_parts(cell_row_onehot, cell_col_mask, rock_parts)
+        rock_picked = pick_joined(cell_row_onehot, cell_col_pair, rock_parts)
         send_rock = slot_weight_flat[None] * rock_picked
         fracture_table = fracture_now.reshape(2, blocks, segment_width)
         send_fracture = pick_values(segment_row_onehot, segment_col_mask, fracture_table)
@@ -240,7 +246,7 @@
             cell_inverse,
             fracture_next.astype(jnp.bfloat16).astype(jnp.float32).reshape(fracture_wide.shape),
         )
-        rock_parts = rock_table.reshape(4, cell_rows, 128)
+        rock_parts = rock_table.reshape(2, cell_rows, 256)
         fracture_now = fracture_next
     return (rock_now, fracture_now)
 

time: 208 us -> 214 us (1.029)
  matrix products: 28.1 us -> 32.2 us
  other arithmetic: 10.3 us -> 14 us
  waiting for transfers between devices: 12 us -> 8.65 us
    dot_general x0 -> x3, matrix products: none -> 10.8 us  [pick_joined(): jnp.einsum('kc,frc->frk', col_mask, parts, preferred_element_type=jnp.flo...]
    dot_general x6 -> x3, matrix products: 15.4 us -> 6.19 us  [pick_parts(): jnp.einsum('kc,grc->grk', col_mask, parts, preferred_element_type=jnp.flo...]
    all_to_all x3, waiting for transfers between devices: 11.9 us -> 8.61 us  [shards(): lax.all_to_all(send.transpose(1, 0, 2), 'slab', split_axis=0, concat_axis...]
    eq x0 -> x1, other arithmetic: none -> 2.48 us  [shards(): (cell_y % 128)[:, None] == lax.broadcasted_iota(jnp.int32, (1, 128), 1)]
  transfers between devices with their start and end apart: 18 -> 18, of which waited for: 1 -> 1; matrix products, arithmetic and copies ran while one was open for 19% -> 22% of each run, Pallas kernels for 0% -> 0%
where the time goes in v8:
time: 214 us; the launch traced here: 213 us
  starting transfers between devices  138 us (64%)
  matrix products  32.2 us (15%)
  other arithmetic  14 us (7%)
  local copies, waits for them, and re-layouts  13.1 us (6%)
  waiting for transfers between devices  8.65 us (4%)
  Pallas kernels  5.74 us (3%)
    ppermute x3, starting transfers between devices, shards(): from_right = lax.ppermute(rock_first, 'plane', backward_plane)  29.1 us
    all_to_all x3, starting transfers between devices, shards(): lax.all_to_all(send.transpose(1, 0, 2), 'slab', split_axis=0, concat_axis...  26.6 us
    ppermute x3, starting transfers between devices, shards(): from_above = lax.ppermute(rock_low, 'slab', backward_slab)  24.1 us
    ppermute x2, starting transfers between devices, shifted(): lax.ppermute(value, axis, [(source, source + steps) for source in range(f...  17.9 us
    ppermute x3, starting transfers between devices, shards(): from_left = lax.ppermute(rock_last, 'plane', forward_plane)  17.2 us
    all_to_all x1, starting transfers between devices, shards(): lax.all_to_all(contact_segment[0], 'slab', split_axis=0, concat_axis=0, t...  16.3 us
    dot_general x6, matrix products, place_values(): jnp.einsum('grk,kc->grc', spread, col_mask, preferred_element_type=jnp.fl...  10.8 us
    dot_general x3, matrix products, pick_joined(): jnp.einsum('kc,frc->frk', col_mask, parts, preferred_element_type=jnp.flo...  10.8 us
  transfers between devices with their start and end apart: 18, of which 1 were waited for; matrix products, arithmetic and copies ran while one was open for 22% of the time, Pallas kernels for 0%

profile of v8, /device:TPU:14, one launch (start us, length us, event | category | flops | bytes accessed | tf_op | source)
XLA Modules:
  0.0 212.8 jit_solution(3880148413682928690)
XLA Ops:
  0.6 16.3 %all-to-all-start = ((s32[64,1,128]{2,1,0:T(1,128)}), s32[64,1,128]{2,1,0:T(1,128)S(1)}, u32[]{:S(2)}, u32[]{:S(2)}) async-start(s32[64,1,128]{2,1,0:T(1,128)} %bitcast.264), calls=%async_computation | async-start | bytes 65536 | tf_op jit(solution)/shard_map/all_to_all | solution.py:140
  17.0 0.7 slice_bitcast_fusion.12
  17.7 8.5 %collective-permute-start.5 = (bf16[2,1,512]{2,1,0:T(2,128)(2,1)S(1)}, bf16[2,1,512]{2,1,0:T(2,128)(2,1)S(1)}, u32[]{:S(2)}, u32[]{:S(2)}) collective-permute-start(bf16[2,1,512]{2,1,0:T(2,128)(2,1)S(1)} %slice_bitcast_fusion.12), channel_id=1, source_target_pairs={{1,0},{2,1},{3,2},{4,3},{5,4},{6,5},{7,6},{9,8},{10,9},{11,10},{12... | collective-permute-start | bytes 6152 | tf_op jit(solution)/shard_map/ppermute | solution.py:17
  26.9 9.4 %collective-permute-start.4 = (bf16[1,8,512]{2,1,0:T(8,128)(2,1)S(1)}, bf16[1,8,512]{2,1,0:T(8,128)(2,1)S(1)}, u32[]{:S(2)}, u32[]{:S(2)}) collective-permute-start(bf16[1,8,512]{2,1,0:T(8,128)(2,1)S(1)} %get-tuple-element.56), channel_id=1, source_target_pairs={{8,0},{16,8},{24,16},{32,24},{40,32},{48,40},{56,48},{64,56},{72,6... | collective-permute-start | bytes 24584 | tf_op jit(solution)/shard_map/ppermute | solution.py:17
  36.3 0.9 fusion.157
  37.8 6.1 %collective-permute-start.2 = (f32[2,2,512]{2,1,0:T(2,128)}, f32[2,2,512]{2,1,0:T(2,128)}, u32[]{:S(2)}, u32[]{:S(2)}) collective-permute-start(f32[2,2,512]{2,1,0:T(2,128)} %bitcast.252), channel_id=1, source_target_pairs={{0,1},{1,2},{2,3},{3,4},{4,5},{5,6},{6,7},{8,9},{9,10},{10,11},{11... | collective-permute-start | bytes 24584 | tf_op jit(solution)/shard_map/ppermute | solution.py:208
  44.5 9.4 %collective-permute-start.3 = (f32[2,2,512]{2,1,0:T(2,128)}, f32[2,2,512]{2,1,0:T(2,128)}, u32[]{:S(2)}, u32[]{:S(2)}) collective-permute-start(f32[2,2,512]{2,1,0:T(2,128)} %bitcast.251), channel_id=1, source_target_pairs={{1,0},{2,1},{3,2},{4,3},{5,4},{6,5},{7,6},{9,8},{10,9},{11,10},{12... | collective-permute-start | bytes 24584 | tf_op jit(solution)/shard_map/ppermute | solution.py:209
  53.9 0.8 slice_bitcast_fusion.6
  56.1 2.0 collective-permute-start.1
  59.5 0.8 add_select_fusion.6
  60.4 0.9 reduce-precision_convert_fusion
  61.3 2.5 %iota_compare_fusion.1 = pred[8192,128]{1,0:T(32,128)(4,1)} fusion(s32[8192]{0:T(1024)S(1)} %get-tuple-element.59), kind=kLoop, calls=%fused_computation.14 | loop fusion | flops 1048576 | bytes 1081344 | tf_op jit(solution)/shard_map/eq | solution.py:162
  63.7 1.3 fusion.63
  65.2 4.0 %fusion.35 = f32[2,8192]{1,0:T(2,128)} fusion(f32[64,8192]{1,0:T(8,128)S(1)} %get-tuple-element.61, pred[8192,128]{1,0:T(32,128)(4,1)} %iota_compare_fusion.1, bf16[2,64,128]{2,1,0:T(8,128)(2,1)S(1)} %get-tuple-element.51, bf16[2,64,128]{2,1,0:T(8,128)(2,1)S(1)} %get-tuple-element.50), kind=kOutput, calls=%fused_computation.39 | convolution fusion | flops 541179904 | bytes 3276800 | tf_op jit(solution)/shard_map/kc,frc->frk/dot_general | solution.py:31
  69.8 2.3 %collective-permute-start = (f32[2,10,512]{2,1,0:T(8,128)}, f32[2,10,512]{2,1,0:T(8,128)}, u32[]{:S(2)}, u32[]{:S(2)}) collective-permute-start(f32[2,10,512]{2,1,0:T(8,128)} %get-tuple-element.78), channel_id=1, source_target_pairs={{0,8},{8,16},{16,24},{24,32},{32,40},{40,48},{48,56},{56,64},{64,7... | collective-permute-start | bytes 122888 | tf_op jit(solution)/shard_map/ppermute | solution.py:206
  73.5 2.1 fusion.38
  76.4 13.8 %all-to-all-start.1 = ((f32[64,4,128]{2,1,0:T(4,128)}), f32[64,4,128]{2,1,0:T(4,128)S(1)}, u32[]{:S(2)}, u32[]{:S(2)}) async-start(f32[64,4,128]{2,1,0:T(4,128)} %maximum_bitcast_fusion), calls=%async_computation.1 | async-start | bytes 262144 | tf_op jit(solution)/shard_map/all_to_all | solution.py:199
  90.2 0.7 bitcast_dynamic-update-slice_fusion.coef_ref
  91.0 0.8 slice.279
  92.4 0.8 slice.280
  93.7 0.9 fusion.47
  95.0 8.6 %all-to-all-done.1 = f32[64,4,128]{2,1,0:T(4,128)S(1)} async-done(((f32[64,4,128]{2,1,0:T(4,128)}), f32[64,4,128]{2,1,0:T(4,128)S(1)}, u32[]{:S(2)}, u32[]{:S(2)}) %all-to-all-start.1) | async-done | bytes 131104 | tf_op jit(solution)/shard_map/all_to_all | solution.py:199
  103.8 2.1 fusion.13
  106.0 2.3 %fusion.4 = f32[4,64,128]{2,1,0:T(8,128)S(1)} fusion(bf16[64,8192]{1,0:T(8,128)(2,1)S(1)} %copy-done.2, bf16[4,8192]{1,0:T(4,128)(2,1)S(1)} %pad_maximum_fusion.2, s32[8192]{0:T(1024)} %copy-done.9), kind=kOutput, calls=%fused_computation.11 | convolution fusion | flops 540016640 | bytes 1277952 | tf_op jit(solution)/shard_map/grk,kc->grc/dot_general | solution.py:47
  110.4 1.9 shard_map.140
  112.3 3.4 %fusion.36 = f32[2,8192]{1,0:T(2,128)S(1)} fusion(f32[64,8192]{1,0:T(8,128)S(1)} %get-tuple-element.61, bf16[2,64,256]{2,1,0:T(8,128)(2,1)} %bitcast.274, pred[8192,128]{1,0:T(32,128)(4,1)} %iota_compare_fusion.1), kind=kOutput, calls=%fused_computation.40 | convolution fusion | flops 541048832 | bytes 3276800 | tf_op jit(solution)/shard_map/kc,frc->frk/dot_general | solution.py:31
  115.8 2.1 fusion.41
  118.6 7.2 %all-to-all-start.2 = ((f32[64,4,128]{2,1,0:T(4,128)}), f32[64,4,128]{2,1,0:T(4,128)S(1)}, u32[]{:S(2)}, u32[]{:S(2)}) async-start(f32[64,4,128]{2,1,0:T(4,128)} %maximum_bitcast_fusion.1), calls=%async_computation.2 | async-start | bytes 262144 | tf_op jit(solution)/shard_map/all_to_all | solution.py:199
  125.9 2.0 collective-permute-start.6
  127.9 11.0 %collective-permute-start.7 = (f32[2,10,512]{2,1,0:T(8,128)}, f32[2,10,512]{2,1,0:T(8,128)S(1)}, u32[]{:S(2)}, u32[]{:S(2)}) collective-permute-start(f32[2,10,512]{2,1,0:T(8,128)} %get-tuple-element.18), channel_id=1, source_target_pairs={{8,0},{16,8},{24,16},{32,24},{40,32},{48,40},{56,48},{64,56},{72,6... | collective-permute-start | bytes 122888 | tf_op jit(solution)/shard_map/ppermute | solution.py:207
  139.0 5.8 %collective-permute-start.8 = (f32[2,2,512]{2,1,0:T(2,128)}, f32[2,2,512]{2,1,0:T(2,128)S(1)}, u32[]{:S(2)}, u32[]{:S(2)}) collective-permute-start(f32[2,2,512]{2,1,0:T(2,128)} %get-tuple-element.19), channel_id=1, source_target_pairs={{0,1},{1,2},{2,3},{3,4},{4,5},{5,6},{6,7},{8,9},{9,10},{10,11},{11... | collective-permute-start | bytes 24584 | tf_op jit(solution)/shard_map/ppermute | solution.py:208
  144.7 9.7 %collective-permute-start.9 = (f32[2,2,512]{2,1,0:T(2,128)}, f32[2,2,512]{2,1,0:T(2,128)}, u32[]{:S(2)}, u32[]{:S(2)}) collective-permute-start(f32[2,2,512]{2,1,0:T(2,128)} %get-tuple-element.20), channel_id=1, source_target_pairs={{1,0},{2,1},{3,2},{4,3},{5,4},{6,5},{7,6},{9,8},{10,9},{11,10},{12... | collective-permute-start | bytes 24584 | tf_op jit(solution)/shard_map/ppermute | solution.py:209
  154.5 0.9 fusion.48
  156.0 2.3 %fusion.10 = f32[4,8,128]{2,1,0:T(8,128)S(1)} fusion(s32[8192]{0:T(1024)} %copy-done.19, bf16[4,8192]{1,0:T(4,128)(2,1)S(1)} %pad_maximum_fusion.5, bf16[8,8192]{1,0:T(8,128)(2,1)} %copy-done.11), kind=kOutput, calls=%fused_computation.17 | convolution fusion | flops 68419584 | bytes 245760 | tf_op jit(solution)/shard_map/grk,kc->grc/dot_general | solution.py:47
  158.5 2.1 fusion.44
  160.8 1.5 fusion.2
  164.1 1.9 shard_map.141
  166.1 3.4 %fusion.37 = f32[2,8192]{1,0:T(2,128)S(1)} fusion(f32[64,8192]{1,0:T(8,128)S(1)} %get-tuple-element.61, bf16[2,64,256]{2,1,0:T(8,128)(2,1)} %bitcast.273, pred[8192,128]{1,0:T(32,128)(4,1)} %iota_compare_fusion.1), kind=kOutput, calls=%fused_computation.41 | convolution fusion | flops 541048832 | bytes 3276800 | tf_op jit(solution)/shard_map/kc,frc->frk/dot_general | solution.py:31
  169.5 0.7 maximum_bitcast_fusion.2
  170.3 5.6 %all-to-all-start.3 = ((f32[64,4,128]{2,1,0:T(4,128)}), f32[64,4,128]{2,1,0:T(4,128)S(1)}, u32[]{:S(2)}, u32[]{:S(2)}) async-start(f32[64,4,128]{2,1,0:T(4,128)} %maximum_bitcast_fusion.2), calls=%async_computation.3 | async-start | bytes 262144 | tf_op jit(solution)/shard_map/all_to_all | solution.py:199
  175.8 2.0 collective-permute-start.10
  177.9 11.0 %collective-permute-start.11 = (f32[2,10,512]{2,1,0:T(8,128)S(1)}, f32[2,10,512]{2,1,0:T(8,128)S(1)}, u32[]{:S(2)}, u32[]{:S(2)}) collective-permute-start(f32[2,10,512]{2,1,0:T(8,128)S(1)} %copy-done.30), channel_id=1, source_target_pairs={{8,0},{16,8},{24,16},{32,24},{40,32},{48,40},{56,48},{64,56},{72,6... | collective-permute-start | bytes 122888 | tf_op jit(solution)/shard_map/ppermute | solution.py:207
  188.9 5.4 %collective-permute-start.12 = (f32[2,2,512]{2,1,0:T(2,128)S(1)}, f32[2,2,512]{2,1,0:T(2,128)S(1)}, u32[]{:S(2)}, u32[]{:S(2)}) collective-permute-start(f32[2,2,512]{2,1,0:T(2,128)S(1)} %copy-done.32), channel_id=1, source_target_pairs={{0,1},{1,2},{2,3},{3,4},{4,5},{5,6},{6,7},{8,9},{9,10},{10,11},{11... | collective-permute-start | bytes 24584 | tf_op jit(solution)/shard_map/ppermute | solution.py:208
  194.4 10.1 %collective-permute-start.13 = (f32[2,2,512]{2,1,0:T(2,128)S(1)}, f32[2,2,512]{2,1,0:T(2,128)S(1)}, u32[]{:S(2)}, u32[]{:S(2)}) collective-permute-start(f32[2,2,512]{2,1,0:T(2,128)S(1)} %copy-done.31), channel_id=1, source_target_pairs={{1,0},{2,1},{3,2},{4,3},{5,4},{6,5},{7,6},{9,8},{10,9},{11,10},{12... | collective-permute-start | bytes 24584 | tf_op jit(solution)/shard_map/ppermute | solution.py:209
  205.3 1.3 fusion.7
  206.7 1.5 fusion
  208.2 0.8 fusion.133
  210.9 1.9 shard_map.142
  (148 shorter events, 18.0 us)
Async XLA Ops:
  0.6 94.0 %copy-start = (bf16[8,3,128,128]{3,2,1,0:T(8,128)(2,1)S(1)}, bf16[8,3,128,128]{3,2,1,0:T(8,128)(2,1)}, u32[]{:S(2)}) copy-start(bf16[8,3,128,128]{3,2,1,0:T(8,128)(2,1)} %param.19) | copy-start | bytes 2359300
  0.6 72.2 %all-to-all-start = ((s32[64,1,128]{2,1,0:T(1,128)}), s32[64,1,128]{2,1,0:T(1,128)S(1)}, u32[]{:S(2)}, u32[]{:S(2)}) async-start(s32[64,1,128]{2,1,0:T(1,128)} %bitcast.264), calls=%async_computation | async-start | bytes 65536 | tf_op jit(solution)/shard_map/all_to_all | solution.py:140
  17.7 55.1 %collective-permute-start.5 = (bf16[2,1,512]{2,1,0:T(2,128)(2,1)S(1)}, bf16[2,1,512]{2,1,0:T(2,128)(2,1)S(1)}, u32[]{:S(2)}, u32[]{:S(2)}) collective-permute-start(bf16[2,1,512]{2,1,0:T(2,128)(2,1)S(1)} %slice_bitcast_fusion.12), channel_id=1, source_target_pairs={{1,0},{2,1},{3,2},{4,3},{5,4},{6,5},{7,6},{9,8},{10,9},{11,10},{12... | collective-permute-start | bytes 6152 | tf_op jit(solution)/shard_map/ppermute | solution.py:17
  26.9 42.9 %collective-permute-start.4 = (bf16[1,8,512]{2,1,0:T(8,128)(2,1)S(1)}, bf16[1,8,512]{2,1,0:T(8,128)(2,1)S(1)}, u32[]{:S(2)}, u32[]{:S(2)}) collective-permute-start(bf16[1,8,512]{2,1,0:T(8,128)(2,1)S(1)} %get-tuple-element.56), channel_id=1, source_target_pairs={{8,0},{16,8},{24,16},{32,24},{40,32},{48,40},{56,48},{64,56},{72,6... | collective-permute-start | bytes 24584 | tf_op jit(solution)/shard_map/ppermute | solution.py:17
  37.8 72.6 %collective-permute-start.2 = (f32[2,2,512]{2,1,0:T(2,128)}, f32[2,2,512]{2,1,0:T(2,128)}, u32[]{:S(2)}, u32[]{:S(2)}) collective-permute-start(f32[2,2,512]{2,1,0:T(2,128)} %bitcast.252), channel_id=1, source_target_pairs={{0,1},{1,2},{2,3},{3,4},{4,5},{5,6},{6,7},{8,9},{9,10},{10,11},{11... | collective-permute-start | bytes 24584 | tf_op jit(solution)/shard_map/ppermute | solution.py:208
  44.5 65.9 %collective-permute-start.3 = (f32[2,2,512]{2,1,0:T(2,128)}, f32[2,2,512]{2,1,0:T(2,128)}, u32[]{:S(2)}, u32[]{:S(2)}) collective-permute-start(f32[2,2,512]{2,1,0:T(2,128)} %bitcast.251), channel_id=1, source_target_pairs={{1,0},{2,1},{3,2},{4,3},{5,4},{6,5},{7,6},{9,8},{10,9},{11,10},{12... | collective-permute-start | bytes 24584 | tf_op jit(solution)/shard_map/ppermute | solution.py:209
  56.1 34.9 %collective-permute-start.1 = (f32[2,10,512]{2,1,0:T(8,128)}, f32[2,10,512]{2,1,0:T(8,128)}, u32[]{:S(2)}, u32[]{:S(2)}) collective-permute-start(f32[2,10,512]{2,1,0:T(8,128)} %get-tuple-element.77), channel_id=1, source_target_pairs={{8,0},{16,8},{24,16},{32,24},{40,32},{48,40},{56,48},{64,56},{72,6... | collective-permute-start | bytes 122888 | tf_op jit(solution)/shard_map/ppermute | solution.py:207
  60.4 3.4 %copy-start.9 = (s32[8192]{0:T(1024)}, s32[8192]{0:T(1024)S(1)}, u32[]{:S(2)}) copy-start(s32[8192]{0:T(1024)S(1)} %get-tuple-element.59) | copy-start | bytes 98308
  61.2 3.8 %copy-start.22 = (f32[1,64,128]{2,1,0:T(8,128)S(1)}, f32[1,64,128]{2,1,0:T(8,128)}, u32[]{:S(2)}) copy-start(f32[1,64,128]{2,1,0:T(8,128)} %param.24) | copy-start | bytes 98308
  61.3 3.8 %copy-start.29 = (s32[1,64]{1,0:T(1,128)S(1)}, s32[1,64]{1,0:T(1,128)}, u32[]{:S(2)}) copy-start(s32[1,64]{1,0:T(1,128)} %param.25) | copy-start | bytes 772
  65.2 4.0 %copy-start.27 = (s32[8,3]{0,1:T(4,128)S(1)}, s32[8,3]{0,1:T(4,128)}, u32[]{:S(2)}) copy-start(s32[8,3]{0,1:T(4,128)} %param.21) | copy-start | bytes 292
  65.2 6.9 %copy-start.8 = (bf16[3,2,8,512]{3,2,1,0:T(8,128)(2,1)S(1)}, bf16[3,2,8,512]{3,2,1,0:T(8,128)(2,1)}, u32[]{:S(2)}) copy-start(bf16[3,2,8,512]{3,2,1,0:T(8,128)(2,1)} %param.15) | copy-start | bytes 147460
  69.2 25.5 %copy-start.17 = (f32[2,1024]{1,0:T(2,128)S(1)}, f32[2,1024]{1,0:T(2,128)}, u32[]{:S(2)}) copy-start(f32[2,1024]{1,0:T(2,128)} %param.18) | copy-start | bytes 24580
  69.8 22.6 %collective-permute-start = (f32[2,10,512]{2,1,0:T(8,128)}, f32[2,10,512]{2,1,0:T(8,128)}, u32[]{:S(2)}, u32[]{:S(2)}) collective-permute-start(f32[2,10,512]{2,1,0:T(8,128)} %get-tuple-element.78), channel_id=1, source_target_pairs={{0,8},{8,16},{16,24},{24,32},{32,40},{40,48},{48,56},{56,64},{64,7... | collective-permute-start | bytes 122888 | tf_op jit(solution)/shard_map/ppermute | solution.py:206
  72.8 2.7 %copy-start.18 = (f32[2,8192]{1,0:T(2,128)S(1)}, f32[2,8192]{1,0:T(2,128)}, u32[]{:S(2)}) copy-start(f32[2,8192]{1,0:T(2,128)} %fusion.35) | copy-start | bytes 196612
  72.9 0.6 copy-start.19
  72.9 33.0 %copy-start.11 = (bf16[8,8192]{1,0:T(8,128)(2,1)}, bf16[8,8192]{1,0:T(8,128)(2,1)S(1)}, u32[]{:S(2)}) copy-start(bf16[8,8192]{1,0:T(8,128)(2,1)S(1)} %get-tuple-element.57) | copy-start | bytes 393220
  72.9 42.8 %copy-start.6 = (f32[8,8192]{1,0:T(8,128)}, f32[8,8192]{1,0:T(8,128)S(1)}, u32[]{:S(2)}) copy-start(f32[8,8192]{1,0:T(8,128)S(1)} %get-tuple-element.58) | copy-start | bytes 786436
  76.4 27.2 %all-to-all-start.1 = ((f32[64,4,128]{2,1,0:T(4,128)}), f32[64,4,128]{2,1,0:T(4,128)S(1)}, u32[]{:S(2)}, u32[]{:S(2)}) async-start(f32[64,4,128]{2,1,0:T(4,128)} %maximum_bitcast_fusion), calls=%async_computation.1 | async-start | bytes 262144 | tf_op jit(solution)/shard_map/all_to_all | solution.py:199
  91.0 17.4 %copy-start.5 = (bf16[6,2,8,512]{3,2,1,0:T(8,128)(2,1)}, bf16[6,2,8,512]{3,2,1,0:T(8,128)(2,1)S(1)}, u32[]{:S(2)}) copy-start(bf16[6,2,8,512]{3,2,1,0:T(8,128)(2,1)S(1)} %bitcast_dynamic-update-slice_fusion.coef_ref) | copy-start | bytes 294916
  103.6 2.4 %copy-start.2 = (bf16[64,8192]{1,0:T(8,128)(2,1)S(1)}, bf16[64,8192]{1,0:T(8,128)(2,1)}, u32[]{:S(2)}) copy-start(bf16[64,8192]{1,0:T(8,128)(2,1)} %get-tuple-element.62) | copy-start | bytes 3145732
  106.0 2.9 %copy-start.1 = (bf16[8,128,128]{2,1,0:T(8,128)(2,1)S(1)}, bf16[8,128,128]{2,1,0:T(8,128)(2,1)}, u32[]{:S(2)}) copy-start(bf16[8,128,128]{2,1,0:T(8,128)(2,1)} %param.20) | copy-start | bytes 786436
  112.3 3.4 %copy-start.20 = (s32[8192]{0:T(1024)S(1)}, s32[8192]{0:T(1024)}, u32[]{:S(2)}) copy-start(s32[8192]{0:T(1024)} %copy-done.19) | copy-start | bytes 98308
  112.3 3.4 %copy-start.26 = (bf16[2,8,128]{2,1,0:T(8,128)(2,1)S(1)}, bf16[2,8,128]{2,1,0:T(8,128)(2,1)}, u32[]{:S(2)}) copy-start(bf16[2,8,128]{2,1,0:T(8,128)(2,1)} %get-tuple-element.74) | copy-start | bytes 12292
  117.9 40.6 %copy-start.21 = (s32[8192]{0:T(1024)S(1)}, s32[8192]{0:T(1024)}, u32[]{:S(2)}) copy-start(s32[8192]{0:T(1024)} %copy-done.19) | copy-start | bytes 98308
  118.6 37.1 %all-to-all-start.2 = ((f32[64,4,128]{2,1,0:T(4,128)}), f32[64,4,128]{2,1,0:T(4,128)S(1)}, u32[]{:S(2)}, u32[]{:S(2)}) async-start(f32[64,4,128]{2,1,0:T(4,128)} %maximum_bitcast_fusion.1), calls=%async_computation.2 | async-start | bytes 262144 | tf_op jit(solution)/shard_map/all_to_all | solution.py:199
  125.9 28.6 %collective-permute-start.6 = (f32[2,10,512]{2,1,0:T(8,128)}, f32[2,10,512]{2,1,0:T(8,128)S(1)}, u32[]{:S(2)}, u32[]{:S(2)}) collective-permute-start(f32[2,10,512]{2,1,0:T(8,128)} %get-tuple-element.17), channel_id=1, source_target_pairs={{0,8},{8,16},{16,24},{24,32},{32,40},{40,48},{48,56},{56,64},{64,7... | collective-permute-start | bytes 122888 | tf_op jit(solution)/shard_map/ppermute | solution.py:206
  127.9 26.6 %collective-permute-start.7 = (f32[2,10,512]{2,1,0:T(8,128)}, f32[2,10,512]{2,1,0:T(8,128)S(1)}, u32[]{:S(2)}, u32[]{:S(2)}) collective-permute-start(f32[2,10,512]{2,1,0:T(8,128)} %get-tuple-element.18), channel_id=1, source_target_pairs={{8,0},{16,8},{24,16},{32,24},{40,32},{48,40},{56,48},{64,56},{72,6... | collective-permute-start | bytes 122888 | tf_op jit(solution)/shard_map/ppermute | solution.py:207
  139.0 24.5 %collective-permute-start.8 = (f32[2,2,512]{2,1,0:T(2,128)}, f32[2,2,512]{2,1,0:T(2,128)S(1)}, u32[]{:S(2)}, u32[]{:S(2)}) collective-permute-start(f32[2,2,512]{2,1,0:T(2,128)} %get-tuple-element.19), channel_id=1, source_target_pairs={{0,1},{1,2},{2,3},{3,4},{4,5},{5,6},{6,7},{8,9},{9,10},{10,11},{11... | collective-permute-start | bytes 24584 | tf_op jit(solution)/shard_map/ppermute | solution.py:208
  144.7 18.8 %collective-permute-start.9 = (f32[2,2,512]{2,1,0:T(2,128)}, f32[2,2,512]{2,1,0:T(2,128)}, u32[]{:S(2)}, u32[]{:S(2)}) collective-permute-start(f32[2,2,512]{2,1,0:T(2,128)} %get-tuple-element.20), channel_id=1, source_target_pairs={{1,0},{2,1},{3,2},{4,3},{5,4},{6,5},{7,6},{9,8},{10,9},{11,10},{12... | collective-permute-start | bytes 24584 | tf_op jit(solution)/shard_map/ppermute | solution.py:209
  154.4 6.2 %copy-start.13 = (f32[2,10,512]{2,1,0:T(8,128)}, f32[2,10,512]{2,1,0:T(8,128)S(1)}, u32[]{:S(2)}) copy-start(f32[2,10,512]{2,1,0:T(8,128)S(1)} %collective-permute-done.6.below_ref) | copy-start | bytes 122884
  154.5 6.1 %copy-start.15 = (f32[2,10,512]{2,1,0:T(8,128)}, f32[2,10,512]{2,1,0:T(8,128)S(1)}, u32[]{:S(2)}) copy-start(f32[2,10,512]{2,1,0:T(8,128)S(1)} %collective-permute-done.7.above_ref) | copy-start | bytes 122884
  155.8 2.8 %copy-start.7 = (f32[8,8192]{1,0:T(8,128)S(1)}, f32[8,8192]{1,0:T(8,128)}, u32[]{:S(2)}) copy-start(f32[8,8192]{1,0:T(8,128)} %copy-done.6) | copy-start | bytes 786436
  156.0 4.8 %copy-start.3 = (bf16[64,8192]{1,0:T(8,128)(2,1)S(1)}, bf16[64,8192]{1,0:T(8,128)(2,1)}, u32[]{:S(2)}) copy-start(bf16[64,8192]{1,0:T(8,128)(2,1)} %get-tuple-element.62) | copy-start | bytes 3145732
  156.0 4.8 %copy-start.10 = (s32[8192]{0:T(1024)S(1)}, s32[8192]{0:T(1024)}, u32[]{:S(2)}) copy-start(s32[8192]{0:T(1024)} %copy-done.9) | copy-start | bytes 98308
  166.0 11.9 %copy-start.30 = (f32[2,10,512]{2,1,0:T(8,128)S(1)}, f32[2,10,512]{2,1,0:T(8,128)}, u32[]{:S(2)}) copy-start(f32[2,10,512]{2,1,0:T(8,128)} %get-tuple-element.24) | copy-start | bytes 122884
  166.0 22.9 %copy-start.32 = (f32[2,2,512]{2,1,0:T(2,128)S(1)}, f32[2,2,512]{2,1,0:T(2,128)}, u32[]{:S(2)}) copy-start(f32[2,2,512]{2,1,0:T(2,128)} %get-tuple-element.25) | copy-start | bytes 24580
  166.0 28.3 %copy-start.31 = (f32[2,2,512]{2,1,0:T(2,128)S(1)}, f32[2,2,512]{2,1,0:T(2,128)}, u32[]{:S(2)}) copy-start(f32[2,2,512]{2,1,0:T(2,128)} %get-tuple-element.26) | copy-start | bytes 24580
  166.0 38.5 %copy-start.28 = (s32[8,3]{0,1:T(4,128)S(1)}, s32[8,3]{0,1:T(4,128)}, u32[]{:S(2)}) copy-start(s32[8,3]{0,1:T(4,128)} %fusion.144) | copy-start | bytes 292
  166.0 39.3 %copy-start.12 = (bf16[8,8192]{1,0:T(8,128)(2,1)S(1)}, bf16[8,8192]{1,0:T(8,128)(2,1)}, u32[]{:S(2)}) copy-start(bf16[8,8192]{1,0:T(8,128)(2,1)} %copy-done.11) | copy-start | bytes 393220
  169.5 37.2 %copy-start.4 = (bf16[64,8192]{1,0:T(8,128)(2,1)S(1)}, bf16[64,8192]{1,0:T(8,128)(2,1)}, u32[]{:S(2)}) copy-start(bf16[64,8192]{1,0:T(8,128)(2,1)} %get-tuple-element.62) | copy-start | bytes 3145732
  170.3 34.8 %all-to-all-start.3 = ((f32[64,4,128]{2,1,0:T(4,128)}), f32[64,4,128]{2,1,0:T(4,128)S(1)}, u32[]{:S(2)}, u32[]{:S(2)}) async-start(f32[64,4,128]{2,1,0:T(4,128)} %maximum_bitcast_fusion.2), calls=%async_computation.3 | async-start | bytes 262144 | tf_op jit(solution)/shard_map/all_to_all | solution.py:199
  175.8 28.6 %collective-permute-start.10 = (f32[2,10,512]{2,1,0:T(8,128)}, f32[2,10,512]{2,1,0:T(8,128)S(1)}, u32[]{:S(2)}, u32[]{:S(2)}) collective-permute-start(f32[2,10,512]{2,1,0:T(8,128)} %get-tuple-element.23), channel_id=1, source_target_pairs={{0,8},{8,16},{16,24},{24,32},{32,40},{40,48},{48,56},{56,64},{64,7... | collective-permute-start | bytes 122888 | tf_op jit(solution)/shard_map/ppermute | solution.py:206
  177.9 26.6 %collective-permute-start.11 = (f32[2,10,512]{2,1,0:T(8,128)S(1)}, f32[2,10,512]{2,1,0:T(8,128)S(1)}, u32[]{:S(2)}, u32[]{:S(2)}) collective-permute-start(f32[2,10,512]{2,1,0:T(8,128)S(1)} %copy-done.30), channel_id=1, source_target_pairs={{8,0},{16,8},{24,16},{32,24},{40,32},{48,40},{56,48},{64,56},{72,6... | collective-permute-start | bytes 122888 | tf_op jit(solution)/shard_map/ppermute | solution.py:207
  188.9 21.3 %collective-permute-start.12 = (f32[2,2,512]{2,1,0:T(2,128)S(1)}, f32[2,2,512]{2,1,0:T(2,128)S(1)}, u32[]{:S(2)}, u32[]{:S(2)}) collective-permute-start(f32[2,2,512]{2,1,0:T(2,128)S(1)} %copy-done.32), channel_id=1, source_target_pairs={{0,1},{1,2},{2,3},{3,4},{4,5},{5,6},{6,7},{8,9},{9,10},{10,11},{11... | collective-permute-start | bytes 24584 | tf_op jit(solution)/shard_map/ppermute | solution.py:208
  194.4 15.9 %collective-permute-start.13 = (f32[2,2,512]{2,1,0:T(2,128)S(1)}, f32[2,2,512]{2,1,0:T(2,128)S(1)}, u32[]{:S(2)}, u32[]{:S(2)}) collective-permute-start(f32[2,2,512]{2,1,0:T(2,128)S(1)} %copy-done.31), channel_id=1, source_target_pairs={{1,0},{2,1},{3,2},{4,3},{5,4},{6,5},{7,6},{9,8},{10,9},{11,10},{12... | collective-permute-start | bytes 24584 | tf_op jit(solution)/shard_map/ppermute | solution.py:209
  204.4 3.7 %copy-start.14 = (f32[2,10,512]{2,1,0:T(8,128)}, f32[2,10,512]{2,1,0:T(8,128)S(1)}, u32[]{:S(2)}) copy-start(f32[2,10,512]{2,1,0:T(8,128)S(1)} %collective-permute-done.10.below_ref) | copy-start | bytes 122884
  204.5 3.7 %copy-start.16 = (f32[2,10,512]{2,1,0:T(8,128)}, f32[2,10,512]{2,1,0:T(8,128)S(1)}, u32[]{:S(2)}) copy-start(f32[2,10,512]{2,1,0:T(8,128)S(1)} %collective-permute-done.11.above_ref) | copy-start | bytes 122884
  (3 other events, 1.8 us)
